TPU v7x, 32 devices: a whole 2x2x4 slice. The times are simulated.
32 devices in a mesh: gx: 4 (over y, x), gy: 8 (over z, core).
Axes of the slice: x: 2, y: 2, z: 4, core: 2. Of those that a mesh axis runs over, the one named last changes fastest.
Arguments:
- atom_data: float32 [4, 16, 32, 2, 128], P(None, 'gx', 'gy'), as said below
- counts: int32 [16, 32, 2], P('gx', 'gy'), may hold values from 32 to 128, as said below
- near_flags: int32 [26, 16, 32, 2], P(None, 'gx', 'gy'), may hold values 0 or 1
- child_up: bfloat16 [8, 81, 81], replicated, may hold values from -0.25 to 0.25
- child_down: bfloat16 [8, 81, 81], replicated, may hold values from -0.5 to 0.5
- leaf_far: bfloat16 [81, 81], replicated, may hold values from -0.1875 to 0.1875
- parent_far: bfloat16 [81, 81], replicated, may hold values from -0.0625 to 0.0625
- column_up: bfloat16 [81, 81], replicated, may hold values from -0.3125 to 0.3125
- column_down: bfloat16 [81, 81], replicated, may hold values from -0.5 to 0.5
- tree_up: bfloat16 [2, 2, 81, 81], replicated, may hold values from -0.5 to 0.5
- tree_down: bfloat16 [2, 2, 81, 81], replicated, may hold values from -0.5 to 0.5
- tree_side: bfloat16 [2, 2, 81, 81], replicated, may hold values from -0.5 to 0.5
- lattice: bfloat16 [81, 81], replicated, may hold values from -0.625 to 0.625
Outputs:
- fields: float32 [4, 16, 32, 2, 128], P(None, 'gx', 'gy')
Inputs may be any that keep to these rules, and one draw needn't show every extreme that they name: `atom_data`: rows 0 to 2 give an atom's position inside its leaf in leaf widths, from 0 to 1; row 3 its charge. Slots at or past a leaf's count are padding. A leaf's atoms fill its first counts slots; some leaf is full.
All inputs are finite; a program needn't handle non-finite values. No bound on the sum of `near_flags` on one device may be relied on, other than what follows from the above.
Results may differ from a plain program's by a relative error of at most 0.0003.
Values sent between devices are 32-bit elements; how exact they have to be, the bound alone decides.
No kernel may reach another device: no remote copies, remote signals or barrier semaphores. Data moves between devices by JAX's collectives and lax.ppermute only.
A program may use at most 64 MiB of HBM per device.

v0:
```python
import functools

import jax
import jax.numpy as jnp
from jax import lax
from jax.experimental import pallas as pl
from jax.experimental.pallas import tpu as pltpu
from jax.sharding import PartitionSpec as P

soften = 0.04
coulomb = 0.1
highest = lax.Precision.HIGHEST


def from_partner(value, axis, bit):
    mask = 2**bit
    pairs = [(source, source ^ mask) for source in range(lax.axis_size(axis))]
    return lax.ppermute(value, axis, pairs)


def extended_2(block, sides, width):
    for axis, dim in sides:
        count = lax.axis_size(axis)
        forward = [(i, i + 1) for i in range(count - 1)]
        forward.append((count - 1, 0))
        backward = [(target, source) for source, target in forward]
        low = lax.ppermute(
            lax.slice_in_dim(block, block.shape[dim] - width, None, axis=dim), axis, forward
        )
        high = lax.ppermute(lax.slice_in_dim(block, 0, width, axis=dim), axis, backward)
        block = jnp.concatenate([low, block, high], axis=dim)
    return block


def wave_table(coef_count, float_type):
    half_count = (coef_count - 1) // 2
    order_index = jnp.arange(1, half_count + 1, dtype=jnp.int32).astype(float_type)
    height = 1.0 - 2.0 * (order_index - 0.5) / half_count
    radius = jnp.sqrt(jnp.maximum(1.0 - height * height, 0.0))
    angle_turn = 2.399963 * order_index
    magnitude = 1.5 + jnp.mod(order_index, 3.0)
    return (
        jnp.stack([radius * jnp.cos(angle_turn), radius * jnp.sin(angle_turn), height])
        * magnitude[None]
    )


def waves_at(atom_data, waves):
    shape_lead = (waves.shape[1],) + (1,) * (atom_data.ndim - 1)
    phases = waves[0].reshape(shape_lead) * (atom_data[0] - 0.5)[None]
    phases = phases + waves[1].reshape(shape_lead) * (atom_data[1] - 0.5)[None]
    phases = phases + waves[2].reshape(shape_lead) * (atom_data[2] - 0.5)[None]
    return (jnp.cos(phases), jnp.sin(phases))


def rotate_by(field, phase):
    half_count = phase.shape[0]
    cosine = jnp.cos(phase)
    sine_part = jnp.sin(phase)
    cos_coef = field[1 : 1 + half_count]
    sin_coef = field[1 + half_count :]
    return jnp.concatenate(
        [
            field[0:1],
            cos_coef * cosine - sin_coef * sine_part,
            cos_coef * sine_part + sin_coef * cosine,
        ],
        axis=0,
    )


def offset_phases(waves, offsets):
    table = jnp.array(offsets, dtype=jnp.float32)
    return (
        table[:, 0:1] * waves[0][None]
        + table[:, 1:2] * waves[1][None]
        + table[:, 2:3] * waves[2][None]
    )


def block_phase(waves, size_x, size_y, size_z, float_type):
    place_x = jnp.arange(size_x, dtype=jnp.int32).astype(float_type)
    place_y = jnp.arange(size_y, dtype=jnp.int32).astype(float_type)
    place_z = jnp.arange(size_z, dtype=jnp.int32).astype(float_type)
    phase = waves[0][:, None, None, None] * place_x[None, :, None, None]
    phase = phase + waves[1][:, None, None, None] * place_y[None, None, :, None]
    return phase + waves[2][:, None, None, None] * place_z[None, None, None, :]


def leaf_moments(atom_data, waves):
    cosine, sine_part = waves_at(atom_data, waves)
    charge = atom_data[3]
    summed = jnp.sum(charge, axis=-1)[None]
    return jnp.concatenate(
        [
            summed,
            jnp.sum(cosine * charge[None], axis=-1),
            jnp.sum(sine_part * charge[None], axis=-1),
        ],
        axis=0,
    )


def evaluate(atom_data, local_exp, waves):
    cosine, sine_part = waves_at(atom_data, waves)
    half_count = waves.shape[1]
    cos_local = local_exp[1 : 1 + half_count][..., None]
    sin_local = local_exp[1 + half_count :][..., None]
    potential = local_exp[0][..., None] + jnp.sum(
        cos_local * cosine + sin_local * sine_part, axis=0
    )
    mixed_term = cos_local * sine_part - sin_local * cosine
    shape_lead = (half_count,) + (1,) * (mixed_term.ndim - 1)
    field_parts = [
        jnp.sum(waves[component].reshape(shape_lead) * mixed_term, axis=0) for component in range(3)
    ]
    return (potential, field_parts)


def near_row(target, source, flag_grid, shift_vec, keep_self):
    weight = source[3] * flag_grid[..., None]
    delta_x = target[0][..., :, None] - (source[0][..., None, :] + shift_vec[0])
    delta_y = target[1][..., :, None] - (source[1][..., None, :] + shift_vec[1])
    delta_z = target[2][..., :, None] - (source[2][..., None, :] + shift_vec[2])
    inverse = lax.rsqrt(delta_x * delta_x + delta_y * delta_y + delta_z * delta_z + soften)
    pair_term = weight[..., None, :] * keep_self * inverse
    cube_term = pair_term * inverse * inverse
    return jnp.stack(
        [
            jnp.sum(pair_term, axis=-1),
            jnp.sum(cube_term * delta_x, axis=-1),
            jnp.sum(cube_term * delta_y, axis=-1),
            jnp.sum(cube_term * delta_z, axis=-1),
        ]
    )


def full_flags(near_flags, float_type):
    flags_float = near_flags.astype(float_type)
    centre = jnp.ones((1,) + flags_float.shape[1:], float_type)
    return jnp.concatenate([flags_float[:13], centre, flags_float[13:]], axis=0)


def leaf_offsets():
    return [
        (shift_x, shift_y, shift_z)
        for shift_x in (-1, 0, 1)
        for shift_y in (-1, 0, 1)
        for shift_z in (-1, 0, 1)
        if (shift_x, shift_y, shift_z) != (0, 0, 0)
    ]


def parent_offsets():
    return [
        (shift_x, shift_y, shift_z)
        for shift_x in range(-2, 3)
        for shift_y in range(-2, 3)
        for shift_z in range(-2, 3)
        if max(abs(shift_x), abs(shift_y), abs(shift_z)) == 2
    ]


def climb_children(moments, matrices):
    coef_count, size_x, size_y, size_z = moments.shape
    parted = moments.reshape(coef_count, size_x // 2, 2, size_y // 2, 2, size_z // 2, 2)
    return jnp.einsum(
        "abckj,jxaybzc->kxyz",
        matrices.reshape(2, 2, 2, coef_count, coef_count),
        parted,
        precision=highest,
    )


def descend_children(parent_local, matrices):
    coef_count, size_x, size_y, size_z = parent_local.shape
    spread = jnp.einsum(
        "abckj,jxyz->kxaybzc",
        matrices.reshape(2, 2, 2, coef_count, coef_count),
        parent_local,
        precision=highest,
    )
    return spread.reshape(coef_count, 2 * size_x, 2 * size_y, 2 * size_z)


def matrix_vector(matrix, vector):
    return jnp.dot(matrix, vector, precision=highest)


def pick_side(matrices, own_side):
    return lax.dynamic_index_in_dim(matrices, own_side, 0, keepdims=False)


def pair_step(matrices, own_side, current, partner):
    return matrix_vector(pick_side(matrices, own_side), current) + matrix_vector(
        pick_side(matrices, 1 - own_side), partner
    )


def chain_tree(column, tree_up, tree_down, tree_side, lattice):
    climbs = tree_up.astype(jnp.float32)
    lowers = tree_down.astype(jnp.float32)
    sideways = tree_side.astype(jnp.float32)
    current = column
    visited = []
    for level_bit in range(lax.axis_size("gx").bit_length() - 1):
        partner = from_partner(current, "gx", level_bit)
        own_side = lax.axis_index("gx") // 2**level_bit % 2
        current = pair_step(climbs[0], own_side, current, partner)
        visited.append((0, own_side, partner))
    for level_bit in range(lax.axis_size("gy").bit_length() - 1):
        partner = from_partner(current, "gy", level_bit)
        own_side = lax.axis_index("gy") // 2**level_bit % 2
        current = pair_step(climbs[1], own_side, current, partner)
        visited.append((1, own_side, partner))
    local_exp = matrix_vector(lattice.astype(jnp.float32), current)
    for axis_num, own_side, partner in reversed(visited):
        local_exp = matrix_vector(pick_side(lowers[axis_num], own_side), local_exp) + matrix_vector(
            pick_side(sideways[axis_num], own_side), partner
        )
    return local_exp


def assemble(near_terms, potential, field_parts, charge, live_slots):
    rows = [coulomb * (near_terms[0] + potential) * live_slots]
    for component in range(3):
        rows.append(coulomb * charge * (near_terms[1 + component] + field_parts[component]))
    return jnp.stack(rows)


NEAR_ROWS = 32
NEAR_PIECES = 8


def near_pairs(tx, ty, tz, srow, mask):
    weight = srow[3:4, :]
    delta_x = tx - srow[0:1, :]
    delta_y = ty - srow[1:2, :]
    delta_z = tz - srow[2:3, :]
    inverse = lax.rsqrt(delta_x * delta_x + delta_y * delta_y + delta_z * delta_z + soften)
    pair_term = weight * inverse
    if mask is not None:
        pair_term = jnp.where(mask, pair_term, 0.0)
    cube_term = pair_term * inverse * inverse
    return (pair_term, cube_term * delta_x, cube_term * delta_y, cube_term * delta_z)


def near_kernel(first_leaf, count_ref, listed_ref, place_ref, kind_ref, target_ref, source_ref, shift_ref, out_ref):
    piece_leaves = out_ref.shape[0]
    listed_width = place_ref.shape[0] // count_ref.shape[0]
    rows = NEAR_ROWS
    lanes = out_ref.shape[2]
    out_ref[...] = jnp.zeros(out_ref.shape, out_ref.dtype)
    lane = lax.broadcasted_iota(jnp.int32, (rows, lanes), 1)
    row = lax.broadcasted_iota(jnp.int32, (rows, lanes), 0)

    def leaf_body(local, carry):
        leaf = first_leaf + local
        chunk_count = (count_ref[leaf] + rows - 1) // rows
        listed = listed_ref[leaf]
        base = leaf * listed_width

        def chunk_body(chunk, carry2):
            first = pl.multiple_of(chunk * rows, rows)
            column = target_ref[local, pl.ds(first, rows), :]
            tx = jnp.broadcast_to(column[:, 0:1], (rows, lanes))
            ty = jnp.broadcast_to(column[:, 1:2], (rows, lanes))
            tz = jnp.broadcast_to(column[:, 2:3], (rows, lanes))
            acc = near_pairs(tx, ty, tz, source_ref[place_ref[base]], row + first != lane)

            def offset_body(number, acc):
                srow = source_ref[place_ref[base + number]] + shift_ref[kind_ref[base + number]]
                terms = near_pairs(tx, ty, tz, srow, None)
                return tuple(a + b for a, b in zip(acc, terms))

            acc = lax.fori_loop(1, listed, offset_body, acc)
            sums = [jnp.sum(part, axis=1, keepdims=True) for part in acc]
            tile = jnp.where(
                lane == 0, sums[0], jnp.where(lane == 1, sums[1], jnp.where(lane == 2, sums[2], sums[3]))
            )
            out_ref[local, pl.ds(first, rows), :] = jnp.where(lane < 4, tile, 0.0)
            return carry2

        lax.fori_loop(0, chunk_count, chunk_body, 0)
        return carry

    lax.fori_loop(0, piece_leaves, leaf_body, 0)


def near_local(charged, rimmed, counts, near_flags):
    size_x, size_y, size_z, slot_count = charged.shape[1:]
    leaf_count = size_x * size_y * size_z
    ext_y = size_y + 2
    target = jnp.transpose(charged, (1, 2, 3, 4, 0)).reshape(leaf_count, slot_count, 4)
    source = jnp.transpose(rimmed, (1, 2, 3, 0, 4)).reshape(-1, 4, slot_count)
    source = jnp.pad(source, ((0, 0), (0, 4), (0, 0)))
    offsets = [(0, 0, 0)] + leaf_offsets()
    shift_rows = jnp.array([[float(v) for v in offset] + [0.0] * 5 for offset in offsets], jnp.float32)
    shift_table = jnp.broadcast_to(shift_rows[:, :, None], (len(offsets), 8, slot_count))
    leaf_x = jnp.arange(size_x, dtype=jnp.int32)[:, None, None]
    leaf_y = jnp.arange(size_y, dtype=jnp.int32)[None, :, None]
    leaf_z = jnp.arange(size_z, dtype=jnp.int32)[None, None, :]
    places = []
    for offset in offsets:
        place = ((leaf_x + 1 + offset[0]) * ext_y + leaf_y + 1 + offset[1]) * size_z + leaf_z + offset[2]
        places.append(jnp.broadcast_to(place, (size_x, size_y, size_z)))
    places = jnp.stack(places).reshape(len(offsets), leaf_count)
    layer = jnp.arange(size_z, dtype=jnp.int32)
    valid = jnp.stack([((layer + offset[2] >= 0) & (layer + offset[2] < size_z)) for offset in offsets[1:]])
    active = (near_flags != 0) & valid[:, None, None, :]
    active = jnp.concatenate([jnp.ones((1, leaf_count), bool), active.reshape(len(offsets) - 1, leaf_count)])
    order = jnp.argsort(jnp.logical_not(active).astype(jnp.int32), axis=0, stable=True)
    listed = jnp.sum(active.astype(jnp.int32), axis=0)
    place_list = jnp.take_along_axis(places, order, axis=0)
    place_list = jnp.where(jnp.take_along_axis(active, order, axis=0), place_list, 0)
    place_list = jnp.transpose(place_list).reshape(-1)
    kind_list = jnp.transpose(order).reshape(-1).astype(jnp.int32)
    count_list = counts.reshape(-1)
    piece = leaf_count // NEAR_PIECES if leaf_count % NEAR_PIECES == 0 else leaf_count
    outs = []
    for first_leaf in range(0, leaf_count, piece):
        pairs = piece * slot_count * slot_count * 10
        outs.append(
            pl.pallas_call(
                functools.partial(near_kernel, first_leaf),
                out_shape=jax.ShapeDtypeStruct((piece, slot_count, 128), jnp.float32),
                in_specs=[pl.BlockSpec(memory_space=pltpu.SMEM)] * 4 + [pl.BlockSpec(memory_space=pltpu.VMEM)] * 3,
                out_specs=pl.BlockSpec(memory_space=pltpu.VMEM),
                cost_estimate=pl.CostEstimate(
                    flops=20 * pairs, transcendentals=pairs, bytes_accessed=8 * piece * slot_count * 128
                ),
            )(count_list, listed, place_list, kind_list, target[first_leaf : first_leaf + piece], source, shift_table)
        )
    out = jnp.concatenate([part[:, :, :4] for part in outs], axis=0)
    near = jnp.transpose(out, (2, 0, 1))
    return near.reshape(4, size_x, size_y, size_z, slot_count)


def body(
    atom_data,
    counts,
    near_flags,
    child_up,
    child_down,
    leaf_far,
    parent_far,
    column_up,
    column_down,
    tree_up,
    tree_down,
    tree_side,
    lattice,
):
    coef_count = lattice.shape[0]
    slot_count = atom_data.shape[4]
    size_x, size_y, size_z = (atom_data.shape[1], atom_data.shape[2], atom_data.shape[3])
    live_slots = (
        jnp.arange(slot_count, dtype=jnp.int32)[None, None, None, :] < counts[..., None]
    ).astype(jnp.float32)
    charged = jnp.concatenate([atom_data[:3], (atom_data[3] * live_slots)[None]], axis=0)
    waves = wave_table(coef_count, jnp.float32)
    half_count = waves.shape[1]
    rimmed = extended_2(charged, (("gx", 1), ("gy", 2)), 1)
    moments = leaf_moments(charged, waves)
    parents = climb_children(moments, child_up.astype(jnp.float32))
    parent_rim = extended_2(parents, (("gx", 1), ("gy", 2)), 2)
    parent_rim = jnp.pad(parent_rim, ((0, 0), (0, 0), (0, 0), (2, 2)))
    half_x, half_y, half_z = (parents.shape[1], parents.shape[2], parents.shape[3])
    phase_grid = block_phase(waves, half_x, half_y, half_z, jnp.float32)
    turned = jnp.sum(rotate_by(parents, phase_grid), axis=(1, 2, 3))
    column = matrix_vector(column_up.astype(jnp.float32), turned)
    column_local = chain_tree(column, tree_up, tree_down, tree_side, lattice)
    leaf_rim = leaf_moments(rimmed, waves)
    leaf_rim = jnp.pad(leaf_rim, ((0, 0), (0, 0), (0, 0), (1, 1)))
    near_terms = near_local(charged, rimmed, counts, near_flags)
    lowered = matrix_vector(column_down.astype(jnp.float32), column_local)
    parent_local = rotate_by(
        jnp.broadcast_to(lowered[:, None, None, None], parents.shape), -phase_grid
    )
    far_parents = parent_offsets()
    parent_stack = jnp.stack(
        [
            parent_rim[
                :,
                2 + offset[0] : 2 + offset[0] + half_x,
                2 + offset[1] : 2 + offset[1] + half_y,
                2 + offset[2] : 2 + offset[2] + half_z,
            ]
            for offset in far_parents
        ]
    )
    parent_turns = offset_phases(waves, far_parents).reshape(len(far_parents), half_count, 1, 1, 1)
    parent_sum = jnp.sum(jax.vmap(rotate_by)(parent_stack, parent_turns), axis=0)
    parent_local = parent_local + jnp.einsum(
        "kj,jxyz->kxyz", parent_far.astype(jnp.float32), parent_sum, precision=highest
    )
    leaf_local = descend_children(parent_local, child_down.astype(jnp.float32))
    near_leaves = leaf_offsets()
    leaf_stack = jnp.stack(
        [
            leaf_rim[
                :,
                1 + offset[0] : 1 + offset[0] + size_x,
                1 + offset[1] : 1 + offset[1] + size_y,
                1 + offset[2] : 1 + offset[2] + size_z,
            ]
            for offset in near_leaves
        ]
    )
    leaf_stack = leaf_stack * (1.0 - near_flags.astype(jnp.float32))[:, None]
    leaf_turns = offset_phases(waves, near_leaves).reshape(len(near_leaves), half_count, 1, 1, 1)
    leaf_sum = jnp.sum(jax.vmap(rotate_by)(leaf_stack, leaf_turns), axis=0)
    leaf_local = leaf_local + jnp.einsum(
        "kj,jxyz->kxyz", leaf_far.astype(jnp.float32), leaf_sum, precision=highest
    )
    potential, field_parts = evaluate(charged, leaf_local, waves)
    return assemble(near_terms, potential, field_parts, charged[3], live_slots)


def solution(mesh):
    in_specs = (
        P(None, "gx", "gy", None, None),
        P("gx", "gy", None),
        P(None, "gx", "gy", None),
        P(),
        P(),
        P(),
        P(),
        P(),
        P(),
        P(),
        P(),
        P(),
        P(),
    )
    out_specs = P(None, "gx", "gy", None, None)
    return jax.shard_map(body, mesh=mesh, in_specs=in_specs, out_specs=out_specs, check_vma=False)
```

profile of v0, /device:TPU:0, one launch (start us, length us, event | category | flops | bytes accessed | tf_op | source)
XLA Modules:
  0.0 145.7 jit_solution(2018368825032895740)
XLA Ops:
  2.7 2.9 %multiply_reduce_fusion.6 = (f32[40,4,4,2]{0,3,2,1:T(2,128)S(1)}, f32[40,4,4,2]{0,3,2,1:T(2,128)S(1)}) fusion(f32[4,4,2,128]{3,2,1,0:T(2,128)S(1)} %bitcast.458, f32[4,4,2,128]{3,2,1,0:T(2,128)S(1)} %get-tuple-element.46, f32[40]{0:T(128)S(1)} %get-tuple-element.112, f32[4,4,2,128]{3,2,1,0:T(2,128)S(1)} %get-tuple-element.47, f32[40]{0:T(128)S(1)} %get-tuple-element.113, ...), kind=kLoop, calls=%fused_computation.55 | loop fusion | flops 1472000 | bytes 76256 | tf_op jit(solution)/shard_map/reduce_sum | solution.py:97
  6.2 3.9 %collective-permute-start.10 = (f32[81,2,2,1]{0,2,1,3:T(2,128)S(1)}, f32[81,2,2,1]{0,2,1,3:T(2,128)S(1)}, u32[]{:S(2)}, u32[]{:S(2)}) collective-permute-start(f32[81,2,2,1]{0,2,1,3:T(2,128)S(1)} %bitcast.472), channel_id=1, source_target_pairs={{8,0},{16,8},{24,16},{0,24},{9,1},{17,9},{25,17},{1,25},{10,2},{18... | collective-permute-start | bytes 3896 | tf_op jit(solution)/shard_map/ppermute | solution.py:30
  10.9 3.0 %collective-permute-start.1 = (f32[4,1,4,2,128]{4,3,2,1,0:T(2,128)S(1)}, f32[4,1,4,2,128]{4,3,2,1,0:T(2,128)S(1)}, u32[]{:S(2)}, u32[]{:S(2)}) collective-permute-start(f32[4,1,4,2,128]{4,3,2,1,0:T(2,128)S(1)} %get-tuple-element.49), channel_id=1, source_target_pairs={{8,0},{16,8},{24,16},{0,24},{9,1},{17,9},{25,17},{1,25},{10,2},{18... | collective-permute-start | bytes 49160 | tf_op jit(solution)/shard_map/ppermute | solution.py:30
  15.0 2.0 %collective-permute-start.4 = (f32[81]{0:T(128)S(1)}, f32[81]{0:T(128)S(1)}, u32[]{:S(2)}, u32[]{:S(2)}) collective-permute-start(f32[81]{0:T(128)S(1)} %bitcast.492), channel_id=1, source_target_pairs={{0,8},{8,0},{16,24},{24,16},{1,9},{9,1},{17,25},{25,17},{2,10},{10... | collective-permute-start | bytes 980 | tf_op jit(solution)/shard_map/ppermute | solution.py:18
  20.8 6.2 %gather_fusion.1 = s32[864]{0:T(1024)S(1)} fusion(s32[27,32]{1,0:T(8,128)S(1)} %stack.99, s32[864]{0:T(1024)S(1)} %reshape.1512), kind=kCustom, calls=%fused_computation.1 | custom fusion | bytes 13824 | tf_op jit(solution)/shard_map/jit(take_along_axis)/gather | solution.py:314
  27.1 7.7 %gather_fusion = pred[864]{0:T(1024)(128)(4,1)S(1)} fusion(pred[27,32]{0,1:T(8,128)(4,1)S(1)} %get-tuple-element.103, s32[864]{0:T(1024)S(1)} %reshape.1512), kind=kCustom, calls=%fused_computation | custom fusion | bytes 8640 | tf_op jit(solution)/shard_map/jit(take_along_axis)/gather | solution.py:315
  37.2 1.4 fusion.97
  41.6 1.6 %collective-permute-start.5 = (f32[81]{0:T(128)S(1)}, f32[81]{0:T(128)S(1)}, u32[]{:S(2)}, u32[]{:S(2)}) collective-permute-start(f32[81]{0:T(128)S(1)} %fusion.12), channel_id=1, source_target_pairs={{0,16},{8,24},{16,0},{24,8},{1,17},{9,25},{17,1},{25,9},{2,18},{10... | collective-permute-start | bytes 980 | tf_op jit(solution)/shard_map/ppermute | solution.py:18
  43.3 1.9 %collective-permute-done.5 = f32[81]{0:T(128)S(1)} collective-permute-done((f32[81]{0:T(128)S(1)}, f32[81]{0:T(128)S(1)}, u32[]{:S(2)}, u32[]{:S(2)}) %collective-permute-start.5) | collective-permute-done | bytes 356 | tf_op jit(solution)/shard_map/ppermute | solution.py:18
  45.5 1.0 collective-permute-done.6
  46.6 1.6 %collective-permute-start.7 = (f32[81]{0:T(128)S(1)}, f32[81]{0:T(128)S(1)}, u32[]{:S(2)}, u32[]{:S(2)}) collective-permute-start(f32[81]{0:T(128)S(1)} %fusion.10), channel_id=1, source_target_pairs={{0,2},{1,3},{2,0},{3,1},{4,6},{5,7},{6,4},{7,5},{8,10},{9,11},{10,... | collective-permute-start | bytes 980 | tf_op jit(solution)/shard_map/ppermute | solution.py:18
  48.5 3.5 %collective-permute-start.12 = (f32[81,6,2,1]{0,2,1,3:T(2,128)S(1)}, f32[81,6,2,1]{0,2,1,3:T(2,128)S(1)}, u32[]{:S(2)}, u32[]{:S(2)}) collective-permute-start(f32[81,6,2,1]{0,2,1,3:T(2,128)S(1)} %pad_maximum_fusion.8), channel_id=1, source_target_pairs={{1,0},{2,1},{3,2},{4,3},{5,4},{6,5},{7,6},{0,7},{9,8},{10,9},{11,1... | collective-permute-start | bytes 11672 | tf_op jit(solution)/shard_map/ppermute | solution.py:30
  53.1 3.5 %collective-permute-done.8 = f32[81]{0:T(128)S(1)} collective-permute-done((f32[81]{0:T(128)S(1)}, f32[81]{0:T(128)S(1)}, u32[]{:S(2)}, u32[]{:S(2)}) %collective-permute-start.8) | collective-permute-done | bytes 356 | tf_op jit(solution)/shard_map/ppermute | solution.py:18
  62.9 3.8 %collective-permute-done.2 = f32[4,6,1,2,128]{4,3,2,1,0:T(2,128)S(1)} collective-permute-done((f32[4,6,1,2,128]{4,3,2,1,0:T(2,128)S(1)}, f32[4,6,1,2,128]{4,3,2,1,0:T(2,128)S(1)}, u32[]{:S(2)}, u32[]{:S(2)}) %collective-permute-start.2) | collective-permute-done | bytes 24608 | tf_op jit(solution)/shard_map/ppermute | solution.py:27
  67.2 6.0 %multiply_reduce_fusion.1 = (f32[40,6,6,2]{0,3,2,1:T(2,128)S(1)}, f32[40,6,6,2]{0,3,2,1:T(2,128)S(1)}) fusion(f32[6,6,2,128]{3,2,1,0:T(2,128)S(1)} %get-tuple-element.28, f32[6,6,2,128]{3,2,1,0:T(2,128)S(1)} %get-tuple-element.29, f32[40]{0:T(128)S(1)} %get-tuple-element.112, f32[6,6,2,128]{3,2,1,0:T(2,128)S(1)} %get-tuple-element.30, ...), kind=kLoop, calls=%fused_computation.3 | loop fusion | flops 3312000 | bytes 170976 | tf_op jit(solution)/shard_map/reduce_sum | solution.py:97
  75.2 6.8 %shard_map.154 = f32[4,128,128]{2,1,0:T(8,128)} custom-call(s32[32]{0:T(128)} %reshape.1502.count_ref, s32[32]{0:T(128)} %convert_reduce_fusion.listed_ref, s32[864]{0:T(1024)} %reshape.1505.place_ref, s32[864]{0:T(1024)} %reshape.1506.kind_ref, f32[4,128,4]{2,1,0:T(8,128)} %get-tuple-element.22.target_ref, f32[72,8,128]{2,1,0:T(8,128)} %pad.11.source_ref, ...), custom_call_target="tpu_custom_call" | custom-call | flops 13107200 | bytes 524288 | tf_op jit(solution)/shard_map/pallas_call | solution.py:324
  82.0 1.1 copy.195
  83.0 7.5 %shard_map.155 = f32[4,128,128]{2,1,0:T(8,128)} custom-call(s32[32]{0:T(128)} %reshape.1502.count_ref, s32[32]{0:T(128)} %convert_reduce_fusion.listed_ref, s32[864]{0:T(1024)} %reshape.1505.place_ref, s32[864]{0:T(1024)} %reshape.1506.kind_ref, f32[4,128,4]{2,1,0:T(8,128)} %get-tuple-element.21.target_ref, f32[72,8,128]{2,1,0:T(8,128)} %pad.11.source_ref, ...), custom_call_target="tpu_custom_call" | custom-call | flops 13107200 | bytes 524288 | tf_op jit(solution)/shard_map/pallas_call | solution.py:324
  90.6 1.1 copy.196
  91.6 6.9 %shard_map.156 = f32[4,128,128]{2,1,0:T(8,128)} custom-call(s32[32]{0:T(128)} %reshape.1502.count_ref, s32[32]{0:T(128)} %convert_reduce_fusion.listed_ref, s32[864]{0:T(1024)} %reshape.1505.place_ref, s32[864]{0:T(1024)} %reshape.1506.kind_ref, f32[4,128,4]{2,1,0:T(8,128)} %get-tuple-element.20.target_ref, f32[72,8,128]{2,1,0:T(8,128)} %pad.11.source_ref, ...), custom_call_target="tpu_custom_call" | custom-call | flops 13107200 | bytes 524288 | tf_op jit(solution)/shard_map/pallas_call | solution.py:324
  98.5 1.1 copy.197
  99.6 7.9 %shard_map.157 = f32[4,128,128]{2,1,0:T(8,128)} custom-call(s32[32]{0:T(128)} %reshape.1502.count_ref, s32[32]{0:T(128)} %convert_reduce_fusion.listed_ref, s32[864]{0:T(1024)} %reshape.1505.place_ref, s32[864]{0:T(1024)} %reshape.1506.kind_ref, f32[4,128,4]{2,1,0:T(8,128)} %get-tuple-element.19.target_ref, f32[72,8,128]{2,1,0:T(8,128)} %pad.11.source_ref, ...), custom_call_target="tpu_custom_call" | custom-call | flops 13107200 | bytes 524288 | tf_op jit(solution)/shard_map/pallas_call | solution.py:324
  107.5 1.1 copy.198
  108.6 6.1 %shard_map.158 = f32[4,128,128]{2,1,0:T(8,128)} custom-call(s32[32]{0:T(128)} %reshape.1502.count_ref, s32[32]{0:T(128)} %convert_reduce_fusion.listed_ref, s32[864]{0:T(1024)} %reshape.1505.place_ref, s32[864]{0:T(1024)} %reshape.1506.kind_ref, f32[4,128,4]{2,1,0:T(8,128)} %get-tuple-element.18.target_ref, f32[72,8,128]{2,1,0:T(8,128)} %pad.11.source_ref, ...), custom_call_target="tpu_custom_call" | custom-call | flops 13107200 | bytes 524288 | tf_op jit(solution)/shard_map/pallas_call | solution.py:324
  114.7 1.1 copy.199
  115.7 7.2 %shard_map.159 = f32[4,128,128]{2,1,0:T(8,128)} custom-call(s32[32]{0:T(128)} %reshape.1502.count_ref, s32[32]{0:T(128)} %convert_reduce_fusion.listed_ref, s32[864]{0:T(1024)} %reshape.1505.place_ref, s32[864]{0:T(1024)} %reshape.1506.kind_ref, f32[4,128,4]{2,1,0:T(8,128)} %get-tuple-element.17.target_ref, f32[72,8,128]{2,1,0:T(8,128)} %pad.11.source_ref, ...), custom_call_target="tpu_custom_call" | custom-call | flops 13107200 | bytes 524288 | tf_op jit(solution)/shard_map/pallas_call | solution.py:324
  122.9 1.1 copy.200
  124.0 6.2 %shard_map.160 = f32[4,128,128]{2,1,0:T(8,128)} custom-call(s32[32]{0:T(128)} %reshape.1502.count_ref, s32[32]{0:T(128)} %convert_reduce_fusion.listed_ref, s32[864]{0:T(1024)} %reshape.1505.place_ref, s32[864]{0:T(1024)} %reshape.1506.kind_ref, f32[4,128,4]{2,1,0:T(8,128)} %get-tuple-element.16.target_ref, f32[72,8,128]{2,1,0:T(8,128)} %pad.11.source_ref, ...), custom_call_target="tpu_custom_call" | custom-call | flops 13107200 | bytes 524288 | tf_op jit(solution)/shard_map/pallas_call | solution.py:324
  130.2 1.1 copy.201
  131.2 7.2 %shard_map.161 = f32[4,128,128]{2,1,0:T(8,128)} custom-call(s32[32]{0:T(128)} %reshape.1502.count_ref, s32[32]{0:T(128)} %convert_reduce_fusion.listed_ref, s32[864]{0:T(1024)} %reshape.1505.place_ref, s32[864]{0:T(1024)} %reshape.1506.kind_ref, f32[4,128,4]{2,1,0:T(8,128)} %get-tuple-element.15.target_ref, f32[72,8,128]{2,1,0:T(8,128)} %pad.11.source_ref, ...), custom_call_target="tpu_custom_call" | custom-call | flops 13107200 | bytes 524288 | tf_op jit(solution)/shard_map/pallas_call | solution.py:324
  138.5 1.1 copy.202
  141.9 3.0 %add_reduce_fusion = (f32[4,4,2,128]{3,2,1,0:T(2,128)S(1)}, f32[4,4,2,128]{3,2,1,0:T(2,128)S(1)}, f32[4,4,2,128]{3,2,1,0:T(2,128)S(1)}, f32[4,4,2,128]{3,2,1,0:T(2,128)S(1)}) fusion(f32[40,4,4,2]{0,3,2,1:T(2,128)S(1)} %copy.253, f32[40,4,4,2]{0,3,2,1:T(2,128)S(1)} %copy.252, f32[4,4,2,128]{3,2,1,0:T(2,128)S(1)} %get-tuple-element.46, ...), kind=kLoop, calls=%fused_computation.53 | loop fusion | flops 2932736 | bytes 125408 | tf_op jit(solution)/shard_map/reduce_sum | solution.py:109
  (317 shorter events, 27.0 us)
Async XLA Ops:
  0.0 5.8 %copy-start = (bf16[8,81,81]{2,0,1:T(8,128)(2,1)S(1)}, bf16[8,81,81]{2,0,1:T(8,128)(2,1)}, u32[]{:S(2)}) copy-start(bf16[8,81,81]{2,0,1:T(8,128)(2,1)} %param.19) | copy-start | bytes 314932
  0.0 17.8 %copy-start.5 = (s32[26,4,4,2]{0,3,2,1:T(2,128)S(1)}, s32[26,4,4,2]{0,3,2,1:T(2,128)}, u32[]{:S(2)}) copy-start(s32[26,4,4,2]{0,3,2,1:T(2,128)} %param.18) | copy-start | bytes 9988
  6.2 42.2 %collective-permute-start.10 = (f32[81,2,2,1]{0,2,1,3:T(2,128)S(1)}, f32[81,2,2,1]{0,2,1,3:T(2,128)S(1)}, u32[]{:S(2)}, u32[]{:S(2)}) collective-permute-start(f32[81,2,2,1]{0,2,1,3:T(2,128)S(1)} %bitcast.472), channel_id=1, source_target_pairs={{8,0},{16,8},{24,16},{0,24},{9,1},{17,9},{25,17},{1,25},{10,2},{18... | collective-permute-start | bytes 3896 | tf_op jit(solution)/shard_map/ppermute | solution.py:30
  10.1 38.3 %collective-permute-start.9 = (f32[81,2,2,1]{0,2,1,3:T(2,128)S(1)}, f32[81,2,2,1]{0,2,1,3:T(2,128)S(1)}, u32[]{:S(2)}, u32[]{:S(2)}) collective-permute-start(f32[81,2,2,1]{0,2,1,3:T(2,128)S(1)} %bitcast.473), channel_id=1, source_target_pairs={{0,8},{8,16},{16,24},{24,0},{1,9},{9,17},{17,25},{25,1},{2,10},{10... | collective-permute-start | bytes 3896 | tf_op jit(solution)/shard_map/ppermute | solution.py:27
  10.9 50.4 %collective-permute-start.1 = (f32[4,1,4,2,128]{4,3,2,1,0:T(2,128)S(1)}, f32[4,1,4,2,128]{4,3,2,1,0:T(2,128)S(1)}, u32[]{:S(2)}, u32[]{:S(2)}) collective-permute-start(f32[4,1,4,2,128]{4,3,2,1,0:T(2,128)S(1)} %get-tuple-element.49), channel_id=1, source_target_pairs={{8,0},{16,8},{24,16},{0,24},{9,1},{17,9},{25,17},{1,25},{10,2},{18... | collective-permute-start | bytes 49160 | tf_op jit(solution)/shard_map/ppermute | solution.py:30
  13.9 47.4 %collective-permute-start = (f32[4,1,4,2,128]{4,3,2,1,0:T(2,128)S(1)}, f32[4,1,4,2,128]{4,3,2,1,0:T(2,128)S(1)}, u32[]{:S(2)}, u32[]{:S(2)}) collective-permute-start(f32[4,1,4,2,128]{4,3,2,1,0:T(2,128)S(1)} %get-tuple-element.48), channel_id=1, source_target_pairs={{0,8},{8,16},{16,24},{24,0},{1,9},{9,17},{17,25},{25,1},{2,10},{10... | collective-permute-start | bytes 49160 | tf_op jit(solution)/shard_map/ppermute | solution.py:27
  15.0 26.5 %collective-permute-start.4 = (f32[81]{0:T(128)S(1)}, f32[81]{0:T(128)S(1)}, u32[]{:S(2)}, u32[]{:S(2)}) collective-permute-start(f32[81]{0:T(128)S(1)} %bitcast.492), channel_id=1, source_target_pairs={{0,8},{8,0},{16,24},{24,16},{1,9},{9,1},{17,25},{25,17},{2,10},{10... | collective-permute-start | bytes 980 | tf_op jit(solution)/shard_map/ppermute | solution.py:18
  37.1 1.6 %copy-start.14 = (f32[98]{0:T(128)S(1)}, f32[98]{0:T(128)}, u32[]{:S(2)}) copy-start(f32[98]{0:T(128)} %constant.266) | copy-start | bytes 1180
  37.1 1.6 %copy-start.15 = (f32[98]{0:T(128)S(1)}, f32[98]{0:T(128)}, u32[]{:S(2)}) copy-start(f32[98]{0:T(128)} %constant.264) | copy-start | bytes 1180
  37.1 1.6 %copy-start.16 = (f32[98]{0:T(128)S(1)}, f32[98]{0:T(128)}, u32[]{:S(2)}) copy-start(f32[98]{0:T(128)} %constant.262) | copy-start | bytes 1180
  37.1 1.9 %copy-start.2 = (bf16[2,2,81,81]{3,1,2,0:T(2,128)(2,1)S(1)}, bf16[2,2,81,81]{3,1,2,0:T(2,128)(2,1)}, u32[]{:S(2)}) copy-start(bf16[2,2,81,81]{3,1,2,0:T(2,128)(2,1)} %param.25) | copy-start | bytes 157468
  37.2 2.3 %copy-start.3 = (bf16[2,2,81,81]{3,1,2,0:T(2,128)(2,1)S(1)}, bf16[2,2,81,81]{3,1,2,0:T(2,128)(2,1)}, u32[]{:S(2)}) copy-start(bf16[2,2,81,81]{3,1,2,0:T(2,128)(2,1)} %param.26) | copy-start | bytes 157468
  37.2 2.4 %copy-start.4 = (bf16[2,2,81,81]{3,1,2,0:T(2,128)(2,1)S(1)}, bf16[2,2,81,81]{3,1,2,0:T(2,128)(2,1)}, u32[]{:S(2)}) copy-start(bf16[2,2,81,81]{3,1,2,0:T(2,128)(2,1)} %param.27) | copy-start | bytes 157468
  38.5 1.7 %copy-start.11 = (f32[26]{0:T(128)S(1)}, f32[26]{0:T(128)}, u32[]{:S(2)}) copy-start(f32[26]{0:T(128)} %constant.272) | copy-start | bytes 316
  38.5 1.7 %copy-start.12 = (f32[26]{0:T(128)S(1)}, f32[26]{0:T(128)}, u32[]{:S(2)}) copy-start(f32[26]{0:T(128)} %constant.270) | copy-start | bytes 316
  38.5 1.7 %copy-start.13 = (f32[26]{0:T(128)S(1)}, f32[26]{0:T(128)}, u32[]{:S(2)}) copy-start(f32[26]{0:T(128)} %constant.268) | copy-start | bytes 316
  38.5 18.2 %copy-start.6 = (bf16[81,81]{1,0:T(8,128)(2,1)S(1)}, bf16[81,81]{1,0:T(8,128)(2,1)}, u32[]{:S(2)}) copy-start(bf16[81,81]{1,0:T(8,128)(2,1)} %param.28) | copy-start | bytes 39370
  38.9 19.6 %copy-start.7 = (bf16[81,81]{1,0:T(8,128)(2,1)S(1)}, bf16[81,81]{1,0:T(8,128)(2,1)}, u32[]{:S(2)}) copy-start(bf16[81,81]{1,0:T(8,128)(2,1)} %param.24) | copy-start | bytes 39370
  40.4 20.7 %copy-start.8 = (bf16[81,81]{1,0:T(8,128)(2,1)S(1)}, bf16[81,81]{1,0:T(8,128)(2,1)}, u32[]{:S(2)}) copy-start(bf16[81,81]{1,0:T(8,128)(2,1)} %param.22) | copy-start | bytes 39370
  40.4 21.5 %copy-start.1 = (bf16[8,81,81]{2,0,1:T(8,128)(2,1)S(1)}, bf16[8,81,81]{2,0,1:T(8,128)(2,1)}, u32[]{:S(2)}) copy-start(bf16[8,81,81]{2,0,1:T(8,128)(2,1)} %param.20) | copy-start | bytes 314932
  41.6 3.6 %collective-permute-start.5 = (f32[81]{0:T(128)S(1)}, f32[81]{0:T(128)S(1)}, u32[]{:S(2)}, u32[]{:S(2)}) collective-permute-start(f32[81]{0:T(128)S(1)} %fusion.12), channel_id=1, source_target_pairs={{0,16},{8,24},{16,0},{24,8},{1,17},{9,25},{17,1},{25,9},{2,18},{10... | collective-permute-start | bytes 980 | tf_op jit(solution)/shard_map/ppermute | solution.py:18
  45.3 1.2 collective-permute-start.6
  46.6 5.4 %collective-permute-start.7 = (f32[81]{0:T(128)S(1)}, f32[81]{0:T(128)S(1)}, u32[]{:S(2)}, u32[]{:S(2)}) collective-permute-start(f32[81]{0:T(128)S(1)} %fusion.10), channel_id=1, source_target_pairs={{0,2},{1,3},{2,0},{3,1},{4,6},{5,7},{6,4},{7,5},{8,10},{9,11},{10,... | collective-permute-start | bytes 980 | tf_op jit(solution)/shard_map/ppermute | solution.py:18
  48.4 10.6 %collective-permute-start.11 = (f32[81,6,2,1]{0,2,1,3:T(2,128)S(1)}, f32[81,6,2,1]{0,2,1,3:T(2,128)S(1)}, u32[]{:S(2)}, u32[]{:S(2)}) collective-permute-start(f32[81,6,2,1]{0,2,1,3:T(2,128)S(1)} %pad_maximum_fusion.8), channel_id=1, source_target_pairs={{0,1},{1,2},{2,3},{3,4},{4,5},{5,6},{6,7},{7,0},{8,9},{9,10},{10,1... | collective-permute-start | bytes 11672 | tf_op jit(solution)/shard_map/ppermute | solution.py:27
  48.5 10.7 %collective-permute-start.12 = (f32[81,6,2,1]{0,2,1,3:T(2,128)S(1)}, f32[81,6,2,1]{0,2,1,3:T(2,128)S(1)}, u32[]{:S(2)}, u32[]{:S(2)}) collective-permute-start(f32[81,6,2,1]{0,2,1,3:T(2,128)S(1)} %pad_maximum_fusion.8), channel_id=1, source_target_pairs={{1,0},{2,1},{3,2},{4,3},{5,4},{6,5},{7,6},{0,7},{9,8},{10,9},{11,1... | collective-permute-start | bytes 11672 | tf_op jit(solution)/shard_map/ppermute | solution.py:30
  52.1 4.5 %collective-permute-start.8 = (f32[81]{0:T(128)S(1)}, f32[81]{0:T(128)S(1)}, u32[]{:S(2)}, u32[]{:S(2)}) collective-permute-start(f32[81]{0:T(128)S(1)} %fusion.9), channel_id=1, source_target_pairs={{0,4},{1,5},{2,6},{3,7},{4,0},{5,1},{6,2},{7,3},{8,12},{9,13},{10,... | collective-permute-start | bytes 980 | tf_op jit(solution)/shard_map/ppermute | solution.py:18
  61.3 1.6 %collective-permute-start.3 = (f32[4,6,1,2,128]{4,3,2,1,0:T(2,128)S(1)}, f32[4,6,1,2,128]{4,3,2,1,0:T(2,128)S(1)}, u32[]{:S(2)}, u32[]{:S(2)}) collective-permute-start(f32[4,6,1,2,128]{4,3,2,1,0:T(2,128)S(1)} %get-tuple-element.33), channel_id=1, source_target_pairs={{1,0},{2,1},{3,2},{4,3},{5,4},{6,5},{7,6},{0,7},{9,8},{10,9},{11,1... | collective-permute-start | bytes 73736 | tf_op jit(solution)/shard_map/ppermute | solution.py:30
  61.4 5.3 %collective-permute-start.2 = (f32[4,6,1,2,128]{4,3,2,1,0:T(2,128)S(1)}, f32[4,6,1,2,128]{4,3,2,1,0:T(2,128)S(1)}, u32[]{:S(2)}, u32[]{:S(2)}) collective-permute-start(f32[4,6,1,2,128]{4,3,2,1,0:T(2,128)S(1)} %get-tuple-element.32), channel_id=1, source_target_pairs={{0,1},{1,2},{2,3},{3,4},{4,5},{5,6},{6,7},{7,0},{8,9},{9,10},{10,1... | collective-permute-start | bytes 73736 | tf_op jit(solution)/shard_map/ppermute | solution.py:27
  67.2 7.2 %copy-start.10 = (f32[27,8]{1,0:T(8,128)S(1)}, f32[27,8]{1,0:T(8,128)}, u32[]{:S(2)}) copy-start(f32[27,8]{1,0:T(8,128)} %constant.249.clone) | copy-start | bytes 2596
  140.3 1.1 copy-start.9
where the time goes:
time: 146 us
  Pallas kernels  55.9 us (38%)
  local copies, waits for them, and re-layouts  35 us (24%)
  other arithmetic  20.5 us (14%)
  starting transfers between devices  17.1 us (12%)
  waiting for transfers between devices  10.8 us (7%)
  matrix products  5.09 us (3%)
    pallas_call x8, Pallas kernels, near_local(): pl.pallas_call(functools.partial(near_kernel, first_leaf), out_shape=jax....  55.9 us
    ppermute x4, starting transfers between devices, extended_2(): lax.ppermute(lax.slice_in_dim(block, 0, width, axis=dim), axis, backward)  10.5 us
    reduce_sum x2, other arithmetic, leaf_moments(): jnp.sum(cosine * charge[None], axis=-1)  8.95 us
    slice x8, local copies, waits for them, and re-layouts, near_local(): out = jnp.concatenate([part[:, :, :4] for part in outs], axis=0)  8.44 us
    gather x3, local copies, waits for them, and re-layouts, near_local(): jnp.take_along_axis(active, order, axis=0)  7.87 us
    ppermute x5, waiting for transfers between devices, from_partner(): return lax.ppermute(value, axis, pairs)  6.45 us
    gather x2, local copies, waits for them, and re-layouts, near_local(): place_list = jnp.take_along_axis(places, order, axis=0)  6.23 us
    ppermute x5, starting transfers between devices, from_partner(): return lax.ppermute(value, axis, pairs)  6.07 us
  transfers between devices with their start and end apart: 13, of which 5 were waited for; matrix products, arithmetic and copies ran while one was open for 22% of the time, Pallas kernels for 0%

commit v1 on v0

--- a/solution.py
+++ b/solution.py
@@ -19,17 +19,30 @@
 
 
 def extended_2(block, sides, width):
+    return extended_joint([(block, width)], sides)[0]
+
+
+def extended_joint(parts, sides):
+    blocks = [block for block, width in parts]
     for axis, dim in sides:
         count = lax.axis_size(axis)
         forward = [(i, i + 1) for i in range(count - 1)]
         forward.append((count - 1, 0))
         backward = [(target, source) for source, target in forward]
-        low = lax.ppermute(
-            lax.slice_in_dim(block, block.shape[dim] - width, None, axis=dim), axis, forward
-        )
-        high = lax.ppermute(lax.slice_in_dim(block, 0, width, axis=dim), axis, backward)
-        block = jnp.concatenate([low, block, high], axis=dim)
-    return block
+        lows = [lax.slice_in_dim(b, b.shape[dim] - w, None, axis=dim) for b, (_, w) in zip(blocks, parts)]
+        highs = [lax.slice_in_dim(b, 0, w, axis=dim) for b, (_, w) in zip(blocks, parts)]
+        sizes = [piece.size for piece in lows]
+        low_all = lax.ppermute(jnp.concatenate([piece.reshape(-1) for piece in lows]), axis, forward)
+        high_all = lax.ppermute(jnp.concatenate([piece.reshape(-1) for piece in highs]), axis, backward)
+        grown = []
+        place = 0
+        for b, piece, size in zip(blocks, lows, sizes):
+            low = low_all[place : place + size].reshape(piece.shape)
+            high = high_all[place : place + size].reshape(piece.shape)
+            place += size
+            grown.append(jnp.concatenate([low, b, high], axis=dim))
+        blocks = grown
+    return blocks
 
 
 def wave_table(coef_count, float_type):
@@ -219,6 +232,51 @@
             pick_side(sideways[axis_num], own_side), partner
         )
     return local_exp
+
+
+def flip_pair(column_grid, axis_num, level_bit):
+    coef_count, size_x, size_y = column_grid.shape
+    span_size = 2**level_bit
+    if axis_num == 0:
+        parted = column_grid.reshape(coef_count, size_x // (2 * span_size), 2, span_size, size_y)
+        return parted[:, :, ::-1].reshape(column_grid.shape)
+    parted = column_grid.reshape(coef_count, size_x, size_y // (2 * span_size), 2, span_size)
+    return parted[:, :, :, ::-1].reshape(column_grid.shape)
+
+
+def side_grid(axis_num, level_bit, size_x, size_y):
+    positions = jnp.arange(size_x if axis_num == 0 else size_y, dtype=jnp.int32)
+    own_side = positions // 2**level_bit % 2
+    return own_side[:, None] if axis_num == 0 else own_side[None, :]
+
+
+def choose_side(matrices, own_side, column_grid):
+    first = jnp.einsum("kj,jxy->kxy", matrices[0], column_grid, precision=highest)
+    second = jnp.einsum("kj,jxy->kxy", matrices[1], column_grid, precision=highest)
+    return jnp.where(own_side[None] == 0, first, second)
+
+
+def gathered_tree(column, tree_up, tree_down, tree_side, lattice):
+    size_x, size_y = lax.axis_size("gx"), lax.axis_size("gy")
+    gathered = lax.all_gather(column, ("gx", "gy")).reshape(size_x, size_y, -1)
+    current = jnp.transpose(gathered, (2, 0, 1))
+    levels = [(0, bit) for bit in range(size_x.bit_length() - 1)] + [
+        (1, bit) for bit in range(size_y.bit_length() - 1)
+    ]
+    visited = []
+    for axis_num, level_bit in levels:
+        partner = flip_pair(current, axis_num, level_bit)
+        own_side = side_grid(axis_num, level_bit, size_x, size_y)
+        climbs = tree_up[axis_num].astype(jnp.float32)
+        current = choose_side(climbs, own_side, current) + choose_side(climbs, 1 - own_side, partner)
+        visited.append((axis_num, own_side, partner))
+    local_exp = jnp.einsum("kj,jxy->kxy", lattice.astype(jnp.float32), current, precision=highest)
+    for axis_num, own_side, partner in reversed(visited):
+        local_exp = choose_side(tree_down[axis_num].astype(jnp.float32), own_side, local_exp) + choose_side(
+            tree_side[axis_num].astype(jnp.float32), own_side, partner
+        )
+    own = lax.dynamic_slice(local_exp, (0, lax.axis_index("gx"), lax.axis_index("gy")), (local_exp.shape[0], 1, 1))
+    return own.reshape(-1)
 
 
 def assemble(near_terms, potential, field_parts, charge, live_slots):
@@ -360,16 +418,15 @@
     charged = jnp.concatenate([atom_data[:3], (atom_data[3] * live_slots)[None]], axis=0)
     waves = wave_table(coef_count, jnp.float32)
     half_count = waves.shape[1]
-    rimmed = extended_2(charged, (("gx", 1), ("gy", 2)), 1)
     moments = leaf_moments(charged, waves)
     parents = climb_children(moments, child_up.astype(jnp.float32))
-    parent_rim = extended_2(parents, (("gx", 1), ("gy", 2)), 2)
+    rimmed, parent_rim = extended_joint([(charged, 1), (parents, 2)], (("gx", 1), ("gy", 2)))
     parent_rim = jnp.pad(parent_rim, ((0, 0), (0, 0), (0, 0), (2, 2)))
     half_x, half_y, half_z = (parents.shape[1], parents.shape[2], parents.shape[3])
     phase_grid = block_phase(waves, half_x, half_y, half_z, jnp.float32)
     turned = jnp.sum(rotate_by(parents, phase_grid), axis=(1, 2, 3))
     column = matrix_vector(column_up.astype(jnp.float32), turned)
-    column_local = chain_tree(column, tree_up, tree_down, tree_side, lattice)
+    column_local = gathered_tree(column, tree_up, tree_down, tree_side, lattice)
     leaf_rim = leaf_moments(rimmed, waves)
     leaf_rim = jnp.pad(leaf_rim, ((0, 0), (0, 0), (0, 0), (1, 1)))
     near_terms = near_local(charged, rimmed, counts, near_flags)

time: 146 us -> 171 us (1.17)
  blocking collectives: 0 us -> 41.1 us
  starting transfers between devices: 17.1 us -> 4.91 us
  waiting for transfers between devices: 10.8 us -> 1.23 us
  matrix products: 5.09 us -> 8.41 us
  local copies, waits for them, and re-layouts: 35 us -> 37.9 us
    unnamed x0 -> x1, blocking collectives: none -> 41.1 us
    ppermute x13 -> x4, starting transfers between devices: 17.1 us -> 4.91 us  [the longest x2 4.9 us: extended_joint(): lax.ppermute(jnp.concatenate([piece.reshape(-1) for piece in highs]), axi...]
    ppermute x13 -> x4, waiting for transfers between devices: 10.8 us -> 1.23 us  [the longest x2 1.23 us: extended_joint(): lax.ppermute(jnp.concatenate([piece.reshape(-1) for piece in lows]), axis...]
    dot_general x0 -> x41, matrix products: none -> 6.45 us  [the longest x20 3.3 us: choose_side(): jnp.einsum('kj,jxy->kxy', matrices[1], column_grid, precision=highest)]
    dot_general x23 -> x2, matrix products: 4.02 us -> 0.87 us  [matrix_vector(): return jnp.dot(matrix, vector, precision=highest)]
  transfers between devices with their start and end apart: 13 -> 4, of which waited for: 5 -> 1; matrix products, arithmetic and copies ran while one was open for 22% -> 19% of each run, Pallas kernels for 0% -> 0%
where the time goes in v1:
time: 171 us
  Pallas kernels  55.7 us (33%)
  blocking collectives  41.1 us (24%)
  local copies, waits for them, and re-layouts  37.9 us (22%)
  other arithmetic  20.5 us (12%)
  matrix products  8.41 us (5%)
  starting transfers between devices  4.91 us (3%)
    pallas_call x8, Pallas kernels, near_local(): pl.pallas_call(functools.partial(near_kernel, first_leaf), out_shape=jax....  55.7 us
    unnamed x1, blocking collectives  41.1 us
    reduce_sum x2, other arithmetic, leaf_moments(): jnp.sum(cosine * charge[None], axis=-1)  8.95 us
    slice x8, local copies, waits for them, and re-layouts, near_local(): out = jnp.concatenate([part[:, :, :4] for part in outs], axis=0)  8.44 us
    gather x3, local copies, waits for them, and re-layouts, near_local(): jnp.take_along_axis(active, order, axis=0)  7.87 us
    gather x2, local copies, waits for them, and re-layouts, near_local(): place_list = jnp.take_along_axis(places, order, axis=0)  6.23 us
    ppermute x2, starting transfers between devices, extended_joint(): lax.ppermute(jnp.concatenate([piece.reshape(-1) for piece in highs]), axi...  4.9 us
  transfers between devices with their start and end apart: 4, of which 1 were waited for; matrix products, arithmetic and copies ran while one was open for 19% of the time, Pallas kernels for 0%

profile of v1, /device:TPU:0, one launch (start us, length us, event | category | flops | bytes accessed | tf_op | source)
XLA Modules:
  0.0 171.2 jit_solution(2235358712489576161)
XLA Ops:
  0.1 0.9 copy.272
  1.0 0.8 slice.625
  1.8 0.9 add_bitcast_fusion.2
  2.6 0.9 fusion.34
  3.5 2.9 %multiply_reduce_fusion.6 = (f32[40,4,4,2]{0,3,2,1:T(2,128)S(1)}, f32[40,4,4,2]{0,3,2,1:T(2,128)S(1)}) fusion(f32[4,4,2,128]{3,2,1,0:T(2,128)S(1)} %bitcast.444, f32[4,4,2,128]{3,2,1,0:T(2,128)S(1)} %get-tuple-element.54, f32[40]{0:T(128)S(1)} %get-tuple-element.102, f32[4,4,2,128]{3,2,1,0:T(2,128)S(1)} %get-tuple-element.55, f32[40]{0:T(128)S(1)} %get-tuple-element.103, ...), kind=kLoop, calls=%fused_computation.52 | loop fusion | flops 1472000 | bytes 76256 | tf_op jit(solution)/shard_map/reduce_sum | solution.py:110
  7.4 3.9 %collective-permute-start.1 = (f32[4420]{0:T(1024)S(1)}, f32[4420]{0:T(1024)S(1)}, u32[]{:S(2)}, u32[]{:S(2)}) collective-permute-start(f32[4420]{0:T(1024)S(1)} %get-tuple-element.100), channel_id=1, source_target_pairs={{8,0},{16,8},{24,16},{0,24},{9,1},{17,9},{25,17},{1,25},{10,2},{18... | collective-permute-start | bytes 53048 | tf_op jit(solution)/shard_map/ppermute | solution.py:36
  12.2 41.1 %all-reduce.3 = f32[2592]{0:T(1024)S(1)} all-reduce(f32[2592]{0:T(1024)S(1)} %dynamic-update-slice), channel_id=2, replica_groups=mesh['gx'=4,'gy'=8] {'gx','gy'}, use_global_device_ids=true, to_apply=%add.3 | all-reduce | flops 2592 | bytes 20736
  62.8 0.8 sort.17
  63.8 6.2 %gather_fusion.1 = s32[864]{0:T(1024)S(1)} fusion(s32[27,32]{1,0:T(8,128)S(1)} %stack.99, s32[864]{0:T(1024)S(1)} %reshape.1791), kind=kCustom, calls=%fused_computation.1 | custom fusion | bytes 13824 | tf_op jit(solution)/shard_map/jit(take_along_axis)/gather | solution.py:372
  70.1 7.7 %gather_fusion = pred[864]{0:T(1024)(128)(4,1)S(1)} fusion(pred[27,32]{0,1:T(8,128)(4,1)S(1)} %get-tuple-element.91, s32[864]{0:T(1024)S(1)} %reshape.1791), kind=kCustom, calls=%fused_computation | custom fusion | bytes 8640 | tf_op jit(solution)/shard_map/jit(take_along_axis)/gather | solution.py:373
  78.6 1.4 fusion.113
  80.6 0.8 convolution_bitcast_fusion.4
  82.9 1.0 collective-permute-start.3
  87.8 1.2 collective-permute-done.2
  89.6 6.0 %multiply_reduce_fusion.1 = (f32[40,6,6,2]{0,3,2,1:T(2,128)S(1)}, f32[40,6,6,2]{0,3,2,1:T(2,128)S(1)}) fusion(f32[6,6,2,128]{3,2,1,0:T(2,128)S(1)} %get-tuple-element.28, f32[6,6,2,128]{3,2,1,0:T(2,128)S(1)} %get-tuple-element.29, f32[40]{0:T(128)S(1)} %get-tuple-element.102, f32[6,6,2,128]{3,2,1,0:T(2,128)S(1)} %get-tuple-element.30, ...), kind=kLoop, calls=%fused_computation.3 | loop fusion | flops 3312000 | bytes 170976 | tf_op jit(solution)/shard_map/reduce_sum | solution.py:110
  97.5 7.2 %shard_map.154 = f32[4,128,128]{2,1,0:T(8,128)} custom-call(s32[32]{0:T(128)} %reshape.1755.count_ref, s32[32]{0:T(128)} %convert_reduce_fusion.listed_ref, s32[864]{0:T(1024)} %reshape.1758.place_ref, s32[864]{0:T(1024)} %reshape.1759.kind_ref, f32[4,128,4]{2,1,0:T(8,128)} %get-tuple-element.22.target_ref, f32[72,8,128]{2,1,0:T(8,128)} %pad.11.source_ref, ...), custom_call_target="tpu_custom_call" | custom-call | flops 13107200 | bytes 524288 | tf_op jit(solution)/shard_map/pallas_call | solution.py:382
  104.7 1.1 copy.289
  105.8 8.8 %shard_map.155 = f32[4,128,128]{2,1,0:T(8,128)} custom-call(s32[32]{0:T(128)} %reshape.1755.count_ref, s32[32]{0:T(128)} %convert_reduce_fusion.listed_ref, s32[864]{0:T(1024)} %reshape.1758.place_ref, s32[864]{0:T(1024)} %reshape.1759.kind_ref, f32[4,128,4]{2,1,0:T(8,128)} %get-tuple-element.21.target_ref, f32[72,8,128]{2,1,0:T(8,128)} %pad.11.source_ref, ...), custom_call_target="tpu_custom_call" | custom-call | flops 13107200 | bytes 524288 | tf_op jit(solution)/shard_map/pallas_call | solution.py:382
  114.6 1.1 copy.290
  115.6 6.8 %shard_map.156 = f32[4,128,128]{2,1,0:T(8,128)} custom-call(s32[32]{0:T(128)} %reshape.1755.count_ref, s32[32]{0:T(128)} %convert_reduce_fusion.listed_ref, s32[864]{0:T(1024)} %reshape.1758.place_ref, s32[864]{0:T(1024)} %reshape.1759.kind_ref, f32[4,128,4]{2,1,0:T(8,128)} %get-tuple-element.20.target_ref, f32[72,8,128]{2,1,0:T(8,128)} %pad.11.source_ref, ...), custom_call_target="tpu_custom_call" | custom-call | flops 13107200 | bytes 524288 | tf_op jit(solution)/shard_map/pallas_call | solution.py:382
  122.5 1.1 copy.291
  123.5 6.4 %shard_map.157 = f32[4,128,128]{2,1,0:T(8,128)} custom-call(s32[32]{0:T(128)} %reshape.1755.count_ref, s32[32]{0:T(128)} %convert_reduce_fusion.listed_ref, s32[864]{0:T(1024)} %reshape.1758.place_ref, s32[864]{0:T(1024)} %reshape.1759.kind_ref, f32[4,128,4]{2,1,0:T(8,128)} %get-tuple-element.19.target_ref, f32[72,8,128]{2,1,0:T(8,128)} %pad.11.source_ref, ...), custom_call_target="tpu_custom_call" | custom-call | flops 13107200 | bytes 524288 | tf_op jit(solution)/shard_map/pallas_call | solution.py:382
  129.9 1.1 copy.292
  131.0 6.4 %shard_map.158 = f32[4,128,128]{2,1,0:T(8,128)} custom-call(s32[32]{0:T(128)} %reshape.1755.count_ref, s32[32]{0:T(128)} %convert_reduce_fusion.listed_ref, s32[864]{0:T(1024)} %reshape.1758.place_ref, s32[864]{0:T(1024)} %reshape.1759.kind_ref, f32[4,128,4]{2,1,0:T(8,128)} %get-tuple-element.18.target_ref, f32[72,8,128]{2,1,0:T(8,128)} %pad.11.source_ref, ...), custom_call_target="tpu_custom_call" | custom-call | flops 13107200 | bytes 524288 | tf_op jit(solution)/shard_map/pallas_call | solution.py:382
  137.4 1.1 copy.293
  138.4 5.8 %shard_map.159 = f32[4,128,128]{2,1,0:T(8,128)} custom-call(s32[32]{0:T(128)} %reshape.1755.count_ref, s32[32]{0:T(128)} %convert_reduce_fusion.listed_ref, s32[864]{0:T(1024)} %reshape.1758.place_ref, s32[864]{0:T(1024)} %reshape.1759.kind_ref, f32[4,128,4]{2,1,0:T(8,128)} %get-tuple-element.17.target_ref, f32[72,8,128]{2,1,0:T(8,128)} %pad.11.source_ref, ...), custom_call_target="tpu_custom_call" | custom-call | flops 13107200 | bytes 524288 | tf_op jit(solution)/shard_map/pallas_call | solution.py:382
  144.2 1.1 copy.294
  145.2 7.3 %shard_map.160 = f32[4,128,128]{2,1,0:T(8,128)} custom-call(s32[32]{0:T(128)} %reshape.1755.count_ref, s32[32]{0:T(128)} %convert_reduce_fusion.listed_ref, s32[864]{0:T(1024)} %reshape.1758.place_ref, s32[864]{0:T(1024)} %reshape.1759.kind_ref, f32[4,128,4]{2,1,0:T(8,128)} %get-tuple-element.16.target_ref, f32[72,8,128]{2,1,0:T(8,128)} %pad.11.source_ref, ...), custom_call_target="tpu_custom_call" | custom-call | flops 13107200 | bytes 524288 | tf_op jit(solution)/shard_map/pallas_call | solution.py:382
  152.5 1.1 copy.295
  153.6 7.0 %shard_map.161 = f32[4,128,128]{2,1,0:T(8,128)} custom-call(s32[32]{0:T(128)} %reshape.1755.count_ref, s32[32]{0:T(128)} %convert_reduce_fusion.listed_ref, s32[864]{0:T(1024)} %reshape.1758.place_ref, s32[864]{0:T(1024)} %reshape.1759.kind_ref, f32[4,128,4]{2,1,0:T(8,128)} %get-tuple-element.15.target_ref, f32[72,8,128]{2,1,0:T(8,128)} %pad.11.source_ref, ...), custom_call_target="tpu_custom_call" | custom-call | flops 13107200 | bytes 524288 | tf_op jit(solution)/shard_map/pallas_call | solution.py:382
  160.6 1.1 copy.296
  167.4 3.0 %add_reduce_fusion = (f32[4,4,2,128]{3,2,1,0:T(2,128)S(1)}, f32[4,4,2,128]{3,2,1,0:T(2,128)S(1)}, f32[4,4,2,128]{3,2,1,0:T(2,128)S(1)}, f32[4,4,2,128]{3,2,1,0:T(2,128)S(1)}) fusion(f32[40,4,4,2]{0,3,2,1:T(2,128)S(1)} %copy.361, f32[40,4,4,2]{0,3,2,1:T(2,128)S(1)} %copy.360, f32[4,4,2,128]{3,2,1,0:T(2,128)S(1)} %get-tuple-element.54, ...), kind=kLoop, calls=%fused_computation.50 | loop fusion | flops 2932736 | bytes 125408 | tf_op jit(solution)/shard_map/reduce_sum | solution.py:122
  (358 shorter events, 26.2 us)
Async XLA Ops:
  0.0 6.7 %copy-start = (bf16[8,81,81]{2,0,1:T(8,128)(2,1)S(1)}, bf16[8,81,81]{2,0,1:T(8,128)(2,1)}, u32[]{:S(2)}) copy-start(bf16[8,81,81]{2,0,1:T(8,128)(2,1)} %param.19) | copy-start | bytes 314932
  0.0 11.8 %copy-start.7 = (bf16[81,81]{1,0:T(8,128)(2,1)S(1)}, bf16[81,81]{1,0:T(8,128)(2,1)}, u32[]{:S(2)}) copy-start(bf16[81,81]{1,0:T(8,128)(2,1)} %param.23) | copy-start | bytes 39370
  0.0 53.3 %copy-start.1 = (bf16[2,2,81,81]{3,1,2,0:T(2,128)(2,1)S(1)}, bf16[2,2,81,81]{3,1,2,0:T(2,128)(2,1)}, u32[]{:S(2)}) copy-start(bf16[2,2,81,81]{3,1,2,0:T(2,128)(2,1)} %param.27) | copy-start | bytes 157468
  0.0 53.5 %copy-start.2 = (bf16[2,2,81,81]{3,1,2,0:T(2,128)(2,1)S(1)}, bf16[2,2,81,81]{3,1,2,0:T(2,128)(2,1)}, u32[]{:S(2)}) copy-start(bf16[2,2,81,81]{3,1,2,0:T(2,128)(2,1)} %param.25) | copy-start | bytes 157468
  7.4 50.1 %copy-start.3 = (bf16[2,2,81,81]{3,1,2,0:T(2,128)(2,1)S(1)}, bf16[2,2,81,81]{3,1,2,0:T(2,128)(2,1)}, u32[]{:S(2)}) copy-start(bf16[2,2,81,81]{3,1,2,0:T(2,128)(2,1)} %param.26) | copy-start | bytes 157468
  7.4 74.5 %collective-permute-start.1 = (f32[4420]{0:T(1024)S(1)}, f32[4420]{0:T(1024)S(1)}, u32[]{:S(2)}, u32[]{:S(2)}) collective-permute-start(f32[4420]{0:T(1024)S(1)} %get-tuple-element.100), channel_id=1, source_target_pairs={{8,0},{16,8},{24,16},{0,24},{9,1},{17,9},{25,17},{1,25},{10,2},{18... | collective-permute-start | bytes 53048 | tf_op jit(solution)/shard_map/ppermute | solution.py:36
  11.4 70.9 %collective-permute-start = (f32[4420]{0:T(1024)S(1)}, f32[4420]{0:T(1024)S(1)}, u32[]{:S(2)}, u32[]{:S(2)}) collective-permute-start(f32[4420]{0:T(1024)S(1)} %get-tuple-element.99), channel_id=1, source_target_pairs={{0,8},{8,16},{16,24},{24,0},{1,9},{9,17},{17,25},{25,1},{2,10},{10... | collective-permute-start | bytes 53048 | tf_op jit(solution)/shard_map/ppermute | solution.py:35
  53.4 4.6 %copy-start.6 = (bf16[81,81]{1,0:T(8,128)(2,1)S(1)}, bf16[81,81]{1,0:T(8,128)(2,1)}, u32[]{:S(2)}) copy-start(bf16[81,81]{1,0:T(8,128)(2,1)} %param.28) | copy-start | bytes 39370
  54.6 6.2 %copy-start.5 = (s32[26,4,4,2]{0,3,2,1:T(2,128)S(1)}, s32[26,4,4,2]{0,3,2,1:T(2,128)}, u32[]{:S(2)}) copy-start(s32[26,4,4,2]{0,3,2,1:T(2,128)} %param.18) | copy-start | bytes 9988
  78.5 2.0 %copy-start.8 = (bf16[81,81]{1,0:T(8,128)(2,1)S(1)}, bf16[81,81]{1,0:T(8,128)(2,1)}, u32[]{:S(2)}) copy-start(bf16[81,81]{1,0:T(8,128)(2,1)} %param.24) | copy-start | bytes 39370
  78.5 3.0 %copy-start.15 = (f32[26]{0:T(128)S(1)}, f32[26]{0:T(128)}, u32[]{:S(2)}) copy-start(f32[26]{0:T(128)} %constant.241) | copy-start | bytes 316
  78.6 3.0 %copy-start.16 = (f32[26]{0:T(128)S(1)}, f32[26]{0:T(128)}, u32[]{:S(2)}) copy-start(f32[26]{0:T(128)} %constant.239) | copy-start | bytes 316
  78.6 3.0 %copy-start.17 = (f32[26]{0:T(128)S(1)}, f32[26]{0:T(128)}, u32[]{:S(2)}) copy-start(f32[26]{0:T(128)} %constant.237) | copy-start | bytes 316
  78.6 3.1 %copy-start.12 = (f32[98]{0:T(128)S(1)}, f32[98]{0:T(128)}, u32[]{:S(2)}) copy-start(f32[98]{0:T(128)} %constant.235) | copy-start | bytes 1180
  78.6 3.1 %copy-start.13 = (f32[98]{0:T(128)S(1)}, f32[98]{0:T(128)}, u32[]{:S(2)}) copy-start(f32[98]{0:T(128)} %constant.233) | copy-start | bytes 1180
  78.6 3.1 %copy-start.14 = (f32[98]{0:T(128)S(1)}, f32[98]{0:T(128)}, u32[]{:S(2)}) copy-start(f32[98]{0:T(128)} %constant.231) | copy-start | bytes 1180
  82.9 4.8 %collective-permute-start.3 = (f32[7116]{0:T(1024)S(1)}, f32[7116]{0:T(1024)S(1)}, u32[]{:S(2)}, u32[]{:S(2)}) collective-permute-start(f32[7116]{0:T(1024)S(1)} %get-tuple-element.90), channel_id=1, source_target_pairs={{1,0},{2,1},{3,2},{4,3},{5,4},{6,5},{7,6},{0,7},{9,8},{10,9},{11,1... | collective-permute-start | bytes 85400 | tf_op jit(solution)/shard_map/ppermute | solution.py:36
  83.9 5.1 %collective-permute-start.2 = (f32[7116]{0:T(1024)S(1)}, f32[7116]{0:T(1024)S(1)}, u32[]{:S(2)}, u32[]{:S(2)}) collective-permute-start(f32[7116]{0:T(1024)S(1)} %get-tuple-element.89), channel_id=1, source_target_pairs={{0,1},{1,2},{2,3},{3,4},{4,5},{5,6},{6,7},{7,0},{8,9},{9,10},{10,1... | collective-permute-start | bytes 85400 | tf_op jit(solution)/shard_map/ppermute | solution.py:35
  89.6 7.1 %copy-start.11 = (f32[27,8]{1,0:T(8,128)S(1)}, f32[27,8]{1,0:T(8,128)}, u32[]{:S(2)}) copy-start(f32[27,8]{1,0:T(8,128)} %constant.218.clone) | copy-start | bytes 2596
  161.9 2.6 %copy-start.9 = (bf16[81,81]{1,0:T(8,128)(2,1)S(1)}, bf16[81,81]{1,0:T(8,128)(2,1)}, u32[]{:S(2)}) copy-start(bf16[81,81]{1,0:T(8,128)(2,1)} %param.22) | copy-start | bytes 39370
  161.9 2.7 %copy-start.4 = (bf16[8,81,81]{2,0,1:T(8,128)(2,1)S(1)}, bf16[8,81,81]{2,0,1:T(8,128)(2,1)}, u32[]{:S(2)}) copy-start(bf16[8,81,81]{2,0,1:T(8,128)(2,1)} %param.20) | copy-start | bytes 314932
  165.8 1.1 copy-start.10

commit v2 on v1

--- a/solution.py
+++ b/solution.py
@@ -210,18 +210,21 @@
     )
 
 
-def chain_tree(column, tree_up, tree_down, tree_side, lattice):
+def chain_tree(column, tree_up, tree_down, tree_side, lattice, hook):
     climbs = tree_up.astype(jnp.float32)
     lowers = tree_down.astype(jnp.float32)
     sideways = tree_side.astype(jnp.float32)
     current = column
     visited = []
+    partner = None
     for level_bit in range(lax.axis_size("gx").bit_length() - 1):
+        current = hook(current, partner)
         partner = from_partner(current, "gx", level_bit)
         own_side = lax.axis_index("gx") // 2**level_bit % 2
         current = pair_step(climbs[0], own_side, current, partner)
         visited.append((0, own_side, partner))
     for level_bit in range(lax.axis_size("gy").bit_length() - 1):
+        current = hook(current, partner)
         partner = from_partner(current, "gy", level_bit)
         own_side = lax.axis_index("gy") // 2**level_bit % 2
         current = pair_step(climbs[1], own_side, current, partner)
@@ -375,23 +378,29 @@
     kind_list = jnp.transpose(order).reshape(-1).astype(jnp.int32)
     count_list = counts.reshape(-1)
     piece = leaf_count // NEAR_PIECES if leaf_count % NEAR_PIECES == 0 else leaf_count
-    outs = []
-    for first_leaf in range(0, leaf_count, piece):
-        pairs = piece * slot_count * slot_count * 10
-        outs.append(
-            pl.pallas_call(
-                functools.partial(near_kernel, first_leaf),
-                out_shape=jax.ShapeDtypeStruct((piece, slot_count, 128), jnp.float32),
-                in_specs=[pl.BlockSpec(memory_space=pltpu.SMEM)] * 4 + [pl.BlockSpec(memory_space=pltpu.VMEM)] * 3,
-                out_specs=pl.BlockSpec(memory_space=pltpu.VMEM),
-                cost_estimate=pl.CostEstimate(
-                    flops=20 * pairs, transcendentals=pairs, bytes_accessed=8 * piece * slot_count * 128
-                ),
-            )(count_list, listed, place_list, kind_list, target[first_leaf : first_leaf + piece], source, shift_table)
-        )
-    out = jnp.concatenate([part[:, :, :4] for part in outs], axis=0)
-    near = jnp.transpose(out, (2, 0, 1))
-    return near.reshape(4, size_x, size_y, size_z, slot_count)
+    pairs = piece * slot_count * slot_count * 10
+
+    def run_piece(number, gate):
+        first_leaf = number * piece
+        own = target[first_leaf : first_leaf + piece]
+        if gate is not None:
+            own, unused = lax.optimization_barrier((own, gate))
+        return pl.pallas_call(
+            functools.partial(near_kernel, first_leaf),
+            out_shape=jax.ShapeDtypeStruct((piece, slot_count, 128), jnp.float32),
+            in_specs=[pl.BlockSpec(memory_space=pltpu.SMEM)] * 4 + [pl.BlockSpec(memory_space=pltpu.VMEM)] * 3,
+            out_specs=pl.BlockSpec(memory_space=pltpu.VMEM),
+            cost_estimate=pl.CostEstimate(
+                flops=20 * pairs, transcendentals=pairs, bytes_accessed=8 * piece * slot_count * 128
+            ),
+        )(count_list, listed, place_list, kind_list, own, source, shift_table)
+
+    def finish_near(outs):
+        out = jnp.concatenate([part[:, :, :4] for part in outs], axis=0)
+        near = jnp.transpose(out, (2, 0, 1))
+        return near.reshape(4, size_x, size_y, size_z, slot_count)
+
+    return leaf_count // piece, run_piece, finish_near
 
 
 def body(
@@ -426,10 +435,23 @@
     phase_grid = block_phase(waves, half_x, half_y, half_z, jnp.float32)
     turned = jnp.sum(rotate_by(parents, phase_grid), axis=(1, 2, 3))
     column = matrix_vector(column_up.astype(jnp.float32), turned)
-    column_local = gathered_tree(column, tree_up, tree_down, tree_side, lattice)
+    piece_count, run_piece, finish_near = near_local(charged, rimmed, counts, near_flags)
+    pieces = []
+
+    def hook(value, prior):
+        number = len(pieces)
+        if number < piece_count:
+            if number > 0:
+                value, unused = lax.optimization_barrier((value, pieces[-1]))
+            pieces.append(run_piece(number, prior))
+        return value
+
+    column_local = chain_tree(column, tree_up, tree_down, tree_side, lattice, hook)
+    while len(pieces) < piece_count:
+        pieces.append(run_piece(len(pieces), None))
+    near_terms = finish_near(pieces)
     leaf_rim = leaf_moments(rimmed, waves)
     leaf_rim = jnp.pad(leaf_rim, ((0, 0), (0, 0), (0, 0), (1, 1)))
-    near_terms = near_local(charged, rimmed, counts, near_flags)
     lowered = matrix_vector(column_down.astype(jnp.float32), column_local)
     parent_local = rotate_by(
         jnp.broadcast_to(lowered[:, None, None, None], parents.shape), -phase_grid

time: 171 us -> 134 us (0.78)
  blocking collectives: 41.1 us -> 0 us
  waiting for transfers between devices: 1.23 us -> 8.73 us
  starting transfers between devices: 4.91 us -> 9.73 us
  matrix products: 8.41 us -> 4.5 us
  local copies, waits for them, and re-layouts: 37.9 us -> 34.6 us
  Pallas kernels: 55.7 us -> 53.7 us
    unnamed x1 -> x0, blocking collectives: 41.1 us -> none
    dot_general x41 -> x0, matrix products: 6.45 us -> none  [the longest x20 3.3 us: choose_side(): jnp.einsum('kj,jxy->kxy', matrices[1], column_grid, precision=highest)]
    ppermute x0 -> x5, waiting for transfers between devices: none -> 4.33 us  [from_partner(): return lax.ppermute(value, axis, pairs)]
    ppermute x0 -> x5, starting transfers between devices: none -> 3.53 us  [from_partner(): return lax.ppermute(value, axis, pairs)]
    slice x12, local copies, waits for them, and re-layouts: 10.2 us -> 7.3 us  [the longest x8 5.67 us: finish_near(): out = jnp.concatenate([part[:, :, :4] for part in outs], axis=0)]
    dot_general x2 -> x23, matrix products: 0.87 us -> 3.41 us  [matrix_vector(): return jnp.dot(matrix, vector, precision=highest)]
    ppermute x2, waiting for transfers between devices: 1.23 us -> 3.53 us  [extended_joint(): lax.ppermute(jnp.concatenate([piece.reshape(-1) for piece in lows]), axis...]
    pallas_call x8, Pallas kernels: 55.7 us -> 53.7 us  [run_piece(): pl.pallas_call(functools.partial(near_kernel, first_leaf), out_shape=jax....]
  transfers between devices with their start and end apart: 4 -> 9, of which waited for: 1 -> 3; matrix products, arithmetic and copies ran while one was open for 19% -> 25% of each run, Pallas kernels for 0% -> 25%
where the time goes in v2:
time: 134 us; the launch traced here: 133 us
  Pallas kernels  53.7 us (40%)
  local copies, waits for them, and re-layouts  34.6 us (26%)
  other arithmetic  20.7 us (15%)
  starting transfers between devices  9.73 us (7%)
  waiting for transfers between devices  8.73 us (7%)
  matrix products  4.5 us (3%)
  between operations  1.42 us (1%)
    pallas_call x8, Pallas kernels, run_piece(): pl.pallas_call(functools.partial(near_kernel, first_leaf), out_shape=jax....  53.7 us
    reduce_sum x2, other arithmetic, leaf_moments(): jnp.sum(cosine * charge[None], axis=-1)  9.13 us
    gather x3, local copies, waits for them, and re-layouts, near_local(): jnp.take_along_axis(active, order, axis=0)  7.87 us
    gather x2, local copies, waits for them, and re-layouts, near_local(): place_list = jnp.take_along_axis(places, order, axis=0)  6.23 us
    ppermute x2, starting transfers between devices, extended_joint(): lax.ppermute(jnp.concatenate([piece.reshape(-1) for piece in highs]), axi...  6.2 us
    slice x8, local copies, waits for them, and re-layouts, finish_near(): out = jnp.concatenate([part[:, :, :4] for part in outs], axis=0)  5.67 us
    ppermute x5, waiting for transfers between devices, from_partner(): return lax.ppermute(value, axis, pairs)  4.33 us
    ppermute x2, waiting for transfers between devices, extended_joint(): lax.ppermute(jnp.concatenate([piece.reshape(-1) for piece in lows]), axis...  3.53 us
  transfers between devices with their start and end apart: 9, of which 3 were waited for; matrix products, arithmetic and copies ran while one was open for 25% of the time, Pallas kernels for 25%

profile of v2, /device:TPU:0, one launch (start us, length us, event | category | flops | bytes accessed | tf_op | source)
XLA Modules:
  0.0 133.4 jit_solution(3748606444246008295)
XLA Ops:
  0.1 0.8 copy.242
  0.9 0.8 slice.549
  1.7 0.9 add_bitcast_fusion.2
  2.6 0.9 fusion.35
  3.5 2.9 %multiply_reduce_fusion.6 = (f32[40,4,4,2]{0,3,2,1:T(2,128)S(1)}, f32[40,4,4,2]{0,3,2,1:T(2,128)S(1)}) fusion(f32[4,4,2,128]{3,2,1,0:T(2,128)S(1)} %bitcast.464, f32[4,4,2,128]{3,2,1,0:T(2,128)S(1)} %get-tuple-element.64, f32[40]{0:T(128)S(1)} %get-tuple-element.132, f32[4,4,2,128]{3,2,1,0:T(2,128)S(1)} %get-tuple-element.65, f32[40]{0:T(128)S(1)} %get-tuple-element.133, ...), kind=kLoop, calls=%fused_computation.55 | loop fusion | flops 1472000 | bytes 76256 | tf_op jit(solution)/shard_map/reduce_sum | solution.py:110
  7.3 3.9 %collective-permute-start.1 = (f32[4420]{0:T(1024)S(1)}, f32[4420]{0:T(1024)S(1)}, u32[]{:S(2)}, u32[]{:S(2)}) collective-permute-start(f32[4420]{0:T(1024)S(1)} %get-tuple-element.130), channel_id=1, source_target_pairs={{8,0},{16,8},{24,16},{0,24},{9,1},{17,9},{25,17},{1,25},{10,2},{18... | collective-permute-start | bytes 53048 | tf_op jit(solution)/shard_map/ppermute | solution.py:36
  11.7 2.0 %collective-permute-start.4 = (f32[81]{0:T(128)S(1)}, f32[81]{0:T(128)S(1)}, u32[]{:S(2)}, u32[]{:S(2)}) collective-permute-start(f32[81]{0:T(128)S(1)} %bitcast.511), channel_id=1, source_target_pairs={{0,8},{8,0},{16,24},{24,16},{1,9},{9,1},{17,25},{25,17},{2,10},{10... | collective-permute-start | bytes 980 | tf_op jit(solution)/shard_map/ppermute | solution.py:18
  15.9 0.8 sort.17
  16.9 6.2 %gather_fusion.1 = s32[864]{0:T(1024)S(1)} fusion(s32[27,32]{1,0:T(8,128)S(1)} %stack.99, s32[864]{0:T(1024)S(1)} %reshape.1605), kind=kCustom, calls=%fused_computation.1 | custom fusion | bytes 13824 | tf_op jit(solution)/shard_map/jit(take_along_axis)/gather | solution.py:375
  23.1 7.7 %gather_fusion = pred[864]{0:T(1024)(128)(4,1)S(1)} fusion(pred[27,32]{0,1:T(8,128)(4,1)S(1)} %get-tuple-element.121, s32[864]{0:T(1024)S(1)} %reshape.1605), kind=kCustom, calls=%fused_computation | custom fusion | bytes 8640 | tf_op jit(solution)/shard_map/jit(take_along_axis)/gather | solution.py:376
  31.6 1.4 %fusion.97 = (f32[4,128,4]{2,1,0:T(8,128)}, f32[4,128,4]{2,1,0:T(8,128)}, f32[4,128,4]{2,1,0:T(8,128)}, f32[4,128,4]{2,1,0:T(8,128)}, f32[4,128,4]{2,1,0:T(8,128...) fusion(f32[32,128,4]{2,1,0:T(8,128)S(1)} %bitcast.461), kind=kLoop, calls=%fused_computation.454 | loop fusion | bytes 131072 | tf_op jit(solution)/shard_map/slice | solution.py:385
  37.4 0.8 convert_reduce_fusion.listed_ref
  39.2 2.3 %collective-permute-start.3 = (f32[7116]{0:T(1024)S(1)}, f32[7116]{0:T(1024)S(1)}, u32[]{:S(2)}, u32[]{:S(2)}) collective-permute-start(f32[7116]{0:T(1024)S(1)} %get-tuple-element.120), channel_id=1, source_target_pairs={{1,0},{2,1},{3,2},{4,3},{5,4},{6,5},{7,6},{0,7},{9,8},{10,9},{11,1... | collective-permute-start | bytes 85400 | tf_op jit(solution)/shard_map/ppermute | solution.py:36
  42.2 0.9 collective-permute-done.3
  43.0 3.5 %collective-permute-done.2 = f32[7116]{0:T(1024)S(1)} collective-permute-done((f32[7116]{0:T(1024)S(1)}, f32[7116]{0:T(1024)S(1)}, u32[]{:S(2)}, u32[]{:S(2)}) %collective-permute-start.2) | collective-permute-done | bytes 28496 | tf_op jit(solution)/shard_map/ppermute | solution.py:35
  47.2 6.2 %multiply_reduce_fusion.1 = (f32[40,6,6,2]{0,3,2,1:T(2,128)S(1)}, f32[40,6,6,2]{0,3,2,1:T(2,128)S(1)}) fusion(f32[6,6,2,128]{3,2,1,0:T(2,128)S(1)} %get-tuple-element.44, f32[6,6,2,128]{3,2,1,0:T(2,128)S(1)} %get-tuple-element.45, f32[40]{0:T(128)S(1)} %get-tuple-element.132, f32[6,6,2,128]{3,2,1,0:T(2,128)S(1)} %get-tuple-element.46, ...), kind=kLoop, calls=%fused_computation.3 | loop fusion | flops 3312000 | bytes 170976 | tf_op jit(solution)/shard_map/reduce_sum | solution.py:110
  55.2 7.4 %shard_map.154 = f32[4,128,128]{2,1,0:T(8,128)} custom-call(s32[32]{0:T(128)} %reshape.1581.count_ref, s32[32]{0:T(128)} %convert_reduce_fusion.listed_ref, s32[864]{0:T(1024)} %reshape.1584.place_ref, s32[864]{0:T(1024)} %reshape.1585.kind_ref, f32[4,128,4]{2,1,0:T(8,128)} %get-tuple-element.38.target_ref, f32[72,8,128]{2,1,0:T(8,128)} %pad.11.source_ref, ...), custom_call_target="tpu_custom_call" | custom-call | flops 13107200 | bytes 524288 | tf_op jit(solution)/shard_map/pallas_call | solution.py:388
  62.6 1.1 copy.262
  63.7 6.9 %shard_map.155 = f32[4,128,128]{2,1,0:T(8,128)} custom-call(s32[32]{0:T(128)} %reshape.1581.count_ref, s32[32]{0:T(128)} %convert_reduce_fusion.listed_ref, s32[864]{0:T(1024)} %reshape.1584.place_ref, s32[864]{0:T(1024)} %reshape.1585.kind_ref, f32[4,128,4]{2,1,0:T(8,128)} %get-tuple-element.15.target_ref, f32[72,8,128]{2,1,0:T(8,128)} %pad.11.source_ref, ...), custom_call_target="tpu_custom_call" | custom-call | flops 13107200 | bytes 524288 | tf_op jit(solution)/shard_map/pallas_call | solution.py:388
  70.5 1.1 copy.263
  71.6 1.5 %collective-permute-start.5 = (f32[81]{0:T(128)S(1)}, f32[81]{0:T(128)S(1)}, u32[]{:S(2)}, u32[]{:S(2)}) collective-permute-start(f32[81]{0:T(128)S(1)} %fusion.12), channel_id=1, source_target_pairs={{0,16},{8,24},{16,0},{24,8},{1,17},{9,25},{17,1},{25,9},{2,18},{10... | collective-permute-start | bytes 980 | tf_op jit(solution)/shard_map/ppermute | solution.py:18
  73.2 8.2 %shard_map.159 = f32[4,128,128]{2,1,0:T(8,128)} custom-call(s32[32]{0:T(128)} %reshape.1581.count_ref, s32[32]{0:T(128)} %convert_reduce_fusion.listed_ref, s32[864]{0:T(1024)} %reshape.1584.place_ref, s32[864]{0:T(1024)} %reshape.1585.kind_ref, f32[4,128,4]{2,1,0:T(8,128)} %get-tuple-element.33.target_ref, f32[72,8,128]{2,1,0:T(8,128)} %pad.11.source_ref, ...), custom_call_target="tpu_custom_call" | custom-call | flops 13107200 | bytes 524288 | tf_op jit(solution)/shard_map/pallas_call | solution.py:388
  81.5 6.8 %shard_map.160 = f32[4,128,128]{2,1,0:T(8,128)} custom-call(s32[32]{0:T(128)} %reshape.1581.count_ref, s32[32]{0:T(128)} %convert_reduce_fusion.listed_ref, s32[864]{0:T(1024)} %reshape.1584.place_ref, s32[864]{0:T(1024)} %reshape.1585.kind_ref, f32[4,128,4]{2,1,0:T(8,128)} %get-tuple-element.32.target_ref, f32[72,8,128]{2,1,0:T(8,128)} %pad.11.source_ref, ...), custom_call_target="tpu_custom_call" | custom-call | flops 13107200 | bytes 524288 | tf_op jit(solution)/shard_map/pallas_call | solution.py:388
  88.2 6.0 %shard_map.161 = f32[4,128,128]{2,1,0:T(8,128)} custom-call(s32[32]{0:T(128)} %reshape.1581.count_ref, s32[32]{0:T(128)} %convert_reduce_fusion.listed_ref, s32[864]{0:T(1024)} %reshape.1584.place_ref, s32[864]{0:T(1024)} %reshape.1585.kind_ref, f32[4,128,4]{2,1,0:T(8,128)} %get-tuple-element.31.target_ref, f32[72,8,128]{2,1,0:T(8,128)} %pad.11.source_ref, ...), custom_call_target="tpu_custom_call" | custom-call | flops 13107200 | bytes 524288 | tf_op jit(solution)/shard_map/pallas_call | solution.py:388
  99.3 6.1 %shard_map.156 = f32[4,128,128]{2,1,0:T(8,128)} custom-call(s32[32]{0:T(128)} %reshape.1581.count_ref, s32[32]{0:T(128)} %convert_reduce_fusion.listed_ref, s32[864]{0:T(1024)} %reshape.1584.place_ref, s32[864]{0:T(1024)} %reshape.1585.kind_ref, f32[4,128,4]{2,1,0:T(8,128)} %get-tuple-element.17.target_ref, f32[72,8,128]{2,1,0:T(8,128)} %pad.11.source_ref, ...), custom_call_target="tpu_custom_call" | custom-call | flops 13107200 | bytes 524288 | tf_op jit(solution)/shard_map/pallas_call | solution.py:388
  105.4 1.1 copy.264
  106.8 5.6 %shard_map.157 = f32[4,128,128]{2,1,0:T(8,128)} custom-call(s32[32]{0:T(128)} %reshape.1581.count_ref, s32[32]{0:T(128)} %convert_reduce_fusion.listed_ref, s32[864]{0:T(1024)} %reshape.1584.place_ref, s32[864]{0:T(1024)} %reshape.1585.kind_ref, f32[4,128,4]{2,1,0:T(8,128)} %get-tuple-element.19.target_ref, f32[72,8,128]{2,1,0:T(8,128)} %pad.11.source_ref, ...), custom_call_target="tpu_custom_call" | custom-call | flops 13107200 | bytes 524288 | tf_op jit(solution)/shard_map/pallas_call | solution.py:388
  112.5 1.1 copy.265
  113.6 6.8 %shard_map.158 = f32[4,128,128]{2,1,0:T(8,128)} custom-call(s32[32]{0:T(128)} %reshape.1581.count_ref, s32[32]{0:T(128)} %convert_reduce_fusion.listed_ref, s32[864]{0:T(1024)} %reshape.1584.place_ref, s32[864]{0:T(1024)} %reshape.1585.kind_ref, f32[4,128,4]{2,1,0:T(8,128)} %get-tuple-element.21.target_ref, f32[72,8,128]{2,1,0:T(8,128)} %pad.11.source_ref, ...), custom_call_target="tpu_custom_call" | custom-call | flops 13107200 | bytes 524288 | tf_op jit(solution)/shard_map/pallas_call | solution.py:388
  120.3 1.1 copy.266
  121.8 4.3 %collective-permute-done.8 = f32[81]{0:T(128)S(1)} collective-permute-done((f32[81]{0:T(128)S(1)}, f32[81]{0:T(128)S(1)}, u32[]{:S(2)}, u32[]{:S(2)}) %collective-permute-start.8) | collective-permute-done | bytes 356 | tf_op jit(solution)/shard_map/ppermute | solution.py:18
  129.6 3.0 %add_reduce_fusion = (f32[4,4,2,128]{3,2,1,0:T(2,128)S(1)}, f32[4,4,2,128]{3,2,1,0:T(2,128)S(1)}, f32[4,4,2,128]{3,2,1,0:T(2,128)S(1)}, f32[4,4,2,128]{3,2,1,0:T(2,128)S(1)}) fusion(f32[40,4,4,2]{0,3,2,1:T(2,128)S(1)} %copy.325, f32[40,4,4,2]{0,3,2,1:T(2,128)S(1)} %copy.324, f32[4,4,2,128]{3,2,1,0:T(2,128)S(1)} %get-tuple-element.64, ...), kind=kLoop, calls=%fused_computation.53 | loop fusion | flops 2932736 | bytes 125408 | tf_op jit(solution)/shard_map/reduce_sum | solution.py:122
  (343 shorter events, 22.2 us)
Async XLA Ops:
  0.0 6.7 %copy-start = (bf16[8,81,81]{2,0,1:T(8,128)(2,1)S(1)}, bf16[8,81,81]{2,0,1:T(8,128)(2,1)}, u32[]{:S(2)}) copy-start(bf16[8,81,81]{2,0,1:T(8,128)(2,1)} %param.19) | copy-start | bytes 314932
  0.0 11.5 %copy-start.9 = (bf16[81,81]{1,0:T(8,128)(2,1)S(1)}, bf16[81,81]{1,0:T(8,128)(2,1)}, u32[]{:S(2)}) copy-start(bf16[81,81]{1,0:T(8,128)(2,1)} %param.23) | copy-start | bytes 39370
  0.0 13.9 %copy-start.8 = (s32[26,4,4,2]{0,3,2,1:T(2,128)S(1)}, s32[26,4,4,2]{0,3,2,1:T(2,128)}, u32[]{:S(2)}) copy-start(s32[26,4,4,2]{0,3,2,1:T(2,128)} %param.18) | copy-start | bytes 9988
  7.3 30.9 %collective-permute-start.1 = (f32[4420]{0:T(1024)S(1)}, f32[4420]{0:T(1024)S(1)}, u32[]{:S(2)}, u32[]{:S(2)}) collective-permute-start(f32[4420]{0:T(1024)S(1)} %get-tuple-element.130), channel_id=1, source_target_pairs={{8,0},{16,8},{24,16},{0,24},{9,1},{17,9},{25,17},{1,25},{10,2},{18... | collective-permute-start | bytes 53048 | tf_op jit(solution)/shard_map/ppermute | solution.py:36
  11.3 27.2 %collective-permute-start = (f32[4420]{0:T(1024)S(1)}, f32[4420]{0:T(1024)S(1)}, u32[]{:S(2)}, u32[]{:S(2)}) collective-permute-start(f32[4420]{0:T(1024)S(1)} %get-tuple-element.129), channel_id=1, source_target_pairs={{0,8},{8,16},{16,24},{24,0},{1,9},{9,17},{17,25},{25,1},{2,10},{10... | collective-permute-start | bytes 53048 | tf_op jit(solution)/shard_map/ppermute | solution.py:35
  11.7 29.8 %collective-permute-start.4 = (f32[81]{0:T(128)S(1)}, f32[81]{0:T(128)S(1)}, u32[]{:S(2)}, u32[]{:S(2)}) collective-permute-start(f32[81]{0:T(128)S(1)} %bitcast.511), channel_id=1, source_target_pairs={{0,8},{8,0},{16,24},{24,16},{1,9},{9,1},{17,25},{25,17},{2,10},{10... | collective-permute-start | bytes 980 | tf_op jit(solution)/shard_map/ppermute | solution.py:18
  31.6 1.4 %copy-start.5 = (bf16[2,2,81,81]{3,1,2,0:T(2,128)(2,1)S(1)}, bf16[2,2,81,81]{3,1,2,0:T(2,128)(2,1)}, u32[]{:S(2)}) copy-start(bf16[2,2,81,81]{3,1,2,0:T(2,128)(2,1)} %param.25) | copy-start | bytes 157468
  31.6 1.9 %copy-start.6 = (bf16[2,2,81,81]{3,1,2,0:T(2,128)(2,1)S(1)}, bf16[2,2,81,81]{3,1,2,0:T(2,128)(2,1)}, u32[]{:S(2)}) copy-start(bf16[2,2,81,81]{3,1,2,0:T(2,128)(2,1)} %param.26) | copy-start | bytes 157468
  31.6 2.0 %copy-start.7 = (bf16[2,2,81,81]{3,1,2,0:T(2,128)(2,1)S(1)}, bf16[2,2,81,81]{3,1,2,0:T(2,128)(2,1)}, u32[]{:S(2)}) copy-start(bf16[2,2,81,81]{3,1,2,0:T(2,128)(2,1)} %param.27) | copy-start | bytes 157468
  33.0 1.2 copy-start.18
  33.0 1.2 copy-start.19
  33.0 1.2 copy-start.20
  33.0 1.4 %copy-start.15 = (f32[98]{0:T(128)S(1)}, f32[98]{0:T(128)}, u32[]{:S(2)}) copy-start(f32[98]{0:T(128)} %constant.266) | copy-start | bytes 1180
  33.1 1.4 %copy-start.16 = (f32[98]{0:T(128)S(1)}, f32[98]{0:T(128)}, u32[]{:S(2)}) copy-start(f32[98]{0:T(128)} %constant.264) | copy-start | bytes 1180
  33.1 1.4 %copy-start.17 = (f32[98]{0:T(128)S(1)}, f32[98]{0:T(128)}, u32[]{:S(2)}) copy-start(f32[98]{0:T(128)} %constant.262) | copy-start | bytes 1180
  39.2 3.8 %collective-permute-start.3 = (f32[7116]{0:T(1024)S(1)}, f32[7116]{0:T(1024)S(1)}, u32[]{:S(2)}, u32[]{:S(2)}) collective-permute-start(f32[7116]{0:T(1024)S(1)} %get-tuple-element.120), channel_id=1, source_target_pairs={{1,0},{2,1},{3,2},{4,3},{5,4},{6,5},{7,6},{0,7},{9,8},{10,9},{11,1... | collective-permute-start | bytes 85400 | tf_op jit(solution)/shard_map/ppermute | solution.py:36
  41.5 5.1 %collective-permute-start.2 = (f32[7116]{0:T(1024)S(1)}, f32[7116]{0:T(1024)S(1)}, u32[]{:S(2)}, u32[]{:S(2)}) collective-permute-start(f32[7116]{0:T(1024)S(1)} %get-tuple-element.119), channel_id=1, source_target_pairs={{0,1},{1,2},{2,3},{3,4},{4,5},{5,6},{6,7},{7,0},{8,9},{9,10},{10,1... | collective-permute-start | bytes 85400 | tf_op jit(solution)/shard_map/ppermute | solution.py:35
  47.2 7.3 %copy-start.14 = (f32[27,8]{1,0:T(8,128)S(1)}, f32[27,8]{1,0:T(8,128)}, u32[]{:S(2)}) copy-start(f32[27,8]{1,0:T(8,128)} %constant.249.clone) | copy-start | bytes 2596
  71.6 27.5 %collective-permute-start.5 = (f32[81]{0:T(128)S(1)}, f32[81]{0:T(128)S(1)}, u32[]{:S(2)}, u32[]{:S(2)}) collective-permute-start(f32[81]{0:T(128)S(1)} %fusion.12), channel_id=1, source_target_pairs={{0,16},{8,24},{16,0},{24,8},{1,17},{9,25},{17,1},{25,9},{2,18},{10... | collective-permute-start | bytes 980 | tf_op jit(solution)/shard_map/ppermute | solution.py:18
  97.1 1.5 %copy-start.1 = (f32[4,128,128]{2,1,0:T(8,128)S(1)}, f32[4,128,128]{2,1,0:T(8,128)}, u32[]{:S(2)}) copy-start(f32[4,128,128]{2,1,0:T(8,128)} %shard_map.159) | copy-start | bytes 786436
  97.2 1.6 %copy-start.2 = (f32[4,128,128]{2,1,0:T(8,128)S(1)}, f32[4,128,128]{2,1,0:T(8,128)}, u32[]{:S(2)}) copy-start(f32[4,128,128]{2,1,0:T(8,128)} %shard_map.160) | copy-start | bytes 786436
  97.2 1.8 %copy-start.3 = (f32[4,128,128]{2,1,0:T(8,128)S(1)}, f32[4,128,128]{2,1,0:T(8,128)}, u32[]{:S(2)}) copy-start(f32[4,128,128]{2,1,0:T(8,128)} %shard_map.161) | copy-start | bytes 786436
  99.2 7.3 %collective-permute-start.6 = (f32[81]{0:T(128)S(1)}, f32[81]{0:T(128)S(1)}, u32[]{:S(2)}, u32[]{:S(2)}) collective-permute-start(f32[81]{0:T(128)S(1)} %fusion.11), channel_id=1, source_target_pairs={{0,1},{1,0},{2,3},{3,2},{4,5},{5,4},{6,7},{7,6},{8,9},{9,8},{10,11... | collective-permute-start | bytes 980 | tf_op jit(solution)/shard_map/ppermute | solution.py:18
  106.6 6.9 %collective-permute-start.7 = (f32[81]{0:T(128)S(1)}, f32[81]{0:T(128)S(1)}, u32[]{:S(2)}, u32[]{:S(2)}) collective-permute-start(f32[81]{0:T(128)S(1)} %fusion.10), channel_id=1, source_target_pairs={{0,2},{1,3},{2,0},{3,1},{4,6},{5,7},{6,4},{7,5},{8,10},{9,11},{10,... | collective-permute-start | bytes 980 | tf_op jit(solution)/shard_map/ppermute | solution.py:18
  106.8 19.4 %copy-start.10 = (bf16[81,81]{1,0:T(8,128)(2,1)S(1)}, bf16[81,81]{1,0:T(8,128)(2,1)}, u32[]{:S(2)}) copy-start(bf16[81,81]{1,0:T(8,128)(2,1)} %param.28) | copy-start | bytes 39370
  112.4 15.6 %copy-start.11 = (bf16[81,81]{1,0:T(8,128)(2,1)S(1)}, bf16[81,81]{1,0:T(8,128)(2,1)}, u32[]{:S(2)}) copy-start(bf16[81,81]{1,0:T(8,128)(2,1)} %param.24) | copy-start | bytes 39370
  112.4 16.0 %copy-start.12 = (bf16[81,81]{1,0:T(8,128)(2,1)S(1)}, bf16[81,81]{1,0:T(8,128)(2,1)}, u32[]{:S(2)}) copy-start(bf16[81,81]{1,0:T(8,128)(2,1)} %param.22) | copy-start | bytes 39370
  112.4 16.2 %copy-start.4 = (bf16[8,81,81]{2,0,1:T(8,128)(2,1)S(1)}, bf16[8,81,81]{2,0,1:T(8,128)(2,1)}, u32[]{:S(2)}) copy-start(bf16[8,81,81]{2,0,1:T(8,128)(2,1)} %param.20) | copy-start | bytes 314932
  112.4 16.7 %copy-start.13 = (bf16[81,81]{1,0:T(8,128)(2,1)S(1)}, bf16[81,81]{1,0:T(8,128)(2,1)}, u32[]{:S(2)}) copy-start(bf16[81,81]{1,0:T(8,128)(2,1)} %param.21) | copy-start | bytes 39370
  121.6 4.5 %collective-permute-start.8 = (f32[81]{0:T(128)S(1)}, f32[81]{0:T(128)S(1)}, u32[]{:S(2)}, u32[]{:S(2)}) collective-permute-start(f32[81]{0:T(128)S(1)} %fusion.9), channel_id=1, source_target_pairs={{0,4},{1,5},{2,6},{3,7},{4,0},{5,1},{6,2},{7,3},{8,12},{9,13},{10,... | collective-permute-start | bytes 980 | tf_op jit(solution)/shard_map/ppermute | solution.py:18

commit v3 on v2

--- a/solution.py
+++ b/solution.py
@@ -306,9 +306,10 @@
     return (pair_term, cube_term * delta_x, cube_term * delta_y, cube_term * delta_z)
 
 
-def near_kernel(first_leaf, count_ref, listed_ref, place_ref, kind_ref, target_ref, source_ref, shift_ref, out_ref):
+def near_kernel(first_leaf, leaf_count, listed_width, table_ref, target_ref, source_ref, shift_ref, out_ref):
     piece_leaves = out_ref.shape[0]
-    listed_width = place_ref.shape[0] // count_ref.shape[0]
+    place_start = 2 * leaf_count
+    kind_start = place_start + leaf_count * listed_width
     rows = NEAR_ROWS
     lanes = out_ref.shape[2]
     out_ref[...] = jnp.zeros(out_ref.shape, out_ref.dtype)
@@ -317,8 +318,8 @@
 
     def leaf_body(local, carry):
         leaf = first_leaf + local
-        chunk_count = (count_ref[leaf] + rows - 1) // rows
-        listed = listed_ref[leaf]
+        chunk_count = (table_ref[leaf] + rows - 1) // rows
+        listed = table_ref[leaf_count + leaf]
         base = leaf * listed_width
 
         def chunk_body(chunk, carry2):
@@ -327,10 +328,10 @@
             tx = jnp.broadcast_to(column[:, 0:1], (rows, lanes))
             ty = jnp.broadcast_to(column[:, 1:2], (rows, lanes))
             tz = jnp.broadcast_to(column[:, 2:3], (rows, lanes))
-            acc = near_pairs(tx, ty, tz, source_ref[place_ref[base]], row + first != lane)
+            acc = near_pairs(tx, ty, tz, source_ref[table_ref[place_start + base]], row + first != lane)
 
             def offset_body(number, acc):
-                srow = source_ref[place_ref[base + number]] + shift_ref[kind_ref[base + number]]
+                srow = source_ref[table_ref[place_start + base + number]] + shift_ref[table_ref[kind_start + base + number]]
                 terms = near_pairs(tx, ty, tz, srow, None)
                 return tuple(a + b for a, b in zip(acc, terms))
 
@@ -370,13 +371,15 @@
     valid = jnp.stack([((layer + offset[2] >= 0) & (layer + offset[2] < size_z)) for offset in offsets[1:]])
     active = (near_flags != 0) & valid[:, None, None, :]
     active = jnp.concatenate([jnp.ones((1, leaf_count), bool), active.reshape(len(offsets) - 1, leaf_count)])
-    order = jnp.argsort(jnp.logical_not(active).astype(jnp.int32), axis=0, stable=True)
     listed = jnp.sum(active.astype(jnp.int32), axis=0)
-    place_list = jnp.take_along_axis(places, order, axis=0)
-    place_list = jnp.where(jnp.take_along_axis(active, order, axis=0), place_list, 0)
-    place_list = jnp.transpose(place_list).reshape(-1)
-    kind_list = jnp.transpose(order).reshape(-1).astype(jnp.int32)
-    count_list = counts.reshape(-1)
+    position = jnp.cumsum(active.astype(jnp.int32), axis=0) - 1
+    slots = jnp.arange(len(offsets), dtype=jnp.int32)
+    chosen = active[None] & (position[None] == slots[:, None, None])
+    kind_list = jnp.sum(jnp.where(chosen, slots[None, :, None], 0), axis=1)
+    place_list = jnp.sum(jnp.where(chosen, places[None], 0), axis=1)
+    table = jnp.concatenate(
+        [counts.reshape(-1), listed, jnp.transpose(place_list).reshape(-1), jnp.transpose(kind_list).reshape(-1)]
+    ).astype(jnp.int32)
     piece = leaf_count // NEAR_PIECES if leaf_count % NEAR_PIECES == 0 else leaf_count
     pairs = piece * slot_count * slot_count * 10
 
@@ -386,14 +389,14 @@
         if gate is not None:
             own, unused = lax.optimization_barrier((own, gate))
         return pl.pallas_call(
-            functools.partial(near_kernel, first_leaf),
+            functools.partial(near_kernel, first_leaf, leaf_count, len(offsets)),
             out_shape=jax.ShapeDtypeStruct((piece, slot_count, 128), jnp.float32),
-            in_specs=[pl.BlockSpec(memory_space=pltpu.SMEM)] * 4 + [pl.BlockSpec(memory_space=pltpu.VMEM)] * 3,
+            in_specs=[pl.BlockSpec(memory_space=pltpu.SMEM)] + [pl.BlockSpec(memory_space=pltpu.VMEM)] * 3,
             out_specs=pl.BlockSpec(memory_space=pltpu.VMEM),
             cost_estimate=pl.CostEstimate(
                 flops=20 * pairs, transcendentals=pairs, bytes_accessed=8 * piece * slot_count * 128
             ),
-        )(count_list, listed, place_list, kind_list, own, source, shift_table)
+        )(table, own, source, shift_table)
 
     def finish_near(outs):
         out = jnp.concatenate([part[:, :, :4] for part in outs], axis=0)
@@ -429,7 +432,7 @@
     half_count = waves.shape[1]
     moments = leaf_moments(charged, waves)
     parents = climb_children(moments, child_up.astype(jnp.float32))
-    rimmed, parent_rim = extended_joint([(charged, 1), (parents, 2)], (("gx", 1), ("gy", 2)))
+    rimmed, parent_rim, leaf_rim = extended_joint([(charged, 1), (parents, 2), (moments, 1)], (("gx", 1), ("gy", 2)))
     parent_rim = jnp.pad(parent_rim, ((0, 0), (0, 0), (0, 0), (2, 2)))
     half_x, half_y, half_z = (parents.shape[1], parents.shape[2], parents.shape[3])
     phase_grid = block_phase(waves, half_x, half_y, half_z, jnp.float32)
@@ -450,7 +453,6 @@
     while len(pieces) < piece_count:
         pieces.append(run_piece(len(pieces), None))
     near_terms = finish_near(pieces)
-    leaf_rim = leaf_moments(rimmed, waves)
     leaf_rim = jnp.pad(leaf_rim, ((0, 0), (0, 0), (0, 0), (1, 1)))
     lowered = matrix_vector(column_down.astype(jnp.float32), column_local)
     parent_local = rotate_by(

time: 134 us -> 116 us (0.87)
  local copies, waits for them, and re-layouts: 34.6 us -> 22.5 us
  other arithmetic: 20.7 us -> 13.2 us
  starting transfers between devices: 9.73 us -> 13.3 us
  waiting for transfers between devices: 8.73 us -> 6 us
    gather x5 -> x0, local copies, waits for them, and re-layouts: 14.1 us -> none  [the longest x3 7.87 us: near_local(): jnp.take_along_axis(active, order, axis=0)]
    reduce_sum x2 -> x1, other arithmetic: 9.13 us -> 2.91 us  [leaf_moments(): jnp.sum(cosine * charge[None], axis=-1)]
    ppermute x5, starting transfers between devices: 3.53 us -> 7.04 us  [from_partner(): return lax.ppermute(value, axis, pairs)]
    ppermute x5, waiting for transfers between devices: 4.33 us -> 1.42 us  [from_partner(): return lax.ppermute(value, axis, pairs)]
    reshape x3, local copies, waits for them, and re-layouts: 2.01 us -> 0.29 us  [the longest x1 0.1 us: near_local(): jnp.transpose(place_list).reshape(-1)]
  transfers between devices with their start and end apart: 9 -> 9, of which waited for: 3 -> 3; matrix products, arithmetic and copies ran while one was open for 25% -> 17% of each run, Pallas kernels for 25% -> 29%
where the time goes in v3:
time: 116 us; the launch traced here: 115 us
  Pallas kernels  53.9 us (46%)
  local copies, waits for them, and re-layouts  22.5 us (19%)
  starting transfers between devices  13.3 us (11%)
  other arithmetic  13.2 us (11%)
  waiting for transfers between devices  6 us (5%)
  matrix products  4.41 us (4%)
  between operations  1.51 us (1%)
    pallas_call x8, Pallas kernels, run_piece(): pl.pallas_call(functools.partial(near_kernel, first_leaf, leaf_count, len...  53.9 us
    ppermute x5, starting transfers between devices, from_partner(): return lax.ppermute(value, axis, pairs)  7.04 us
    ppermute x2, starting transfers between devices, extended_joint(): lax.ppermute(jnp.concatenate([piece.reshape(-1) for piece in highs]), axi...  6.1 us
    slice x8, local copies, waits for them, and re-layouts, finish_near(): out = jnp.concatenate([part[:, :, :4] for part in outs], axis=0)  5.68 us
    ppermute x2, waiting for transfers between devices, extended_joint(): lax.ppermute(jnp.concatenate([piece.reshape(-1) for piece in lows]), axis...  4.16 us
    dot_general x23, matrix products, matrix_vector(): return jnp.dot(matrix, vector, precision=highest)  3.31 us
    reduce_sum x1, other arithmetic, evaluate(): jnp.sum(cos_local * cosine + sin_local * sine_part, axis=0)  2.97 us
    reduce_sum x1, other arithmetic, leaf_moments(): jnp.sum(cosine * charge[None], axis=-1)  2.91 us
  transfers between devices with their start and end apart: 9, of which 3 were waited for; matrix products, arithmetic and copies ran while one was open for 17% of the time, Pallas kernels for 29%

profile of v3, /device:TPU:0, one launch (start us, length us, event | category | flops | bytes accessed | tf_op | source)
XLA Modules:
  0.0 114.9 jit_solution(14978080484068008387)
XLA Ops:
  0.1 0.8 copy.283
  0.9 0.8 slice.584
  1.7 0.9 add_bitcast_fusion.2
  2.6 0.9 fusion.42
  3.5 2.9 %multiply_reduce_fusion.4 = (f32[40,4,4,2]{0,3,2,1:T(2,128)S(1)}, f32[40,4,4,2]{0,3,2,1:T(2,128)S(1)}) fusion(f32[4,4,2,128]{3,2,1,0:T(2,128)S(1)} %bitcast.464, f32[4,4,2,128]{3,2,1,0:T(2,128)S(1)} %get-tuple-element.75, f32[40]{0:T(128)S(1)} %get-tuple-element.130, f32[4,4,2,128]{3,2,1,0:T(2,128)S(1)} %get-tuple-element.76, f32[40]{0:T(128)S(1)} %get-tuple-element.131, ...), kind=kLoop, calls=%fused_computation.50 | loop fusion | flops 1472000 | bytes 76256 | tf_op jit(solution)/shard_map/reduce_sum | solution.py:110
  8.1 3.9 %collective-permute-start.1 = (f32[5068]{0:T(1024)S(1)}, f32[5068]{0:T(1024)S(1)}, u32[]{:S(2)}, u32[]{:S(2)}) collective-permute-start(f32[5068]{0:T(1024)S(1)} %concatenate.99), channel_id=1, source_target_pairs={{8,0},{16,8},{24,16},{0,24},{9,1},{17,9},{25,17},{1,25},{10,2},{18... | collective-permute-start | bytes 60824 | tf_op jit(solution)/shard_map/ppermute | solution.py:36
  12.8 2.0 %collective-permute-start.4 = (f32[81]{0:T(128)S(1)}, f32[81]{0:T(128)S(1)}, u32[]{:S(2)}, u32[]{:S(2)}) collective-permute-start(f32[81]{0:T(128)S(1)} %bitcast.509), channel_id=1, source_target_pairs={{0,8},{8,0},{16,24},{24,16},{1,9},{9,1},{17,25},{25,17},{2,10},{10... | collective-permute-start | bytes 980 | tf_op jit(solution)/shard_map/ppermute | solution.py:18
  17.0 0.6 copy.288
  17.8 1.4 %fusion.90 = (f32[4,128,4]{2,1,0:T(8,128)}, f32[4,128,4]{2,1,0:T(8,128)}, f32[4,128,4]{2,1,0:T(8,128)}, f32[4,128,4]{2,1,0:T(8,128)}, f32[4,128,4]{2,1,0:T(8,128...) fusion(f32[32,128,4]{2,1,0:T(8,128)S(1)} %bitcast.461), kind=kLoop, calls=%fused_computation.449 | loop fusion | bytes 131072 | tf_op jit(solution)/shard_map/slice | solution.py:388
  22.1 0.7 concatenate.91.table_ref
  25.2 2.2 %collective-permute-start.3 = (f32[8088]{0:T(1024)S(1)}, f32[8088]{0:T(1024)S(1)}, u32[]{:S(2)}, u32[]{:S(2)}) collective-permute-start(f32[8088]{0:T(1024)S(1)} %concatenate.104), channel_id=1, source_target_pairs={{1,0},{2,1},{3,2},{4,3},{5,4},{6,5},{7,6},{0,7},{9,8},{10,9},{11,1... | collective-permute-start | bytes 97064 | tf_op jit(solution)/shard_map/ppermute | solution.py:36
  29.5 4.2 %collective-permute-done.2 = f32[8088]{0:T(1024)S(1)} collective-permute-done((f32[8088]{0:T(1024)S(1)}, f32[8088]{0:T(1024)S(1)}, u32[]{:S(2)}, u32[]{:S(2)}) %collective-permute-start.2) | collective-permute-done | bytes 32384 | tf_op jit(solution)/shard_map/ppermute | solution.py:35
  34.3 0.7 pad.11.source_ref
  35.1 0.7 broadcast_in_dim.39.shift_ref
  35.8 6.3 %shard_map.154 = f32[4,128,128]{2,1,0:T(8,128)} custom-call(s32[1792]{0:T(1024)} %concatenate.91.table_ref, f32[4,128,4]{2,1,0:T(8,128)} %get-tuple-element.36.target_ref, f32[72,8,128]{2,1,0:T(8,128)} %pad.11.source_ref, f32[27,8,128]{2,1,0:T(8,128)} %broadcast_in_dim.39.shift_ref), custom_call_target="tpu_custom_call" | custom-call | flops 13107200 | bytes 524288 | tf_op jit(solution)/shard_map/pallas_call | solution.py:391
  42.1 1.1 copy.313
  43.1 7.6 %shard_map.155 = f32[4,128,128]{2,1,0:T(8,128)} custom-call(s32[1792]{0:T(1024)} %concatenate.91.table_ref, f32[4,128,4]{2,1,0:T(8,128)} %get-tuple-element.13.target_ref, f32[72,8,128]{2,1,0:T(8,128)} %pad.11.source_ref, f32[27,8,128]{2,1,0:T(8,128)} %broadcast_in_dim.39.shift_ref), custom_call_target="tpu_custom_call" | custom-call | flops 13107200 | bytes 524288 | tf_op jit(solution)/shard_map/pallas_call | solution.py:391
  50.7 1.1 copy.314
  52.0 7.9 %shard_map.159 = f32[4,128,128]{2,1,0:T(8,128)} custom-call(s32[1792]{0:T(1024)} %concatenate.91.table_ref, f32[4,128,4]{2,1,0:T(8,128)} %get-tuple-element.31.target_ref, f32[72,8,128]{2,1,0:T(8,128)} %pad.11.source_ref, f32[27,8,128]{2,1,0:T(8,128)} %broadcast_in_dim.39.shift_ref), custom_call_target="tpu_custom_call" | custom-call | flops 13107200 | bytes 524288 | tf_op jit(solution)/shard_map/pallas_call | solution.py:391
  59.9 5.8 %shard_map.160 = f32[4,128,128]{2,1,0:T(8,128)} custom-call(s32[1792]{0:T(1024)} %concatenate.91.table_ref, f32[4,128,4]{2,1,0:T(8,128)} %get-tuple-element.30.target_ref, f32[72,8,128]{2,1,0:T(8,128)} %pad.11.source_ref, f32[27,8,128]{2,1,0:T(8,128)} %broadcast_in_dim.39.shift_ref), custom_call_target="tpu_custom_call" | custom-call | flops 13107200 | bytes 524288 | tf_op jit(solution)/shard_map/pallas_call | solution.py:391
  65.7 6.0 %shard_map.161 = f32[4,128,128]{2,1,0:T(8,128)} custom-call(s32[1792]{0:T(1024)} %concatenate.91.table_ref, f32[4,128,4]{2,1,0:T(8,128)} %get-tuple-element.29.target_ref, f32[72,8,128]{2,1,0:T(8,128)} %pad.11.source_ref, f32[27,8,128]{2,1,0:T(8,128)} %broadcast_in_dim.39.shift_ref), custom_call_target="tpu_custom_call" | custom-call | flops 13107200 | bytes 524288 | tf_op jit(solution)/shard_map/pallas_call | solution.py:391
  77.1 7.3 %shard_map.156 = f32[4,128,128]{2,1,0:T(8,128)} custom-call(s32[1792]{0:T(1024)} %concatenate.91.table_ref, f32[4,128,4]{2,1,0:T(8,128)} %get-tuple-element.15.target_ref, f32[72,8,128]{2,1,0:T(8,128)} %pad.11.source_ref, f32[27,8,128]{2,1,0:T(8,128)} %broadcast_in_dim.39.shift_ref), custom_call_target="tpu_custom_call" | custom-call | flops 13107200 | bytes 524288 | tf_op jit(solution)/shard_map/pallas_call | solution.py:391
  84.4 1.1 copy.315
  85.7 1.2 %collective-permute-start.7 = (f32[81]{0:T(128)S(1)}, f32[81]{0:T(128)S(1)}, u32[]{:S(2)}, u32[]{:S(2)}) collective-permute-start(f32[81]{0:T(128)S(1)} %fusion.10), channel_id=1, source_target_pairs={{0,2},{1,3},{2,0},{3,1},{4,6},{5,7},{6,4},{7,5},{8,10},{9,11},{10,... | collective-permute-start | bytes 980 | tf_op jit(solution)/shard_map/ppermute | solution.py:18
  87.0 6.5 %shard_map.157 = f32[4,128,128]{2,1,0:T(8,128)} custom-call(s32[1792]{0:T(1024)} %concatenate.91.table_ref, f32[4,128,4]{2,1,0:T(8,128)} %get-tuple-element.17.target_ref, f32[72,8,128]{2,1,0:T(8,128)} %pad.11.source_ref, f32[27,8,128]{2,1,0:T(8,128)} %broadcast_in_dim.39.shift_ref), custom_call_target="tpu_custom_call" | custom-call | flops 13107200 | bytes 524288 | tf_op jit(solution)/shard_map/pallas_call | solution.py:391
  93.5 1.1 copy.316
  94.5 6.4 %shard_map.158 = f32[4,128,128]{2,1,0:T(8,128)} custom-call(s32[1792]{0:T(1024)} %concatenate.91.table_ref, f32[4,128,4]{2,1,0:T(8,128)} %get-tuple-element.19.target_ref, f32[72,8,128]{2,1,0:T(8,128)} %pad.11.source_ref, f32[27,8,128]{2,1,0:T(8,128)} %broadcast_in_dim.39.shift_ref), custom_call_target="tpu_custom_call" | custom-call | flops 13107200 | bytes 524288 | tf_op jit(solution)/shard_map/pallas_call | solution.py:391
  101.0 1.1 copy.317
  102.3 3.8 %collective-permute-start.8 = (f32[81]{0:T(128)S(1)}, f32[81]{0:T(128)S(1)}, u32[]{:S(2)}, u32[]{:S(2)}) collective-permute-start(f32[81]{0:T(128)S(1)} %fusion.9), channel_id=1, source_target_pairs={{0,4},{1,5},{2,6},{3,7},{4,0},{5,1},{6,2},{7,3},{8,12},{9,13},{10,... | collective-permute-start | bytes 980 | tf_op jit(solution)/shard_map/ppermute | solution.py:18
  106.1 1.4 %collective-permute-done.8 = f32[81]{0:T(128)S(1)} collective-permute-done((f32[81]{0:T(128)S(1)}, f32[81]{0:T(128)S(1)}, u32[]{:S(2)}, u32[]{:S(2)}) %collective-permute-start.8) | collective-permute-done | bytes 356 | tf_op jit(solution)/shard_map/ppermute | solution.py:18
  111.1 3.0 %add_reduce_fusion = (f32[4,4,2,128]{3,2,1,0:T(2,128)S(1)}, f32[4,4,2,128]{3,2,1,0:T(2,128)S(1)}, f32[4,4,2,128]{3,2,1,0:T(2,128)S(1)}, f32[4,4,2,128]{3,2,1,0:T(2,128)S(1)}) fusion(f32[40,4,4,2]{0,3,2,1:T(2,128)S(1)} %copy.383, f32[40,4,4,2]{0,3,2,1:T(2,128)S(1)} %copy.382, f32[4,4,2,128]{3,2,1,0:T(2,128)S(1)} %get-tuple-element.75, ...), kind=kLoop, calls=%fused_computation.48 | loop fusion | flops 2932736 | bytes 125408 | tf_op jit(solution)/shard_map/reduce_sum | solution.py:122
  114.2 0.7 pad_maximum_fusion.1
  (361 shorter events, 21.4 us)
Async XLA Ops:
  0.0 6.7 %copy-start = (bf16[8,81,81]{2,0,1:T(8,128)(2,1)S(1)}, bf16[8,81,81]{2,0,1:T(8,128)(2,1)}, u32[]{:S(2)}) copy-start(bf16[8,81,81]{2,0,1:T(8,128)(2,1)} %param.19) | copy-start | bytes 314932
  0.0 12.7 %copy-start.9 = (bf16[81,81]{1,0:T(8,128)(2,1)S(1)}, bf16[81,81]{1,0:T(8,128)(2,1)}, u32[]{:S(2)}) copy-start(bf16[81,81]{1,0:T(8,128)(2,1)} %param.23) | copy-start | bytes 39370
  0.0 15.0 %copy-start.8 = (s32[26,4,4,2]{0,3,2,1:T(2,128)S(1)}, s32[26,4,4,2]{0,3,2,1:T(2,128)}, u32[]{:S(2)}) copy-start(s32[26,4,4,2]{0,3,2,1:T(2,128)} %param.18) | copy-start | bytes 9988
  8.1 14.7 %collective-permute-start.1 = (f32[5068]{0:T(1024)S(1)}, f32[5068]{0:T(1024)S(1)}, u32[]{:S(2)}, u32[]{:S(2)}) collective-permute-start(f32[5068]{0:T(1024)S(1)} %concatenate.99), channel_id=1, source_target_pairs={{8,0},{16,8},{24,16},{0,24},{9,1},{17,9},{25,17},{1,25},{10,2},{18... | collective-permute-start | bytes 60824 | tf_op jit(solution)/shard_map/ppermute | solution.py:36
  12.4 10.7 %collective-permute-start = (f32[5068]{0:T(1024)S(1)}, f32[5068]{0:T(1024)S(1)}, u32[]{:S(2)}, u32[]{:S(2)}) collective-permute-start(f32[5068]{0:T(1024)S(1)} %concatenate.98), channel_id=1, source_target_pairs={{0,8},{8,16},{16,24},{24,0},{1,9},{9,17},{17,25},{25,1},{2,10},{10... | collective-permute-start | bytes 60824 | tf_op jit(solution)/shard_map/ppermute | solution.py:35
  12.8 14.6 %collective-permute-start.4 = (f32[81]{0:T(128)S(1)}, f32[81]{0:T(128)S(1)}, u32[]{:S(2)}, u32[]{:S(2)}) collective-permute-start(f32[81]{0:T(128)S(1)} %bitcast.509), channel_id=1, source_target_pairs={{0,8},{8,0},{16,24},{24,16},{1,9},{9,1},{17,25},{25,17},{2,10},{10... | collective-permute-start | bytes 980 | tf_op jit(solution)/shard_map/ppermute | solution.py:18
  17.6 1.5 %copy-start.5 = (bf16[2,2,81,81]{3,1,2,0:T(2,128)(2,1)S(1)}, bf16[2,2,81,81]{3,1,2,0:T(2,128)(2,1)}, u32[]{:S(2)}) copy-start(bf16[2,2,81,81]{3,1,2,0:T(2,128)(2,1)} %param.25) | copy-start | bytes 157468
  17.7 1.9 %copy-start.6 = (bf16[2,2,81,81]{3,1,2,0:T(2,128)(2,1)S(1)}, bf16[2,2,81,81]{3,1,2,0:T(2,128)(2,1)}, u32[]{:S(2)}) copy-start(bf16[2,2,81,81]{3,1,2,0:T(2,128)(2,1)} %param.26) | copy-start | bytes 157468
  17.7 2.0 %copy-start.7 = (bf16[2,2,81,81]{3,1,2,0:T(2,128)(2,1)S(1)}, bf16[2,2,81,81]{3,1,2,0:T(2,128)(2,1)}, u32[]{:S(2)}) copy-start(bf16[2,2,81,81]{3,1,2,0:T(2,128)(2,1)} %param.27) | copy-start | bytes 157468
  17.7 2.9 %copy-start.18 = (f32[26]{0:T(128)S(1)}, f32[26]{0:T(128)}, u32[]{:S(2)}) copy-start(f32[26]{0:T(128)} %constant.246) | copy-start | bytes 316
  17.7 2.9 %copy-start.19 = (f32[26]{0:T(128)S(1)}, f32[26]{0:T(128)}, u32[]{:S(2)}) copy-start(f32[26]{0:T(128)} %constant.244) | copy-start | bytes 316
  17.7 2.9 %copy-start.20 = (f32[26]{0:T(128)S(1)}, f32[26]{0:T(128)}, u32[]{:S(2)}) copy-start(f32[26]{0:T(128)} %constant.242) | copy-start | bytes 316
  17.7 3.0 %copy-start.15 = (f32[98]{0:T(128)S(1)}, f32[98]{0:T(128)}, u32[]{:S(2)}) copy-start(f32[98]{0:T(128)} %constant.240) | copy-start | bytes 1180
  17.7 3.0 %copy-start.16 = (f32[98]{0:T(128)S(1)}, f32[98]{0:T(128)}, u32[]{:S(2)}) copy-start(f32[98]{0:T(128)} %constant.238) | copy-start | bytes 1180
  17.7 3.0 %copy-start.17 = (f32[98]{0:T(128)S(1)}, f32[98]{0:T(128)}, u32[]{:S(2)}) copy-start(f32[98]{0:T(128)} %constant.236) | copy-start | bytes 1180
  25.0 10.1 %copy-start.14 = (f32[27,8]{1,0:T(8,128)S(1)}, f32[27,8]{1,0:T(8,128)}, u32[]{:S(2)}) copy-start(f32[27,8]{1,0:T(8,128)} %constant.223.clone) | copy-start | bytes 2596
  25.2 4.0 %collective-permute-start.3 = (f32[8088]{0:T(1024)S(1)}, f32[8088]{0:T(1024)S(1)}, u32[]{:S(2)}, u32[]{:S(2)}) collective-permute-start(f32[8088]{0:T(1024)S(1)} %concatenate.104), channel_id=1, source_target_pairs={{1,0},{2,1},{3,2},{4,3},{5,4},{6,5},{7,6},{0,7},{9,8},{10,9},{11,1... | collective-permute-start | bytes 97064 | tf_op jit(solution)/shard_map/ppermute | solution.py:36
  28.4 5.3 %collective-permute-start.2 = (f32[8088]{0:T(1024)S(1)}, f32[8088]{0:T(1024)S(1)}, u32[]{:S(2)}, u32[]{:S(2)}) collective-permute-start(f32[8088]{0:T(1024)S(1)} %concatenate.103), channel_id=1, source_target_pairs={{0,1},{1,2},{2,3},{3,4},{4,5},{5,6},{6,7},{7,0},{8,9},{9,10},{10,1... | collective-permute-start | bytes 97064 | tf_op jit(solution)/shard_map/ppermute | solution.py:35
  51.8 25.0 %collective-permute-start.5 = (f32[81]{0:T(128)S(1)}, f32[81]{0:T(128)S(1)}, u32[]{:S(2)}, u32[]{:S(2)}) collective-permute-start(f32[81]{0:T(128)S(1)} %fusion.12), channel_id=1, source_target_pairs={{0,16},{8,24},{16,0},{24,8},{1,17},{9,25},{17,1},{25,9},{2,18},{10... | collective-permute-start | bytes 980 | tf_op jit(solution)/shard_map/ppermute | solution.py:18
  74.4 2.1 %copy-start.1 = (f32[4,128,128]{2,1,0:T(8,128)S(1)}, f32[4,128,128]{2,1,0:T(8,128)}, u32[]{:S(2)}) copy-start(f32[4,128,128]{2,1,0:T(8,128)} %shard_map.159) | copy-start | bytes 786436
  74.4 2.2 %copy-start.2 = (f32[4,128,128]{2,1,0:T(8,128)S(1)}, f32[4,128,128]{2,1,0:T(8,128)}, u32[]{:S(2)}) copy-start(f32[4,128,128]{2,1,0:T(8,128)} %shard_map.160) | copy-start | bytes 786436
  74.9 1.8 %copy-start.3 = (f32[4,128,128]{2,1,0:T(8,128)S(1)}, f32[4,128,128]{2,1,0:T(8,128)}, u32[]{:S(2)}) copy-start(f32[4,128,128]{2,1,0:T(8,128)} %shard_map.161) | copy-start | bytes 786436
  76.9 8.6 %collective-permute-start.6 = (f32[81]{0:T(128)S(1)}, f32[81]{0:T(128)S(1)}, u32[]{:S(2)}, u32[]{:S(2)}) collective-permute-start(f32[81]{0:T(128)S(1)} %fusion.11), channel_id=1, source_target_pairs={{0,1},{1,0},{2,3},{3,2},{4,5},{5,4},{6,7},{7,6},{8,9},{9,8},{10,11... | collective-permute-start | bytes 980 | tf_op jit(solution)/shard_map/ppermute | solution.py:18
  84.4 23.3 %copy-start.10 = (bf16[81,81]{1,0:T(8,128)(2,1)S(1)}, bf16[81,81]{1,0:T(8,128)(2,1)}, u32[]{:S(2)}) copy-start(bf16[81,81]{1,0:T(8,128)(2,1)} %param.28) | copy-start | bytes 39370
  84.4 25.1 %copy-start.11 = (bf16[81,81]{1,0:T(8,128)(2,1)S(1)}, bf16[81,81]{1,0:T(8,128)(2,1)}, u32[]{:S(2)}) copy-start(bf16[81,81]{1,0:T(8,128)(2,1)} %param.24) | copy-start | bytes 39370
  84.4 25.5 %copy-start.12 = (bf16[81,81]{1,0:T(8,128)(2,1)S(1)}, bf16[81,81]{1,0:T(8,128)(2,1)}, u32[]{:S(2)}) copy-start(bf16[81,81]{1,0:T(8,128)(2,1)} %param.22) | copy-start | bytes 39370
  84.4 25.7 %copy-start.4 = (bf16[8,81,81]{2,0,1:T(8,128)(2,1)S(1)}, bf16[8,81,81]{2,0,1:T(8,128)(2,1)}, u32[]{:S(2)}) copy-start(bf16[8,81,81]{2,0,1:T(8,128)(2,1)} %param.20) | copy-start | bytes 314932
  84.4 26.2 %copy-start.13 = (bf16[81,81]{1,0:T(8,128)(2,1)S(1)}, bf16[81,81]{1,0:T(8,128)(2,1)}, u32[]{:S(2)}) copy-start(bf16[81,81]{1,0:T(8,128)(2,1)} %param.21) | copy-start | bytes 39370
  85.7 8.9 %collective-permute-start.7 = (f32[81]{0:T(128)S(1)}, f32[81]{0:T(128)S(1)}, u32[]{:S(2)}, u32[]{:S(2)}) collective-permute-start(f32[81]{0:T(128)S(1)} %fusion.10), channel_id=1, source_target_pairs={{0,2},{1,3},{2,0},{3,1},{4,6},{5,7},{6,4},{7,5},{8,10},{9,11},{10,... | collective-permute-start | bytes 980 | tf_op jit(solution)/shard_map/ppermute | solution.py:18
  102.3 5.3 %collective-permute-start.8 = (f32[81]{0:T(128)S(1)}, f32[81]{0:T(128)S(1)}, u32[]{:S(2)}, u32[]{:S(2)}) collective-permute-start(f32[81]{0:T(128)S(1)} %fusion.9), channel_id=1, source_target_pairs={{0,4},{1,5},{2,6},{3,7},{4,0},{5,1},{6,2},{7,3},{8,12},{9,13},{10,... | collective-permute-start | bytes 980 | tf_op jit(solution)/shard_map/ppermute | solution.py:18

commit v4 on v3

--- a/solution.py
+++ b/solution.py
@@ -306,13 +306,12 @@
     return (pair_term, cube_term * delta_x, cube_term * delta_y, cube_term * delta_z)
 
 
-def near_kernel(first_leaf, leaf_count, listed_width, table_ref, target_ref, source_ref, shift_ref, out_ref):
+def near_kernel(first_leaf, leaf_count, listed_width, table_ref, target_ref, source_ref, shift_ref, out_ref, tile_ref):
     piece_leaves = out_ref.shape[0]
     place_start = 2 * leaf_count
     kind_start = place_start + leaf_count * listed_width
     rows = NEAR_ROWS
     lanes = out_ref.shape[2]
-    out_ref[...] = jnp.zeros(out_ref.shape, out_ref.dtype)
     lane = lax.broadcasted_iota(jnp.int32, (rows, lanes), 1)
     row = lax.broadcasted_iota(jnp.int32, (rows, lanes), 0)
 
@@ -321,6 +320,7 @@
         chunk_count = (table_ref[leaf] + rows - 1) // rows
         listed = table_ref[leaf_count + leaf]
         base = leaf * listed_width
+        tile_ref[...] = jnp.zeros(tile_ref.shape, tile_ref.dtype)
 
         def chunk_body(chunk, carry2):
             first = pl.multiple_of(chunk * rows, rows)
@@ -330,20 +330,24 @@
             tz = jnp.broadcast_to(column[:, 2:3], (rows, lanes))
             acc = near_pairs(tx, ty, tz, source_ref[table_ref[place_start + base]], row + first != lane)
 
-            def offset_body(number, acc):
-                srow = source_ref[table_ref[place_start + base + number]] + shift_ref[table_ref[kind_start + base + number]]
-                terms = near_pairs(tx, ty, tz, srow, None)
-                return tuple(a + b for a, b in zip(acc, terms))
-
-            acc = lax.fori_loop(1, listed, offset_body, acc)
+            def offset_body(pair_number, acc):
+                number = base + 1 + 2 * pair_number
+                first_row = source_ref[table_ref[place_start + number]] + shift_ref[table_ref[kind_start + number]]
+                second_row = source_ref[table_ref[place_start + number + 1]] + shift_ref[table_ref[kind_start + number + 1]]
+                first_terms = near_pairs(tx, ty, tz, first_row, None)
+                second_terms = near_pairs(tx, ty, tz, second_row, None)
+                return tuple(a + b + c for a, b, c in zip(acc, first_terms, second_terms))
+
+            acc = lax.fori_loop(0, listed // 2, offset_body, acc)
             sums = [jnp.sum(part, axis=1, keepdims=True) for part in acc]
             tile = jnp.where(
                 lane == 0, sums[0], jnp.where(lane == 1, sums[1], jnp.where(lane == 2, sums[2], sums[3]))
             )
-            out_ref[local, pl.ds(first, rows), :] = jnp.where(lane < 4, tile, 0.0)
+            tile_ref[pl.ds(first, rows), :] = jnp.where(lane < 4, tile, 0.0)
             return carry2
 
         lax.fori_loop(0, chunk_count, chunk_body, 0)
+        out_ref[local] = jnp.transpose(tile_ref[...])[0 : out_ref.shape[1], :]
         return carry
 
     lax.fori_loop(0, piece_leaves, leaf_body, 0)
@@ -355,7 +359,8 @@
     ext_y = size_y + 2
     target = jnp.transpose(charged, (1, 2, 3, 4, 0)).reshape(leaf_count, slot_count, 4)
     source = jnp.transpose(rimmed, (1, 2, 3, 0, 4)).reshape(-1, 4, slot_count)
-    source = jnp.pad(source, ((0, 0), (0, 4), (0, 0)))
+    source = jnp.pad(source, ((0, 1), (0, 4), (0, 0)))
+    empty_leaf = source.shape[0] - 1
     offsets = [(0, 0, 0)] + leaf_offsets()
     shift_rows = jnp.array([[float(v) for v in offset] + [0.0] * 5 for offset in offsets], jnp.float32)
     shift_table = jnp.broadcast_to(shift_rows[:, :, None], (len(offsets), 8, slot_count))
@@ -372,11 +377,13 @@
     active = (near_flags != 0) & valid[:, None, None, :]
     active = jnp.concatenate([jnp.ones((1, leaf_count), bool), active.reshape(len(offsets) - 1, leaf_count)])
     listed = jnp.sum(active.astype(jnp.int32), axis=0)
+    listed = listed + (listed + 1) % 2
     position = jnp.cumsum(active.astype(jnp.int32), axis=0) - 1
     slots = jnp.arange(len(offsets), dtype=jnp.int32)
     chosen = active[None] & (position[None] == slots[:, None, None])
     kind_list = jnp.sum(jnp.where(chosen, slots[None, :, None], 0), axis=1)
     place_list = jnp.sum(jnp.where(chosen, places[None], 0), axis=1)
+    place_list = jnp.where(slots[:, None] < jnp.sum(active.astype(jnp.int32), axis=0)[None], place_list, empty_leaf)
     table = jnp.concatenate(
         [counts.reshape(-1), listed, jnp.transpose(place_list).reshape(-1), jnp.transpose(kind_list).reshape(-1)]
     ).astype(jnp.int32)
@@ -390,17 +397,18 @@
             own, unused = lax.optimization_barrier((own, gate))
         return pl.pallas_call(
             functools.partial(near_kernel, first_leaf, leaf_count, len(offsets)),
-            out_shape=jax.ShapeDtypeStruct((piece, slot_count, 128), jnp.float32),
+            out_shape=jax.ShapeDtypeStruct((piece, 8, slot_count), jnp.float32),
             in_specs=[pl.BlockSpec(memory_space=pltpu.SMEM)] + [pl.BlockSpec(memory_space=pltpu.VMEM)] * 3,
             out_specs=pl.BlockSpec(memory_space=pltpu.VMEM),
+            scratch_shapes=[pltpu.VMEM((slot_count, 128), jnp.float32)],
             cost_estimate=pl.CostEstimate(
                 flops=20 * pairs, transcendentals=pairs, bytes_accessed=8 * piece * slot_count * 128
             ),
         )(table, own, source, shift_table)
 
     def finish_near(outs):
-        out = jnp.concatenate([part[:, :, :4] for part in outs], axis=0)
-        near = jnp.transpose(out, (2, 0, 1))
+        out = jnp.concatenate(outs, axis=0)
+        near = jnp.transpose(out[:, :4, :], (1, 0, 2))
         return near.reshape(4, size_x, size_y, size_z, slot_count)
 
     return leaf_count // piece, run_piece, finish_near

time: 116 us -> 111 us (0.957)
  waiting for transfers between devices: 6 us -> 10.7 us
  Pallas kernels: 53.9 us -> 50 us
  starting transfers between devices: 13.3 us -> 10.5 us
  local copies, waits for them, and re-layouts: 22.5 us -> 19.8 us
    slice x8 -> x0, local copies, waits for them, and re-layouts: 5.68 us -> none  [finish_near(): out = jnp.concatenate([part[:, :, :4] for part in outs], axis=0)]
    ppermute x5, waiting for transfers between devices: 1.42 us -> 6.11 us  [from_partner(): return lax.ppermute(value, axis, pairs)]
    pallas_call x8, Pallas kernels: 53.9 us -> 50 us  [run_piece(): pl.pallas_call(functools.partial(near_kernel, first_leaf, leaf_count, len...]
    unnamed x159 -> x168, local copies, waits for them, and re-layouts: 1.99 us -> 4.99 us
    ppermute x5, starting transfers between devices: 7.04 us -> 4.19 us  [from_partner(): return lax.ppermute(value, axis, pairs)]
  transfers between devices with their start and end apart: 9 -> 9, of which waited for: 3 -> 5; matrix products, arithmetic and copies ran while one was open for 17% -> 17% of each run, Pallas kernels for 29% -> 16%
where the time goes in v4:
time: 111 us; the launch traced here: 110 us
  Pallas kernels  50 us (45%)
  local copies, waits for them, and re-layouts  19.8 us (18%)
  other arithmetic  13.2 us (12%)
  waiting for transfers between devices  10.7 us (10%)
  starting transfers between devices  10.5 us (9%)
  matrix products  4.43 us (4%)
  between operations  1.56 us (1%)
    pallas_call x8, Pallas kernels, run_piece(): pl.pallas_call(functools.partial(near_kernel, first_leaf, leaf_count, len...  50 us
    ppermute x5, waiting for transfers between devices, from_partner(): return lax.ppermute(value, axis, pairs)  6.11 us
    ppermute x2, starting transfers between devices, extended_joint(): lax.ppermute(jnp.concatenate([piece.reshape(-1) for piece in highs]), axi...  6.1 us
    unnamed x168, local copies, waits for them, and re-layouts  4.99 us
    ppermute x5, starting transfers between devices, from_partner(): return lax.ppermute(value, axis, pairs)  4.19 us
    ppermute x2, waiting for transfers between devices, extended_joint(): lax.ppermute(jnp.concatenate([piece.reshape(-1) for piece in lows]), axis...  4.16 us
    dot_general x23, matrix products, matrix_vector(): return jnp.dot(matrix, vector, precision=highest)  3.33 us
    reduce_sum x1, other arithmetic, evaluate(): jnp.sum(cos_local * cosine + sin_local * sine_part, axis=0)  2.97 us
  transfers between devices with their start and end apart: 9, of which 5 were waited for; matrix products, arithmetic and copies ran while one was open for 17% of the time, Pallas kernels for 16%

profile of v4, /device:TPU:0, one launch (start us, length us, event | category | flops | bytes accessed | tf_op | source)
XLA Modules:
  0.0 110.1 jit_solution(12237383379047109808)
XLA Ops:
  0.1 0.8 copy.357
  0.9 0.8 slice.563
  1.7 0.9 add_bitcast_fusion.2
  2.6 0.9 fusion.42
  3.5 2.9 %multiply_reduce_fusion.4 = (f32[40,4,4,2]{0,3,2,1:T(2,128)S(1)}, f32[40,4,4,2]{0,3,2,1:T(2,128)S(1)}) fusion(f32[4,4,2,128]{3,2,1,0:T(2,128)S(1)} %bitcast.458, f32[4,4,2,128]{3,2,1,0:T(2,128)S(1)} %get-tuple-element.75, f32[40]{0:T(128)S(1)} %get-tuple-element.130, f32[4,4,2,128]{3,2,1,0:T(2,128)S(1)} %get-tuple-element.76, f32[40]{0:T(128)S(1)} %get-tuple-element.131, ...), kind=kLoop, calls=%fused_computation.50 | loop fusion | flops 1472000 | bytes 76256 | tf_op jit(solution)/shard_map/reduce_sum | solution.py:110
  8.1 3.9 %collective-permute-start.1 = (f32[5068]{0:T(1024)S(1)}, f32[5068]{0:T(1024)S(1)}, u32[]{:S(2)}, u32[]{:S(2)}) collective-permute-start(f32[5068]{0:T(1024)S(1)} %concatenate.99), channel_id=1, source_target_pairs={{8,0},{16,8},{24,16},{0,24},{9,1},{17,9},{25,17},{1,25},{10,2},{18... | collective-permute-start | bytes 60824 | tf_op jit(solution)/shard_map/ppermute | solution.py:36
  12.8 2.0 %collective-permute-start.4 = (f32[81]{0:T(128)S(1)}, f32[81]{0:T(128)S(1)}, u32[]{:S(2)}, u32[]{:S(2)}) collective-permute-start(f32[81]{0:T(128)S(1)} %bitcast.493), channel_id=1, source_target_pairs={{0,8},{8,0},{16,24},{24,16},{1,9},{9,1},{17,25},{25,17},{2,10},{10... | collective-permute-start | bytes 980 | tf_op jit(solution)/shard_map/ppermute | solution.py:18
  17.4 0.6 copy.362
  18.1 1.3 %fusion.92 = (f32[4,128,4]{2,1,0:T(8,128)}, f32[4,128,4]{2,1,0:T(8,128)}, f32[4,128,4]{2,1,0:T(8,128)}, f32[4,128,4]{2,1,0:T(8,128)}, f32[4,128,4]{2,1,0:T(8,128...) fusion(f32[32,128,4]{2,1,0:T(8,128)S(1)} %bitcast.455), kind=kLoop, calls=%fused_computation.465 | loop fusion | bytes 131072 | tf_op jit(solution)/shard_map/slice | solution.py:395
  22.1 0.7 concatenate.91.table_ref
  25.2 2.2 %collective-permute-start.3 = (f32[8088]{0:T(1024)S(1)}, f32[8088]{0:T(1024)S(1)}, u32[]{:S(2)}, u32[]{:S(2)}) collective-permute-start(f32[8088]{0:T(1024)S(1)} %concatenate.104), channel_id=1, source_target_pairs={{1,0},{2,1},{3,2},{4,3},{5,4},{6,5},{7,6},{0,7},{9,8},{10,9},{11,1... | collective-permute-start | bytes 97064 | tf_op jit(solution)/shard_map/ppermute | solution.py:36
  29.5 4.2 %collective-permute-done.2 = f32[8088]{0:T(1024)S(1)} collective-permute-done((f32[8088]{0:T(1024)S(1)}, f32[8088]{0:T(1024)S(1)}, u32[]{:S(2)}, u32[]{:S(2)}) %collective-permute-start.2) | collective-permute-done | bytes 32384 | tf_op jit(solution)/shard_map/ppermute | solution.py:35
  34.3 0.7 pad.11.source_ref
  35.1 0.7 broadcast_in_dim.44.shift_ref
  35.8 6.5 %shard_map.154 = f32[4,8,128]{2,1,0:T(8,128)} custom-call(s32[1792]{0:T(1024)} %concatenate.91.table_ref, f32[4,128,4]{2,1,0:T(8,128)} %get-tuple-element.36.target_ref, f32[73,8,128]{2,1,0:T(8,128)} %pad.11.source_ref, f32[27,8,128]{2,1,0:T(8,128)} %broadcast_in_dim.44.shift_ref), custom_call_target="tpu_custom_call" | custom-call | flops 13107200 | bytes 524288 | tf_op jit(solution)/shard_map/pallas_call | solution.py:398
  42.3 0.7 constant_dynamic-update-slice_fusion.7
  43.0 5.7 %shard_map.155 = f32[4,8,128]{2,1,0:T(8,128)} custom-call(s32[1792]{0:T(1024)} %concatenate.91.table_ref, f32[4,128,4]{2,1,0:T(8,128)} %get-tuple-element.13.target_ref, f32[73,8,128]{2,1,0:T(8,128)} %pad.11.source_ref, f32[27,8,128]{2,1,0:T(8,128)} %broadcast_in_dim.44.shift_ref), custom_call_target="tpu_custom_call" | custom-call | flops 13107200 | bytes 524288 | tf_op jit(solution)/shard_map/pallas_call | solution.py:398
  48.8 1.0 collective-permute-start.5
  49.9 6.2 %shard_map.159 = f32[4,8,128]{2,1,0:T(8,128)} custom-call(s32[1792]{0:T(1024)} %concatenate.91.table_ref, f32[4,128,4]{2,1,0:T(8,128)} %get-tuple-element.31.target_ref, f32[73,8,128]{2,1,0:T(8,128)} %pad.11.source_ref, f32[27,8,128]{2,1,0:T(8,128)} %broadcast_in_dim.44.shift_ref), custom_call_target="tpu_custom_call" | custom-call | flops 13107200 | bytes 524288 | tf_op jit(solution)/shard_map/pallas_call | solution.py:398
  56.1 5.8 %shard_map.160 = f32[4,8,128]{2,1,0:T(8,128)} custom-call(s32[1792]{0:T(1024)} %concatenate.91.table_ref, f32[4,128,4]{2,1,0:T(8,128)} %get-tuple-element.30.target_ref, f32[73,8,128]{2,1,0:T(8,128)} %pad.11.source_ref, f32[27,8,128]{2,1,0:T(8,128)} %broadcast_in_dim.44.shift_ref), custom_call_target="tpu_custom_call" | custom-call | flops 13107200 | bytes 524288 | tf_op jit(solution)/shard_map/pallas_call | solution.py:398
  66.7 5.9 %shard_map.161 = f32[4,8,128]{2,1,0:T(8,128)} custom-call(s32[1792]{0:T(1024)} %concatenate.91.table_ref, f32[4,128,4]{2,1,0:T(8,128)} %get-tuple-element.29.target_ref, f32[73,8,128]{2,1,0:T(8,128)} %pad.11.source_ref, f32[27,8,128]{2,1,0:T(8,128)} %broadcast_in_dim.44.shift_ref), custom_call_target="tpu_custom_call" | custom-call | flops 13107200 | bytes 524288 | tf_op jit(solution)/shard_map/pallas_call | solution.py:398
  72.6 7.7 %shard_map.156 = f32[4,8,128]{2,1,0:T(8,128)} custom-call(s32[1792]{0:T(1024)} %concatenate.91.table_ref, f32[4,128,4]{2,1,0:T(8,128)} %get-tuple-element.15.target_ref, f32[73,8,128]{2,1,0:T(8,128)} %pad.11.source_ref, f32[27,8,128]{2,1,0:T(8,128)} %broadcast_in_dim.44.shift_ref), custom_call_target="tpu_custom_call" | custom-call | flops 13107200 | bytes 524288 | tf_op jit(solution)/shard_map/pallas_call | solution.py:398
  80.5 0.8 constant_dynamic-update-slice_fusion.5
  81.5 5.8 %shard_map.157 = f32[4,8,128]{2,1,0:T(8,128)} custom-call(s32[1792]{0:T(1024)} %concatenate.91.table_ref, f32[4,128,4]{2,1,0:T(8,128)} %get-tuple-element.17.target_ref, f32[73,8,128]{2,1,0:T(8,128)} %pad.11.source_ref, f32[27,8,128]{2,1,0:T(8,128)} %broadcast_in_dim.44.shift_ref), custom_call_target="tpu_custom_call" | custom-call | flops 13107200 | bytes 524288 | tf_op jit(solution)/shard_map/pallas_call | solution.py:398
  87.6 0.8 constant_dynamic-update-slice_fusion.4
  88.4 2.7 %collective-permute-done.7 = f32[81]{0:T(128)S(1)} collective-permute-done((f32[81]{0:T(128)S(1)}, f32[81]{0:T(128)S(1)}, u32[]{:S(2)}, u32[]{:S(2)}) %collective-permute-start.7) | collective-permute-done | bytes 356 | tf_op jit(solution)/shard_map/ppermute | solution.py:18
  91.1 6.3 %shard_map.158 = f32[4,8,128]{2,1,0:T(8,128)} custom-call(s32[1792]{0:T(1024)} %concatenate.91.table_ref, f32[4,128,4]{2,1,0:T(8,128)} %get-tuple-element.19.target_ref, f32[73,8,128]{2,1,0:T(8,128)} %pad.11.source_ref, f32[27,8,128]{2,1,0:T(8,128)} %broadcast_in_dim.44.shift_ref), custom_call_target="tpu_custom_call" | custom-call | flops 13107200 | bytes 524288 | tf_op jit(solution)/shard_map/pallas_call | solution.py:398
  97.4 0.7 constant_dynamic-update-slice_fusion.3
  98.3 1.2 %collective-permute-start.8 = (f32[81]{0:T(128)S(1)}, f32[81]{0:T(128)S(1)}, u32[]{:S(2)}, u32[]{:S(2)}) collective-permute-start(f32[81]{0:T(128)S(1)} %fusion.9), channel_id=1, source_target_pairs={{0,4},{1,5},{2,6},{3,7},{4,0},{5,1},{6,2},{7,3},{8,12},{9,13},{10,... | collective-permute-start | bytes 980 | tf_op jit(solution)/shard_map/ppermute | solution.py:18
  99.6 3.2 %collective-permute-done.8 = f32[81]{0:T(128)S(1)} collective-permute-done((f32[81]{0:T(128)S(1)}, f32[81]{0:T(128)S(1)}, u32[]{:S(2)}, u32[]{:S(2)}) %collective-permute-start.8) | collective-permute-done | bytes 356 | tf_op jit(solution)/shard_map/ppermute | solution.py:18
  106.3 3.0 %add_reduce_fusion = (f32[4,4,2,128]{3,2,1,0:T(2,128)S(1)}, f32[4,4,2,128]{3,2,1,0:T(2,128)S(1)}, f32[4,4,2,128]{3,2,1,0:T(2,128)S(1)}, f32[4,4,2,128]{3,2,1,0:T(2,128)S(1)}) fusion(f32[40,4,4,2]{0,3,2,1:T(2,128)S(1)} %copy.449, f32[40,4,4,2]{0,3,2,1:T(2,128)S(1)} %copy.448, f32[4,4,2,128]{3,2,1,0:T(2,128)S(1)} %get-tuple-element.75, ...), kind=kLoop, calls=%fused_computation.48 | loop fusion | flops 2932736 | bytes 125408 | tf_op jit(solution)/shard_map/reduce_sum | solution.py:122
  109.5 0.7 pad_maximum_fusion.1
  (365 shorter events, 21.3 us)
Async XLA Ops:
  0.0 6.7 %copy-start = (bf16[8,81,81]{2,0,1:T(8,128)(2,1)S(1)}, bf16[8,81,81]{2,0,1:T(8,128)(2,1)}, u32[]{:S(2)}) copy-start(bf16[8,81,81]{2,0,1:T(8,128)(2,1)} %param.19) | copy-start | bytes 314932
  0.0 12.7 %copy-start.6 = (bf16[81,81]{1,0:T(8,128)(2,1)S(1)}, bf16[81,81]{1,0:T(8,128)(2,1)}, u32[]{:S(2)}) copy-start(bf16[81,81]{1,0:T(8,128)(2,1)} %param.23) | copy-start | bytes 39370
  0.0 14.9 %copy-start.5 = (s32[26,4,4,2]{0,3,2,1:T(2,128)S(1)}, s32[26,4,4,2]{0,3,2,1:T(2,128)}, u32[]{:S(2)}) copy-start(s32[26,4,4,2]{0,3,2,1:T(2,128)} %param.18) | copy-start | bytes 9988
  8.1 14.7 %collective-permute-start.1 = (f32[5068]{0:T(1024)S(1)}, f32[5068]{0:T(1024)S(1)}, u32[]{:S(2)}, u32[]{:S(2)}) collective-permute-start(f32[5068]{0:T(1024)S(1)} %concatenate.99), channel_id=1, source_target_pairs={{8,0},{16,8},{24,16},{0,24},{9,1},{17,9},{25,17},{1,25},{10,2},{18... | collective-permute-start | bytes 60824 | tf_op jit(solution)/shard_map/ppermute | solution.py:36
  12.4 10.7 %collective-permute-start = (f32[5068]{0:T(1024)S(1)}, f32[5068]{0:T(1024)S(1)}, u32[]{:S(2)}, u32[]{:S(2)}) collective-permute-start(f32[5068]{0:T(1024)S(1)} %concatenate.98), channel_id=1, source_target_pairs={{0,8},{8,16},{16,24},{24,0},{1,9},{9,17},{17,25},{25,1},{2,10},{10... | collective-permute-start | bytes 60824 | tf_op jit(solution)/shard_map/ppermute | solution.py:35
  12.8 14.6 %collective-permute-start.4 = (f32[81]{0:T(128)S(1)}, f32[81]{0:T(128)S(1)}, u32[]{:S(2)}, u32[]{:S(2)}) collective-permute-start(f32[81]{0:T(128)S(1)} %bitcast.493), channel_id=1, source_target_pairs={{0,8},{8,0},{16,24},{24,16},{1,9},{9,1},{17,25},{25,17},{2,10},{10... | collective-permute-start | bytes 980 | tf_op jit(solution)/shard_map/ppermute | solution.py:18
  18.0 1.5 %copy-start.2 = (bf16[2,2,81,81]{3,1,2,0:T(2,128)(2,1)S(1)}, bf16[2,2,81,81]{3,1,2,0:T(2,128)(2,1)}, u32[]{:S(2)}) copy-start(bf16[2,2,81,81]{3,1,2,0:T(2,128)(2,1)} %param.25) | copy-start | bytes 157468
  18.0 1.8 %copy-start.3 = (bf16[2,2,81,81]{3,1,2,0:T(2,128)(2,1)S(1)}, bf16[2,2,81,81]{3,1,2,0:T(2,128)(2,1)}, u32[]{:S(2)}) copy-start(bf16[2,2,81,81]{3,1,2,0:T(2,128)(2,1)} %param.26) | copy-start | bytes 157468
  18.0 1.9 %copy-start.4 = (bf16[2,2,81,81]{3,1,2,0:T(2,128)(2,1)S(1)}, bf16[2,2,81,81]{3,1,2,0:T(2,128)(2,1)}, u32[]{:S(2)}) copy-start(bf16[2,2,81,81]{3,1,2,0:T(2,128)(2,1)} %param.27) | copy-start | bytes 157468
  18.1 2.5 %copy-start.19 = (f32[26]{0:T(128)S(1)}, f32[26]{0:T(128)}, u32[]{:S(2)}) copy-start(f32[26]{0:T(128)} %constant.257) | copy-start | bytes 316
  18.1 2.5 %copy-start.20 = (f32[26]{0:T(128)S(1)}, f32[26]{0:T(128)}, u32[]{:S(2)}) copy-start(f32[26]{0:T(128)} %constant.255) | copy-start | bytes 316
  18.1 2.5 %copy-start.21 = (f32[26]{0:T(128)S(1)}, f32[26]{0:T(128)}, u32[]{:S(2)}) copy-start(f32[26]{0:T(128)} %constant.253) | copy-start | bytes 316
  18.1 2.7 %copy-start.16 = (f32[98]{0:T(128)S(1)}, f32[98]{0:T(128)}, u32[]{:S(2)}) copy-start(f32[98]{0:T(128)} %constant.251) | copy-start | bytes 1180
  18.1 2.7 %copy-start.17 = (f32[98]{0:T(128)S(1)}, f32[98]{0:T(128)}, u32[]{:S(2)}) copy-start(f32[98]{0:T(128)} %constant.249) | copy-start | bytes 1180
  18.1 2.7 %copy-start.18 = (f32[98]{0:T(128)S(1)}, f32[98]{0:T(128)}, u32[]{:S(2)}) copy-start(f32[98]{0:T(128)} %constant.247) | copy-start | bytes 1180
  25.0 10.1 %copy-start.15 = (f32[27,8]{1,0:T(8,128)S(1)}, f32[27,8]{1,0:T(8,128)}, u32[]{:S(2)}) copy-start(f32[27,8]{1,0:T(8,128)} %constant.234.clone) | copy-start | bytes 2596
  25.2 4.0 %collective-permute-start.3 = (f32[8088]{0:T(1024)S(1)}, f32[8088]{0:T(1024)S(1)}, u32[]{:S(2)}, u32[]{:S(2)}) collective-permute-start(f32[8088]{0:T(1024)S(1)} %concatenate.104), channel_id=1, source_target_pairs={{1,0},{2,1},{3,2},{4,3},{5,4},{6,5},{7,6},{0,7},{9,8},{10,9},{11,1... | collective-permute-start | bytes 97064 | tf_op jit(solution)/shard_map/ppermute | solution.py:36
  28.4 5.3 %collective-permute-start.2 = (f32[8088]{0:T(1024)S(1)}, f32[8088]{0:T(1024)S(1)}, u32[]{:S(2)}, u32[]{:S(2)}) collective-permute-start(f32[8088]{0:T(1024)S(1)} %concatenate.103), channel_id=1, source_target_pairs={{0,1},{1,2},{2,3},{3,4},{4,5},{5,6},{6,7},{7,0},{8,9},{9,10},{10,1... | collective-permute-start | bytes 97064 | tf_op jit(solution)/shard_map/ppermute | solution.py:35
  48.8 23.8 %collective-permute-start.5 = (f32[81]{0:T(128)S(1)}, f32[81]{0:T(128)S(1)}, u32[]{:S(2)}, u32[]{:S(2)}) collective-permute-start(f32[81]{0:T(128)S(1)} %fusion.12), channel_id=1, source_target_pairs={{0,16},{8,24},{16,0},{24,8},{1,17},{9,25},{17,1},{25,9},{2,18},{10... | collective-permute-start | bytes 980 | tf_op jit(solution)/shard_map/ppermute | solution.py:18
  56.1 8.1 %copy-start.13 = (f32[4,8,128]{2,1,0:T(8,128)S(1)}, f32[4,8,128]{2,1,0:T(8,128)}, u32[]{:S(2)}) copy-start(f32[4,8,128]{2,1,0:T(8,128)} %shard_map.155) | copy-start | bytes 49156
  72.5 25.6 %copy-start.12 = (f32[4,8,128]{2,1,0:T(8,128)S(1)}, f32[4,8,128]{2,1,0:T(8,128)}, u32[]{:S(2)}) copy-start(f32[4,8,128]{2,1,0:T(8,128)} %shard_map.159) | copy-start | bytes 49156
  72.5 25.6 %copy-start.11 = (f32[4,8,128]{2,1,0:T(8,128)S(1)}, f32[4,8,128]{2,1,0:T(8,128)}, u32[]{:S(2)}) copy-start(f32[4,8,128]{2,1,0:T(8,128)} %shard_map.160) | copy-start | bytes 49156
  72.5 25.6 %copy-start.14 = (f32[4,8,128]{2,1,0:T(8,128)S(1)}, f32[4,8,128]{2,1,0:T(8,128)}, u32[]{:S(2)}) copy-start(f32[4,8,128]{2,1,0:T(8,128)} %shard_map.161) | copy-start | bytes 49156
  72.5 30.4 %copy-start.7 = (bf16[81,81]{1,0:T(8,128)(2,1)S(1)}, bf16[81,81]{1,0:T(8,128)(2,1)}, u32[]{:S(2)}) copy-start(bf16[81,81]{1,0:T(8,128)(2,1)} %param.28) | copy-start | bytes 39370
  72.5 32.2 %copy-start.8 = (bf16[81,81]{1,0:T(8,128)(2,1)S(1)}, bf16[81,81]{1,0:T(8,128)(2,1)}, u32[]{:S(2)}) copy-start(bf16[81,81]{1,0:T(8,128)(2,1)} %param.24) | copy-start | bytes 39370
  72.6 32.6 %copy-start.9 = (bf16[81,81]{1,0:T(8,128)(2,1)S(1)}, bf16[81,81]{1,0:T(8,128)(2,1)}, u32[]{:S(2)}) copy-start(bf16[81,81]{1,0:T(8,128)(2,1)} %param.22) | copy-start | bytes 39370
  72.6 32.8 %copy-start.1 = (bf16[8,81,81]{2,0,1:T(8,128)(2,1)S(1)}, bf16[8,81,81]{2,0,1:T(8,128)(2,1)}, u32[]{:S(2)}) copy-start(bf16[8,81,81]{2,0,1:T(8,128)(2,1)} %param.20) | copy-start | bytes 314932
  80.2 25.6 %copy-start.10 = (bf16[81,81]{1,0:T(8,128)(2,1)S(1)}, bf16[81,81]{1,0:T(8,128)(2,1)}, u32[]{:S(2)}) copy-start(bf16[81,81]{1,0:T(8,128)(2,1)} %param.21) | copy-start | bytes 39370
  80.4 1.2 %collective-permute-start.6 = (f32[81]{0:T(128)S(1)}, f32[81]{0:T(128)S(1)}, u32[]{:S(2)}, u32[]{:S(2)}) collective-permute-start(f32[81]{0:T(128)S(1)} %fusion.11), channel_id=1, source_target_pairs={{0,1},{1,0},{2,3},{3,2},{4,5},{5,4},{6,7},{7,6},{8,9},{9,8},{10,11... | collective-permute-start | bytes 980 | tf_op jit(solution)/shard_map/ppermute | solution.py:18
  87.5 3.6 %collective-permute-start.7 = (f32[81]{0:T(128)S(1)}, f32[81]{0:T(128)S(1)}, u32[]{:S(2)}, u32[]{:S(2)}) collective-permute-start(f32[81]{0:T(128)S(1)} %fusion.10), channel_id=1, source_target_pairs={{0,2},{1,3},{2,0},{3,1},{4,6},{5,7},{6,4},{7,5},{8,10},{9,11},{10,... | collective-permute-start | bytes 980 | tf_op jit(solution)/shard_map/ppermute | solution.py:18
  98.3 4.5 %collective-permute-start.8 = (f32[81]{0:T(128)S(1)}, f32[81]{0:T(128)S(1)}, u32[]{:S(2)}, u32[]{:S(2)}) collective-permute-start(f32[81]{0:T(128)S(1)} %fusion.9), channel_id=1, source_target_pairs={{0,4},{1,5},{2,6},{3,7},{4,0},{5,1},{6,2},{7,3},{8,12},{9,13},{10,... | collective-permute-start | bytes 980 | tf_op jit(solution)/shard_map/ppermute | solution.py:18

commit v5 on v4

--- a/solution.py
+++ b/solution.py
@@ -310,13 +310,14 @@
     piece_leaves = out_ref.shape[0]
     place_start = 2 * leaf_count
     kind_start = place_start + leaf_count * listed_width
+    order_start = kind_start + leaf_count * listed_width
     rows = NEAR_ROWS
     lanes = out_ref.shape[2]
     lane = lax.broadcasted_iota(jnp.int32, (rows, lanes), 1)
     row = lax.broadcasted_iota(jnp.int32, (rows, lanes), 0)
 
     def leaf_body(local, carry):
-        leaf = first_leaf + local
+        leaf = table_ref[order_start + first_leaf + local]
         chunk_count = (table_ref[leaf] + rows - 1) // rows
         listed = table_ref[leaf_count + leaf]
         base = leaf * listed_width
@@ -358,8 +359,21 @@
     leaf_count = size_x * size_y * size_z
     ext_y = size_y + 2
     target = jnp.transpose(charged, (1, 2, 3, 4, 0)).reshape(leaf_count, slot_count, 4)
-    source = jnp.transpose(rimmed, (1, 2, 3, 0, 4)).reshape(-1, 4, slot_count)
-    source = jnp.pad(source, ((0, 1), (0, 4), (0, 0)))
+    inner = [
+        leaf
+        for leaf in range(leaf_count)
+        if 0 < leaf // (size_y * size_z) < size_x - 1 and 0 < leaf // size_z % size_y < size_y - 1
+    ]
+    order = inner + [leaf for leaf in range(leaf_count) if leaf not in inner]
+    back = [order.index(leaf) for leaf in range(leaf_count)]
+    target = jnp.concatenate([target[leaf : leaf + 1] for leaf in order], axis=0)
+
+    def source_table(grid):
+        table = jnp.transpose(grid, (1, 2, 3, 0, 4)).reshape(-1, 4, slot_count)
+        return jnp.pad(table, ((0, 1), (0, 4), (0, 0)))
+
+    source = source_table(rimmed)
+    early_source = source_table(jnp.pad(charged, ((0, 0), (1, 1), (1, 1), (0, 0), (0, 0))))
     empty_leaf = source.shape[0] - 1
     offsets = [(0, 0, 0)] + leaf_offsets()
     shift_rows = jnp.array([[float(v) for v in offset] + [0.0] * 5 for offset in offsets], jnp.float32)
@@ -385,7 +399,13 @@
     place_list = jnp.sum(jnp.where(chosen, places[None], 0), axis=1)
     place_list = jnp.where(slots[:, None] < jnp.sum(active.astype(jnp.int32), axis=0)[None], place_list, empty_leaf)
     table = jnp.concatenate(
-        [counts.reshape(-1), listed, jnp.transpose(place_list).reshape(-1), jnp.transpose(kind_list).reshape(-1)]
+        [
+            counts.reshape(-1),
+            listed,
+            jnp.transpose(place_list).reshape(-1),
+            jnp.transpose(kind_list).reshape(-1),
+            jnp.array(order, jnp.int32),
+        ]
     ).astype(jnp.int32)
     piece = leaf_count // NEAR_PIECES if leaf_count % NEAR_PIECES == 0 else leaf_count
     pairs = piece * slot_count * slot_count * 10
@@ -393,6 +413,7 @@
     def run_piece(number, gate):
         first_leaf = number * piece
         own = target[first_leaf : first_leaf + piece]
+        early = all(leaf in inner for leaf in order[first_leaf : first_leaf + piece])
         if gate is not None:
             own, unused = lax.optimization_barrier((own, gate))
         return pl.pallas_call(
@@ -404,10 +425,11 @@
             cost_estimate=pl.CostEstimate(
                 flops=20 * pairs, transcendentals=pairs, bytes_accessed=8 * piece * slot_count * 128
             ),
-        )(table, own, source, shift_table)
+        )(table, own, early_source if early else source, shift_table)
 
     def finish_near(outs):
         out = jnp.concatenate(outs, axis=0)
+        out = jnp.concatenate([out[place : place + 1] for place in back], axis=0)
         near = jnp.transpose(out[:, :4, :], (1, 0, 2))
         return near.reshape(4, size_x, size_y, size_z, slot_count)
 

time: 111 us -> 131 us (1.18)
  local copies, waits for them, and re-layouts: 19.8 us -> 30.5 us
  other arithmetic: 13.2 us -> 20.6 us
  matrix products: 4.43 us -> 7.82 us
  Pallas kernels: 50 us -> 52.2 us
  waiting for transfers between devices: 10.7 us -> 8.92 us
    dot_general x23, matrix products: 3.33 us -> 6.73 us  [matrix_vector(): return jnp.dot(matrix, vector, precision=highest)]
    pallas_call x8, Pallas kernels: 50 us -> 52.2 us  [run_piece(): pl.pallas_call(functools.partial(near_kernel, first_leaf, leaf_count, len...]
    slice x5, local copies, waits for them, and re-layouts: 0.15 us -> 2.27 us  [extended_joint(): high = high_all[place:place + size].reshape(piece.shape)]
    slice x5, local copies, waits for them, and re-layouts: 0.15 us -> 2.25 us  [extended_joint(): low = low_all[place:place + size].reshape(piece.shape)]
    mul x3, other arithmetic: 0.22 us -> 2.13 us  [near_local(): ((leaf_x + 1 + offset[0]) * ext_y + leaf_y + 1 + offset[1]) * size_z]
    ppermute x5, waiting for transfers between devices: 6.11 us -> 4.33 us  [from_partner(): return lax.ppermute(value, axis, pairs)]
    mul x3, other arithmetic: 0.01 us -> 1.64 us  [near_local(): (leaf_x + 1 + offset[0]) * ext_y + leaf_y + 1 + offset[1]]
    slice x1 -> x4, local copies, waits for them, and re-layouts: 1.34 us -> 2.79 us  [run_piece(): own = target[first_leaf:first_leaf + piece]]
  transfers between devices with their start and end apart: 9 -> 9, of which waited for: 5 -> 3; matrix products, arithmetic and copies ran while one was open for 17% -> 30% of each run, Pallas kernels for 16% -> 24%
where the time goes in v5:
time: 131 us
  Pallas kernels  52.2 us (40%)
  local copies, waits for them, and re-layouts  30.5 us (23%)
  other arithmetic  20.6 us (16%)
  starting transfers between devices  9.38 us (7%)
  waiting for transfers between devices  8.92 us (7%)
  matrix products  7.82 us (6%)
  between operations  1.67 us (1%)
    pallas_call x8, Pallas kernels, run_piece(): pl.pallas_call(functools.partial(near_kernel, first_leaf, leaf_count, len...  52.2 us
    dot_general x23, matrix products, matrix_vector(): return jnp.dot(matrix, vector, precision=highest)  6.73 us
    ppermute x2, starting transfers between devices, extended_joint(): lax.ppermute(jnp.concatenate([piece.reshape(-1) for piece in highs]), axi...  4.81 us
    ppermute x5, waiting for transfers between devices, from_partner(): return lax.ppermute(value, axis, pairs)  4.33 us
    ppermute x2, waiting for transfers between devices, extended_joint(): lax.ppermute(jnp.concatenate([piece.reshape(-1) for piece in lows]), axis...  4.33 us
    unnamed x204, local copies, waits for them, and re-layouts  4.28 us
    ppermute x5, starting transfers between devices, from_partner(): return lax.ppermute(value, axis, pairs)  3.86 us
    reduce_sum x1, other arithmetic, evaluate(): jnp.sum(cos_local * cosine + sin_local * sine_part, axis=0)  2.98 us
  transfers between devices with their start and end apart: 9, of which 3 were waited for; matrix products, arithmetic and copies ran while one was open for 30% of the time, Pallas kernels for 24%

profile of v5, /device:TPU:0, one launch (start us, length us, event | category | flops | bytes accessed | tf_op | source)
XLA Modules:
  0.0 131.1 jit_solution(11638011825663581138)
XLA Ops:
  0.1 0.8 copy.379
  0.9 0.9 add_bitcast_fusion.2
  1.8 0.9 fusion.41
  2.8 2.9 %multiply_reduce_fusion.4 = (f32[40,4,4,2]{0,3,2,1:T(2,128)S(1)}, f32[40,4,4,2]{0,3,2,1:T(2,128)S(1)}) fusion(f32[4,4,2,128]{3,2,1,0:T(2,128)S(1)} %bitcast.465, f32[4,4,2,128]{3,2,1,0:T(2,128)S(1)} %get-tuple-element.78, f32[40]{0:T(128)S(1)} %get-tuple-element.133, f32[4,4,2,128]{3,2,1,0:T(2,128)S(1)} %get-tuple-element.79, f32[40]{0:T(128)S(1)} %get-tuple-element.134, ...), kind=kLoop, calls=%fused_computation.50 | loop fusion | flops 1472000 | bytes 76256 | tf_op jit(solution)/shard_map/reduce_sum | solution.py:110
  6.5 1.5 %fusion.88 = f32[1,81]{1,0:T(1,128)} fusion(bf16[81,81]{1,0:T(8,128)(2,1)} %param.24, f32[81]{0:T(128)S(1)} %maximum_reduce_fusion.2), kind=kOutput, calls=%fused_computation.431 | convolution fusion | flops 78732 | bytes 13770 | tf_op jit(solution)/shard_map/dot_general | solution.py:200
  8.0 2.9 %collective-permute-start = (f32[81]{0:T(128)}, f32[81]{0:T(128)}, u32[]{:S(2)}, u32[]{:S(2)}) collective-permute-start(f32[81]{0:T(128)} %bitcast.28), channel_id=1, source_target_pairs={{0,8},{8,0},{16,24},{24,16},{1,9},{9,1},{17,25},{25,17},{2,10},{10... | collective-permute-start | bytes 980 | tf_op jit(solution)/shard_map/ppermute | solution.py:18
  11.0 0.8 slice.674
  13.5 1.5 %collective-permute-start.3 = (f32[5068]{0:T(1024)}, f32[5068]{0:T(1024)}, u32[]{:S(2)}, u32[]{:S(2)}) collective-permute-start(f32[5068]{0:T(1024)} %concatenate.111), channel_id=1, source_target_pairs={{8,0},{16,8},{24,16},{0,24},{9,1},{17,9},{25,17},{1,25},{10,2},{18... | collective-permute-start | bytes 60824 | tf_op jit(solution)/shard_map/ppermute | solution.py:36
  21.1 1.1 fusion.92
  26.6 0.9 select_reduce_fusion
  28.5 0.9 copy.384
  29.4 0.9 fusion.95
  30.5 0.8 convolution_bitcast_fusion.24
  31.5 0.9 fusion.94
  32.3 0.9 fusion.93
  34.5 0.8 pad_maximum_fusion
  37.1 6.7 %shard_map.163 = f32[4,8,128]{2,1,0:T(8,128)} custom-call(s32[1824]{0:T(1024)} %concatenate.102.table_ref, f32[4,128,4]{2,1,0:T(8,128)} %get-tuple-element.33.target_ref, f32[73,8,128]{2,1,0:T(8,128)} %pad.19.source_ref, f32[27,8,128]{2,1,0:T(8,128)} %broadcast_in_dim.43.shift_ref), custom_call_target="tpu_custom_call" | custom-call | flops 13107200 | bytes 524288 | tf_op jit(solution)/shard_map/pallas_call | solution.py:419
  44.1 0.9 copy.410
  45.4 0.8 fusion.12
  46.2 0.9 collective-permute-start.1
  47.2 6.0 %shard_map.165 = f32[4,8,128]{2,1,0:T(8,128)} custom-call(s32[1824]{0:T(1024)} %concatenate.102.table_ref, f32[4,128,4]{2,1,0:T(8,128)} %get-tuple-element.15.target_ref, f32[73,8,128]{2,1,0:T(8,128)} %pad.19.source_ref, f32[27,8,128]{2,1,0:T(8,128)} %broadcast_in_dim.43.shift_ref), custom_call_target="tpu_custom_call" | custom-call | flops 13107200 | bytes 524288 | tf_op jit(solution)/shard_map/pallas_call | solution.py:419
  60.0 3.3 %collective-permute-start.5 = (f32[8088]{0:T(1024)S(1)}, f32[8088]{0:T(1024)S(1)}, u32[]{:S(2)}, u32[]{:S(2)}) collective-permute-start(f32[8088]{0:T(1024)S(1)} %concatenate.116), channel_id=1, source_target_pairs={{1,0},{2,1},{3,2},{4,3},{5,4},{6,5},{7,6},{0,7},{9,8},{10,9},{11,1... | collective-permute-start | bytes 97064 | tf_op jit(solution)/shard_map/ppermute | solution.py:36
  65.3 4.3 %collective-permute-done.4 = f32[8088]{0:T(1024)S(1)} collective-permute-done((f32[8088]{0:T(1024)S(1)}, f32[8088]{0:T(1024)S(1)}, u32[]{:S(2)}, u32[]{:S(2)}) %collective-permute-start.4) | collective-permute-done | bytes 32384 | tf_op jit(solution)/shard_map/ppermute | solution.py:35
  71.0 7.0 %shard_map.164 = f32[4,8,128]{2,1,0:T(8,128)} custom-call(s32[1824]{0:T(1024)} %concatenate.102.table_ref, f32[4,128,4]{2,1,0:T(8,128)} %bitcast.468, f32[73,8,128]{2,1,0:T(8,128)} %pad.20.source_ref, f32[27,8,128]{2,1,0:T(8,128)} %broadcast_in_dim.43.shift_ref), custom_call_target="tpu_custom_call" | custom-call | flops 13107200 | bytes 524288 | tf_op jit(solution)/shard_map/pallas_call | solution.py:419
  78.7 7.6 %shard_map.166 = f32[4,8,128]{2,1,0:T(8,128)} custom-call(s32[1824]{0:T(1024)} %concatenate.102.table_ref, f32[4,128,4]{2,1,0:T(8,128)} %bitcast.469, f32[73,8,128]{2,1,0:T(8,128)} %pad.20.source_ref, f32[27,8,128]{2,1,0:T(8,128)} %broadcast_in_dim.43.shift_ref), custom_call_target="tpu_custom_call" | custom-call | flops 13107200 | bytes 524288 | tf_op jit(solution)/shard_map/pallas_call | solution.py:419
  86.3 6.6 %shard_map.168 = f32[4,8,128]{2,1,0:T(8,128)} custom-call(s32[1824]{0:T(1024)} %concatenate.102.table_ref, f32[4,128,4]{2,1,0:T(8,128)} %get-tuple-element.38.target_ref, f32[73,8,128]{2,1,0:T(8,128)} %pad.20.source_ref, f32[27,8,128]{2,1,0:T(8,128)} %broadcast_in_dim.43.shift_ref), custom_call_target="tpu_custom_call" | custom-call | flops 13107200 | bytes 524288 | tf_op jit(solution)/shard_map/pallas_call | solution.py:419
  92.9 6.0 %shard_map.169 = f32[4,8,128]{2,1,0:T(8,128)} custom-call(s32[1824]{0:T(1024)} %concatenate.102.table_ref, f32[4,128,4]{2,1,0:T(8,128)} %get-tuple-element.30.target_ref, f32[73,8,128]{2,1,0:T(8,128)} %pad.20.source_ref, f32[27,8,128]{2,1,0:T(8,128)} %broadcast_in_dim.43.shift_ref), custom_call_target="tpu_custom_call" | custom-call | flops 13107200 | bytes 524288 | tf_op jit(solution)/shard_map/pallas_call | solution.py:419
  103.8 5.8 %shard_map.170 = f32[4,8,128]{2,1,0:T(8,128)} custom-call(s32[1824]{0:T(1024)} %concatenate.102.table_ref, f32[4,128,4]{2,1,0:T(8,128)} %get-tuple-element.29.target_ref, f32[73,8,128]{2,1,0:T(8,128)} %pad.20.source_ref, f32[27,8,128]{2,1,0:T(8,128)} %broadcast_in_dim.43.shift_ref), custom_call_target="tpu_custom_call" | custom-call | flops 13107200 | bytes 524288 | tf_op jit(solution)/shard_map/pallas_call | solution.py:419
  109.6 6.6 %shard_map.167 = f32[4,8,128]{2,1,0:T(8,128)} custom-call(s32[1824]{0:T(1024)} %concatenate.102.table_ref, f32[4,128,4]{2,1,0:T(8,128)} %get-tuple-element.19.target_ref, f32[73,8,128]{2,1,0:T(8,128)} %pad.20.source_ref, f32[27,8,128]{2,1,0:T(8,128)} %broadcast_in_dim.43.shift_ref), custom_call_target="tpu_custom_call" | custom-call | flops 13107200 | bytes 524288 | tf_op jit(solution)/shard_map/pallas_call | solution.py:419
  118.8 4.3 %collective-permute-done.8 = f32[81]{0:T(128)S(1)} collective-permute-done((f32[81]{0:T(128)S(1)}, f32[81]{0:T(128)S(1)}, u32[]{:S(2)}, u32[]{:S(2)}) %collective-permute-start.8) | collective-permute-done | bytes 356 | tf_op jit(solution)/shard_map/ppermute | solution.py:18
  124.9 0.8 fusion.18
  127.3 3.0 %add_reduce_fusion = (f32[4,4,2,128]{3,2,1,0:T(2,128)S(1)}, f32[4,4,2,128]{3,2,1,0:T(2,128)S(1)}, f32[4,4,2,128]{3,2,1,0:T(2,128)S(1)}, f32[4,4,2,128]{3,2,1,0:T(2,128)S(1)}) fusion(f32[40,4,4,2]{0,3,2,1:T(2,128)S(1)} %copy.474, f32[40,4,4,2]{0,3,2,1:T(2,128)S(1)} %copy.473, f32[4,4,2,128]{3,2,1,0:T(2,128)S(1)} %copy-done.10, f32[40]{0:T(128)S(1)} %copy-done.28, ...), kind=kLoop, calls=%fused_computation.48 | loop fusion | flops 2932736 | bytes 125408 | tf_op jit(solution)/shard_map/reduce_sum | solution.py:122
  (410 shorter events, 39.7 us)
Async XLA Ops:
  0.0 17.3 %copy-start.2 = (s32[26,4,4,2]{0,3,2,1:T(2,128)S(1)}, s32[26,4,4,2]{0,3,2,1:T(2,128)}, u32[]{:S(2)}) copy-start(s32[26,4,4,2]{0,3,2,1:T(2,128)} %param.19) | copy-start | bytes 9988
  1.7 9.2 %copy-start.7 = (f32[4,4,2,128]{3,2,1,0:T(2,128)}, f32[4,4,2,128]{3,2,1,0:T(2,128)S(1)}, u32[]{:S(2)}) copy-start(f32[4,4,2,128]{3,2,1,0:T(2,128)S(1)} %get-tuple-element.76) | copy-start | bytes 49156
  1.8 9.2 %copy-start.9 = (f32[4,4,2,128]{3,2,1,0:T(2,128)}, f32[4,4,2,128]{3,2,1,0:T(2,128)S(1)}, u32[]{:S(2)}) copy-start(f32[4,4,2,128]{3,2,1,0:T(2,128)S(1)} %get-tuple-element.78) | copy-start | bytes 49156
  1.8 9.2 %copy-start.11 = (f32[4,4,2,128]{3,2,1,0:T(2,128)}, f32[4,4,2,128]{3,2,1,0:T(2,128)S(1)}, u32[]{:S(2)}) copy-start(f32[4,4,2,128]{3,2,1,0:T(2,128)S(1)} %get-tuple-element.79) | copy-start | bytes 49156
  2.7 9.2 %copy-start.25 = (f32[40]{0:T(128)}, f32[40]{0:T(128)S(1)}, u32[]{:S(2)}) copy-start(f32[40]{0:T(128)S(1)} %get-tuple-element.134) | copy-start | bytes 484
  2.7 9.2 %copy-start.30 = (f32[40]{0:T(128)}, f32[40]{0:T(128)S(1)}, u32[]{:S(2)}) copy-start(f32[40]{0:T(128)S(1)} %broadcast_multiply_fusion.3) | copy-start | bytes 484
  8.0 37.3 %collective-permute-start = (f32[81]{0:T(128)}, f32[81]{0:T(128)}, u32[]{:S(2)}, u32[]{:S(2)}) collective-permute-start(f32[81]{0:T(128)} %bitcast.28), channel_id=1, source_target_pairs={{0,8},{8,0},{16,24},{24,16},{1,9},{9,1},{17,25},{25,17},{2,10},{10... | collective-permute-start | bytes 980 | tf_op jit(solution)/shard_map/ppermute | solution.py:18
  13.5 40.0 %collective-permute-start.3 = (f32[5068]{0:T(1024)}, f32[5068]{0:T(1024)}, u32[]{:S(2)}, u32[]{:S(2)}) collective-permute-start(f32[5068]{0:T(1024)} %concatenate.111), channel_id=1, source_target_pairs={{8,0},{16,8},{24,16},{0,24},{9,1},{17,9},{25,17},{1,25},{10,2},{18... | collective-permute-start | bytes 60824 | tf_op jit(solution)/shard_map/ppermute | solution.py:36
  16.0 38.5 %collective-permute-start.2 = (f32[5068]{0:T(1024)}, f32[5068]{0:T(1024)}, u32[]{:S(2)}, u32[]{:S(2)}) collective-permute-start(f32[5068]{0:T(1024)} %concatenate.110), channel_id=1, source_target_pairs={{0,8},{8,16},{16,24},{24,0},{1,9},{9,17},{17,25},{25,1},{2,10},{10... | collective-permute-start | bytes 60824 | tf_op jit(solution)/shard_map/ppermute | solution.py:35
  30.3 6.1 %copy-start.18 = (f32[27,8]{1,0:T(8,128)S(1)}, f32[27,8]{1,0:T(8,128)}, u32[]{:S(2)}) copy-start(f32[27,8]{1,0:T(8,128)} %constant.236.clone) | copy-start | bytes 2596
  46.2 7.0 %collective-permute-start.1 = (f32[81]{0:T(128)S(1)}, f32[81]{0:T(128)S(1)}, u32[]{:S(2)}, u32[]{:S(2)}) collective-permute-start(f32[81]{0:T(128)S(1)} %fusion.12), channel_id=1, source_target_pairs={{0,16},{8,24},{16,0},{24,8},{1,17},{9,25},{17,1},{25,9},{2,18},{10... | collective-permute-start | bytes 980 | tf_op jit(solution)/shard_map/ppermute | solution.py:18
  53.3 10.1 %collective-permute-start.6 = (f32[81]{0:T(128)S(1)}, f32[81]{0:T(128)S(1)}, u32[]{:S(2)}, u32[]{:S(2)}) collective-permute-start(f32[81]{0:T(128)S(1)} %fusion.11), channel_id=1, source_target_pairs={{0,1},{1,0},{2,3},{3,2},{4,5},{5,4},{6,7},{7,6},{8,9},{9,8},{10,11... | collective-permute-start | bytes 980 | tf_op jit(solution)/shard_map/ppermute | solution.py:18
  60.0 4.9 %collective-permute-start.5 = (f32[8088]{0:T(1024)S(1)}, f32[8088]{0:T(1024)S(1)}, u32[]{:S(2)}, u32[]{:S(2)}) collective-permute-start(f32[8088]{0:T(1024)S(1)} %concatenate.116), channel_id=1, source_target_pairs={{1,0},{2,1},{3,2},{4,3},{5,4},{6,5},{7,6},{0,7},{9,8},{10,9},{11,1... | collective-permute-start | bytes 97064 | tf_op jit(solution)/shard_map/ppermute | solution.py:36
  64.3 5.3 %collective-permute-start.4 = (f32[8088]{0:T(1024)S(1)}, f32[8088]{0:T(1024)S(1)}, u32[]{:S(2)}, u32[]{:S(2)}) collective-permute-start(f32[8088]{0:T(1024)S(1)} %concatenate.115), channel_id=1, source_target_pairs={{0,1},{1,2},{2,3},{3,4},{4,5},{5,6},{6,7},{7,0},{8,9},{9,10},{10,1... | collective-permute-start | bytes 97064 | tf_op jit(solution)/shard_map/ppermute | solution.py:35
  86.3 23.4 %collective-permute-start.7 = (f32[81]{0:T(128)S(1)}, f32[81]{0:T(128)S(1)}, u32[]{:S(2)}, u32[]{:S(2)}) collective-permute-start(f32[81]{0:T(128)S(1)} %fusion.10), channel_id=1, source_target_pairs={{0,2},{1,3},{2,0},{3,1},{4,6},{5,7},{6,4},{7,5},{8,10},{9,11},{10,... | collective-permute-start | bytes 980 | tf_op jit(solution)/shard_map/ppermute | solution.py:18
  92.9 8.4 %copy-start.17 = (f32[4,8,128]{2,1,0:T(8,128)S(1)}, f32[4,8,128]{2,1,0:T(8,128)}, u32[]{:S(2)}) copy-start(f32[4,8,128]{2,1,0:T(8,128)} %shard_map.166) | copy-start | bytes 49156
  102.7 14.3 %copy-start.13 = (f32[4,8,128]{2,1,0:T(8,128)S(1)}, f32[4,8,128]{2,1,0:T(8,128)}, u32[]{:S(2)}) copy-start(f32[4,8,128]{2,1,0:T(8,128)} %shard_map.163) | copy-start | bytes 49156
  102.7 15.0 %copy-start.16 = (f32[4,8,128]{2,1,0:T(8,128)S(1)}, f32[4,8,128]{2,1,0:T(8,128)}, u32[]{:S(2)}) copy-start(f32[4,8,128]{2,1,0:T(8,128)} %shard_map.168) | copy-start | bytes 49156
  102.7 15.0 %copy-start.14 = (f32[4,8,128]{2,1,0:T(8,128)S(1)}, f32[4,8,128]{2,1,0:T(8,128)}, u32[]{:S(2)}) copy-start(f32[4,8,128]{2,1,0:T(8,128)} %shard_map.165) | copy-start | bytes 49156
  102.7 15.0 %copy-start.15 = (f32[4,8,128]{2,1,0:T(8,128)S(1)}, f32[4,8,128]{2,1,0:T(8,128)}, u32[]{:S(2)}) copy-start(f32[4,8,128]{2,1,0:T(8,128)} %shard_map.169) | copy-start | bytes 49156
  102.7 20.5 %copy-start.3 = (bf16[81,81]{1,0:T(8,128)(2,1)S(1)}, bf16[81,81]{1,0:T(8,128)(2,1)}, u32[]{:S(2)}) copy-start(bf16[81,81]{1,0:T(8,128)(2,1)} %param.29) | copy-start | bytes 39370
  103.2 22.5 %copy-start.4 = (bf16[81,81]{1,0:T(8,128)(2,1)S(1)}, bf16[81,81]{1,0:T(8,128)(2,1)}, u32[]{:S(2)}) copy-start(bf16[81,81]{1,0:T(8,128)(2,1)} %param.25) | copy-start | bytes 39370
  103.3 22.7 %copy-start.20 = (f32[40,2]{0,1:T(2,128)S(1)}, f32[40,2]{0,1:T(2,128)}, u32[]{:S(2)}) copy-start(f32[40,2]{0,1:T(2,128)} %copy-done.19) | copy-start | bytes 964
  103.3 22.7 %copy-start.22 = (f32[40,2]{0,1:T(2,128)S(1)}, f32[40,2]{0,1:T(2,128)}, u32[]{:S(2)}) copy-start(f32[40,2]{0,1:T(2,128)} %copy-done.21) | copy-start | bytes 964
  103.3 22.8 %copy-start.31 = (f32[40]{0:T(128)S(1)}, f32[40]{0:T(128)}, u32[]{:S(2)}) copy-start(f32[40]{0:T(128)} %copy-done.30) | copy-start | bytes 484
  103.3 22.9 %copy-start.5 = (bf16[81,81]{1,0:T(8,128)(2,1)S(1)}, bf16[81,81]{1,0:T(8,128)(2,1)}, u32[]{:S(2)}) copy-start(bf16[81,81]{1,0:T(8,128)(2,1)} %param.23) | copy-start | bytes 39370
  103.3 23.0 %copy-start.1 = (bf16[8,81,81]{2,0,1:T(8,128)(2,1)S(1)}, bf16[8,81,81]{2,0,1:T(8,128)(2,1)}, u32[]{:S(2)}) copy-start(bf16[8,81,81]{2,0,1:T(8,128)(2,1)} %param.21) | copy-start | bytes 314932
  103.3 23.5 %copy-start.6 = (bf16[81,81]{1,0:T(8,128)(2,1)S(1)}, bf16[81,81]{1,0:T(8,128)(2,1)}, u32[]{:S(2)}) copy-start(bf16[81,81]{1,0:T(8,128)(2,1)} %param.22) | copy-start | bytes 39370
  103.3 24.0 %copy-start.8 = (f32[4,4,2,128]{3,2,1,0:T(2,128)S(1)}, f32[4,4,2,128]{3,2,1,0:T(2,128)}, u32[]{:S(2)}) copy-start(f32[4,4,2,128]{3,2,1,0:T(2,128)} %copy-done.7) | copy-start | bytes 49156
  103.3 24.0 %copy-start.10 = (f32[4,4,2,128]{3,2,1,0:T(2,128)S(1)}, f32[4,4,2,128]{3,2,1,0:T(2,128)}, u32[]{:S(2)}) copy-start(f32[4,4,2,128]{3,2,1,0:T(2,128)} %copy-done.9) | copy-start | bytes 49156
  103.3 24.0 %copy-start.12 = (f32[4,4,2,128]{3,2,1,0:T(2,128)S(1)}, f32[4,4,2,128]{3,2,1,0:T(2,128)}, u32[]{:S(2)}) copy-start(f32[4,4,2,128]{3,2,1,0:T(2,128)} %copy-done.11) | copy-start | bytes 49156
  118.6 4.5 %collective-permute-start.8 = (f32[81]{0:T(128)S(1)}, f32[81]{0:T(128)S(1)}, u32[]{:S(2)}, u32[]{:S(2)}) collective-permute-start(f32[81]{0:T(128)S(1)} %fusion.9), channel_id=1, source_target_pairs={{0,4},{1,5},{2,6},{3,7},{4,0},{5,1},{6,2},{7,3},{8,12},{9,13},{10,... | collective-permute-start | bytes 980 | tf_op jit(solution)/shard_map/ppermute | solution.py:18
  (16 other events, 85.6 us)
